TPU v7x, 32 devices: a whole 2x2x4 slice. The times are simulated.
32 devices in a mesh: row: 8 (over y, x, core), col: 4 (over z).
Axes of the slice: x: 2, y: 2, z: 4, core: 2. Of those that a mesh axis runs over, the one named last changes fastest.
Arguments:
- tokens: bfloat16 [512, 8192], P('col', 'row'), may hold values from -6 to 6
- cotangent: bfloat16 [512, 8192], P('col', 'row'), may hold values from -1.5 to 1.5
- gate_weight: bfloat16 [8192, 28672], P('row', 'col'), may hold values from -0.0625 to 0.0625
- up_weight: bfloat16 [8192, 28672], P('row', 'col'), may hold values from -0.0625 to 0.0625
- down_weight: bfloat16 [28672, 8192], P('col', 'row'), may hold values from -0.03125 to 0.03125
Outputs:
- input_grad: bfloat16 [512, 8192], P('col', 'row')
- gate_grad: bfloat16 [8192, 28672], P('row', 'col')
- up_grad: bfloat16 [8192, 28672], P('row', 'col')
- down_grad: bfloat16 [28672, 8192], P('col', 'row')
All inputs are finite; a program needn't handle non-finite values.
Results may differ from a plain program's by a relative error of at most 0.02.
Values may be sent and summed in bfloat16 or wider, within the bound.
No kernel may reach another device: no remote copies, remote signals or barrier semaphores. Data moves between devices by JAX's collectives and lax.ppermute only.
A program may use at most 256 MiB of HBM per device.

v0:
```python
import jax
import jax.numpy as jnp
from jax import lax
from jax.sharding import PartitionSpec as P

N_CHUNKS = 4
F32 = jnp.float32
BF16 = jnp.bfloat16


def activations(gate, up, back):
    sigma = jax.nn.sigmoid(gate)
    silu_gate = gate * sigma
    hidden = (silu_gate * up).astype(BF16)
    grad_gate_act = (back * up * sigma * (1.0 + gate * (1.0 - sigma))).astype(BF16)
    grad_up_act = (back * silu_gate).astype(BF16)
    return hidden, grad_gate_act, grad_up_act


def contract_rows(left, right):
    return lax.dot_general(
        left, right, (((0,), (0,)), ((), ())), preferred_element_type=F32
    )


def contract_cols(left, right):
    return lax.dot_general(
        left, right, (((1,), (1,)), ((), ())), preferred_element_type=F32
    )


def chip_ring(chips):
    if chips < 4 or chips % 2:
        return list(range(chips))
    half = chips // 2
    return list(range(half)) + list(range(chips - 1, half - 1, -1))


def ring_plan(n_row):
    chips = n_row // 2
    ring = chip_ring(chips)
    place = {chip: i for i, chip in enumerate(ring)}
    position = []
    pairs = []
    for r in range(n_row):
        chip, core = divmod(r, 2)
        p = place[chip]
        position.append(p if core == 0 else (-p) % chips)
        step = 1 if core == 0 else -1
        pairs.append((r, ring[(p + step) % chips] * 2 + core))
    return chips, position, pairs


def make_per_device(n_row):
    chips, position, ring_pairs = ring_plan(n_row)
    core_pairs = [(r, r ^ 1) for r in range(n_row)]

    def rows(arrays, start, size):
        return tuple(lax.dynamic_slice_in_dim(a, start, size, 0) for a in arrays)

    def put(arrays, pieces, start):
        return tuple(
            lax.dynamic_update_slice_in_dim(a, p, start, 0) for a, p in zip(arrays, pieces)
        )

    def per_device(tokens, cotangent, gate_weight, up_weight, down_weight):
        r = lax.axis_index("row")
        core = r % 2
        pos = jnp.asarray(position, jnp.int32)[r]
        width = tokens.shape[1]
        panel = lax.all_gather(
            jnp.concatenate([tokens, cotangent], axis=1), "col", axis=0, tiled=True
        )
        x_panel = panel[:, :width]
        dy_panel = panel[:, width:]
        n_tok = x_panel.shape[0]
        half = n_tok // 2
        block = half // chips
        columns = gate_weight.shape[1]
        w = columns // N_CHUNKS

        input_acc = jnp.zeros((n_tok, width), F32)
        gate_out = jnp.zeros((width, columns), BF16)
        up_out = jnp.zeros((width, columns), BF16)
        down_out = jnp.zeros((columns, width), BF16)
        x_chunk, dy_chunk = x_panel, dy_panel
        reduced = {}
        grads = {}
        for j in range(N_CHUNKS):
            cols = slice(j * w, (j + 1) * w)
            gw = gate_weight[:, cols]
            uw = up_weight[:, cols]
            parts = (
                jnp.dot(x_chunk, gw, preferred_element_type=F32).astype(BF16),
                jnp.dot(x_chunk, uw, preferred_element_type=F32).astype(BF16),
                contract_cols(dy_chunk, down_weight[cols, :]).astype(BF16),
            )
            own = rows(parts, core * half, half)
            other = rows(parts, (1 - core) * half, half)
            waits = tuple(reduced.get(j - 1, ())) + tuple(grads.get(j - 2, ()))
            if waits:
                other, _ = lax.optimization_barrier((other, waits))
            got = lax.ppermute(other, "row", core_pairs)
            x_chunk, dy_chunk, _ = lax.optimization_barrier((x_panel, dy_panel, got))
            summed = tuple(a.astype(F32) + b.astype(F32) for a, b in zip(own, got))
            acc = rows(summed, ((pos - 1) % chips) * block, block)
            for s in range(chips - 1):
                got = lax.ppermute(tuple(a.astype(BF16) for a in acc), "row", ring_pairs)
                mine = rows(summed, ((pos - s - 2) % chips) * block, block)
                acc = tuple(a.astype(F32) + b for a, b in zip(got, mine))
            reduced[j] = acc
            act = activations(*acc)
            held = tuple(jnp.zeros((half, w), BF16) for _ in act)
            held = put(held, act, pos * block)
            cur = act
            for s in range(chips - 1):
                cur = lax.ppermute(cur, "row", ring_pairs)
                held = put(held, cur, ((pos - s - 1) % chips) * block)
            partner = lax.ppermute(held, "row", core_pairs)
            full = tuple(jnp.zeros((n_tok, w), BF16) for _ in act)
            full = put(full, held, core * half)
            full = put(full, partner, (1 - core) * half)
            hidden, grad_gate_act, grad_up_act = full
            down_piece = contract_rows(hidden, dy_panel).astype(BF16)
            gate_piece = contract_rows(x_panel, grad_gate_act).astype(BF16)
            up_piece = contract_rows(x_panel, grad_up_act).astype(BF16)
            input_acc = (
                input_acc
                + contract_cols(grad_gate_act, gw)
                + contract_cols(grad_up_act, uw)
            )
            grads[j] = (down_piece, gate_piece, up_piece, input_acc)
            gate_out = lax.dynamic_update_slice(gate_out, gate_piece, (0, j * w))
            up_out = lax.dynamic_update_slice(up_out, up_piece, (0, j * w))
            down_out = lax.dynamic_update_slice(down_out, down_piece, (j * w, 0))
        input_sum = lax.psum_scatter(
            input_acc.astype(BF16), "col", scatter_dimension=0, tiled=True
        )
        return input_sum, gate_out, up_out, down_out

    return per_device


def solution(mesh):
    in_specs = (P("col", "row"), P("col", "row"), P("row", "col"), P("row", "col"), P("col", "row"))
    out_specs = (P("col", "row"), P("row", "col"), P("row", "col"), P("col", "row"))
    return jax.shard_map(
        make_per_device(mesh.shape["row"]),
        mesh=mesh,
        in_specs=in_specs,
        out_specs=out_specs,
        check_vma=False,
    )
```

profile of v0, /device:TPU:0, one launch (start us, length us, event | category | flops | bytes accessed | tf_op | source)
XLA Modules:
  0.0 474.6 jit_solution(829353379885857170)
XLA Ops:
  9.2 49.6 %all-gather.2.cloned.1.call-done = bf16[512,2048]{1,0:T(8,128)(2,1)} async-done(((bf16[128,2048]{1,0:T(8,128)(2,1)}), bf16[512,2048]{1,0:T(8,128)(2,1)}) %all-gather.2.cloned.1.call-update) | async-done | bytes 2097168 | tf_op jit(solution)/shard_map/all_gather | solution.py:71
  58.8 4.6 fusion.49
  64.6 4.1 fusion.46
  71.5 4.1 fusion.70
  82.0 4.5 fusion.52
  86.5 4.1 fusion.55
  90.7 4.3 fusion.73
  126.4 3.5 collective-permute-done.40
  133.4 2.5 collective-permute-done.16
  150.5 3.5 collective-permute-done.18
  155.3 4.1 fusion.58
  159.4 4.1 fusion.61
  164.6 4.1 fusion.76
  171.5 3.7 collective-permute-done.21
  195.9 3.5 collective-permute-done.27
  203.2 4.1 fusion.42
  209.5 5.5 %fusion.82 = f32[512,1024]{1,0:T(8,128)} fusion(f32[512,1024]{1,0:T(8,128)S(1)} %fusion.42, bf16[512,1792]{1,0:T(8,128)(2,1)S(1)} %constant_dynamic-update-slice_fusion.69, bf16[1024,7168]{1,0:T(8,128)(2,1)} %param.8), kind=kOutput, calls=%fused_computation.84 | convolution fusion | flops 1879572480 | bytes 9699328 | tf_op jit(solution)/shard_map/dot_general | solution.py:27
  217.8 10.5 %dynamic_update_slice.320 = bf16[7168,1024]{1,0:T(8,128)(2,1)} pad(bf16[1792,1024]{1,0:T(8,128)(2,1)S(1)} %convolution_convert_fusion.11, bf16[]{:T(256)} %constant.117.clone.1), padding=0_5376x0_0 | pad | bytes 18350082 | tf_op jit(solution)/shard_map/dynamic_update_slice | solution.py:135
  228.3 3.2 dynamic_update_slice.312
  232.8 7.1 %dynamic_update_slice.316 = bf16[1024,7168]{1,0:T(8,128)(2,1)} pad(bf16[1024,1792]{1,0:T(8,128)(2,1)S(1)} %convolution_convert_fusion.9, bf16[]{:T(256)} %constant.117.clone.1), padding=0_0x0_5376 | pad | bytes 18350082 | tf_op jit(solution)/shard_map/dynamic_update_slice | solution.py:134
  243.2 2.7 collective-permute-done.36
  260.4 3.5 collective-permute-done.38
  266.6 4.1 fusion.64
  270.7 4.8 %fusion.67 = bf16[512,1792]{1,0:T(8,128)(2,1)S(1)} fusion(bf16[512,1024]{1,0:T(8,128)(2,1)S(1)} %get-tuple-element.30, bf16[1024,7168]{1,0:T(8,128)(2,1)} %param.9), kind=kOutput, calls=%fused_computation.65 | convolution fusion | flops 1879965696 | bytes 6553600 | tf_op jit(solution)/shard_map/dot_general | solution.py:95
  276.7 4.1 fusion.79
  291.7 2.7 collective-permute-done.45
  297.7 2.7 collective-permute-done.54
  303.7 2.7 collective-permute-done.51
  309.1 3.3 collective-permute-done.47
  319.8 5.4 %fusion.34 = f32[512,1024]{1,0:T(8,128)} fusion(bf16[512,1792]{1,0:T(8,128)(2,1)S(1)} %constant_dynamic-update-slice_fusion.57, bf16[1024,7168]{1,0:T(8,128)(2,1)} %param.8), kind=kOutput, calls=%fused_computation.46 | convolution fusion | flops 1879048192 | bytes 7602176 | tf_op jit(solution)/shard_map/dot_general | solution.py:27
  326.5 6.7 %add_add_fusion = f32[512,1024]{1,0:T(8,128)} fusion(f32[512,1024]{1,0:T(8,128)} %fusion.82, f32[512,1024]{1,0:T(8,128)} %fusion.34, bf16[512,1792]{1,0:T(8,128)(2,1)S(1)} %constant_dynamic-update-slice_fusion.51, bf16[1024,7168]{1,0:T(8,128)(2,1)} %param.9), kind=kOutput, calls=%fused_computation.71 | convolution fusion | flops 1880096768 | bytes 11796480 | tf_op jit(solution)/shard_map/dot_general | solution.py:27
  334.5 4.0 constant_dynamic-update-slice_fusion.12
  338.5 4.0 constant_dynamic-update-slice_fusion.13
  344.7 4.3 collective-permute-done.61
  352.4 2.7 collective-permute-done.89
  358.4 2.7 collective-permute-done.58
  367.9 3.9 collective-permute-done.77
  375.2 2.7 collective-permute-done.69
  388.4 4.8 %fusion.22 = f32[512,1024]{1,0:T(8,128)S(1)} fusion(bf16[512,1792]{1,0:T(8,128)(2,1)S(1)} %constant_dynamic-update-slice_fusion.33, bf16[1024,7168]{1,0:T(8,128)(2,1)} %param.9), kind=kOutput, calls=%fused_computation.34 | convolution fusion | flops 1879048192 | bytes 7602176 | tf_op jit(solution)/shard_map/dot_general | solution.py:27
  393.3 4.1 fusion.26
  397.5 4.0 fusion.1
  429.9 4.8 %fusion.18 = f32[512,1024]{1,0:T(8,128)S(1)} fusion(bf16[512,1792]{1,0:T(8,128)(2,1)S(1)} %constant_dynamic-update-slice_fusion.21, bf16[1024,7168]{1,0:T(8,128)(2,1)} %param.8), kind=kOutput, calls=%fused_computation.30 | convolution fusion | flops 1879048192 | bytes 7602176 | tf_op jit(solution)/shard_map/dot_general | solution.py:27
  436.2 5.4 %add_convert_fusion = bf16[512,1024]{1,0:T(8,128)(2,1)} fusion(f32[512,1024]{1,0:T(8,128)S(1)} %fusion.18, f32[512,1024]{1,0:T(8,128)S(1)} %fusion.22, f32[512,1024]{1,0:T(8,128)S(1)} %copy-done.22, f32[512,1024]{1,0:T(8,128)S(1)} %fusion.26, bf16[512,1792]{1,0:T(8,128)(2,1)S(1)} %constant_dynamic-update-slice_fusion.15, bf16[1024,7168]{1,0:T(8,128)(2,1)} %param.9), kind=kOutput, calls=%fused_computation.70 | convolution fusion | flops 1881669632 | bytes 14942208 | tf_op jit(solution)/shard_map/dot_general | solution.py:27
  441.6 5.5 %fusion.3 = bf16[1024,7168]{1,0:T(8,128)(2,1)} fusion(bf16[1024,7168]{1,0:T(8,128)(2,1)} %constant_dynamic-update-slice_fusion.13, bf16[512,1792]{1,0:T(8,128)(2,1)} %copy-done.2, bf16[512,2048]{1,0:T(8,128)(2,1)S(1)} %copy-done.1), kind=kOutput, calls=%fused_computation.7 | convolution fusion | flops 1880883200 | bytes 6553600 | tf_op jit(solution)/shard_map/dot_general | solution.py:21
  448.9 4.0 fusion.4
  452.9 4.0 fusion.2
  456.9 4.0 fusion
  460.8 6.5 %reduce-scatter.2.cloned.1.call-done = bf16[128,1024]{1,0:T(8,128)(2,1)} async-done(((bf16[512,1024]{1,0:T(8,128)(2,1)}), bf16[128,1024]{1,0:T(8,128)(2,1)}) %reduce-scatter.2.cloned.1.call-update) | async-done | bytes 262160 | tf_op jit(solution)/shard_map/reduce_scatter | solution.py:136
  (390 shorter events, 206.5 us)
Async XLA Ops:
  7.2 51.6 %all-gather.2.cloned.1.call-start = ((), (), s32[]{:S(2)}) async-start(), calls=%async_computation.1 | async-start | bytes 2621440 | tf_op jit(solution)/shard_map/all_gather | solution.py:71
  9.1 458.2 %reduce-scatter.2.cloned.1.call-start = ((), (), s32[]{:S(2)}) async-start(), calls=%async_computation.2 | async-start | bytes 1310720 | tf_op jit(solution)/shard_map/reduce_scatter | solution.py:136
  64.6 17.3 %collective-permute-start.8 = (bf16[256,1792]{1,0:T(8,128)(2,1)S(1)}, bf16[256,1792]{1,0:T(8,128)(2,1)}, u32[]{:S(2)}, u32[]{:S(2)}) collective-permute-start(bf16[256,1792]{1,0:T(8,128)(2,1)S(1)} %constant_dynamic-slice_fusion.9), channel_id=1, source_target_pairs={{0,4},{4,0},{8,12},{12,8},{16,20},{20,16},{24,28},{28,24},{1,5},{5... | collective-permute-start | bytes 2752520 | tf_op jit(solution)/shard_map/ppermute | solution.py:103
  71.0 11.0 %collective-permute-start.4 = (bf16[256,1792]{1,0:T(8,128)(2,1)}, bf16[256,1792]{1,0:T(8,128)(2,1)}, u32[]{:S(2)}, u32[]{:S(2)}) collective-permute-start(bf16[256,1792]{1,0:T(8,128)(2,1)} %constant_dynamic-slice_fusion.10), channel_id=1, source_target_pairs={{0,4},{4,0},{8,12},{12,8},{16,20},{20,16},{24,28},{28,24},{1,5},{5... | collective-permute-start | bytes 2752520 | tf_op jit(solution)/shard_map/ppermute | solution.py:103
  103.3 7.8 %collective-permute-start.2 = (bf16[64,1792]{1,0:T(8,128)(2,1)S(1)}, bf16[64,1792]{1,0:T(8,128)(2,1)S(1)}, u32[]{:S(2)}, u32[]{:S(2)}) collective-permute-start(bf16[64,1792]{1,0:T(8,128)(2,1)S(1)} %add_convert_fusion.24), channel_id=1, source_target_pairs={{0,8},{4,20},{8,24},{12,4},{16,0},{20,28},{24,16},{28,12},{1,9},{5... | collective-permute-start | bytes 688136 | tf_op jit(solution)/shard_map/ppermute | solution.py:108
  105.8 7.8 %collective-permute-start.10 = (bf16[64,1792]{1,0:T(8,128)(2,1)S(1)}, bf16[64,1792]{1,0:T(8,128)(2,1)S(1)}, u32[]{:S(2)}, u32[]{:S(2)}) collective-permute-start(bf16[64,1792]{1,0:T(8,128)(2,1)S(1)} %add_convert_fusion.20), channel_id=1, source_target_pairs={{0,8},{4,20},{8,24},{12,4},{16,0},{20,28},{24,16},{28,12},{1,9},{5... | collective-permute-start | bytes 688136 | tf_op jit(solution)/shard_map/ppermute | solution.py:108
  108.7 7.3 %collective-permute-start.6 = (bf16[64,1792]{1,0:T(8,128)(2,1)S(1)}, bf16[64,1792]{1,0:T(8,128)(2,1)S(1)}, u32[]{:S(2)}, u32[]{:S(2)}) collective-permute-start(bf16[64,1792]{1,0:T(8,128)(2,1)S(1)} %add_convert_fusion.22), channel_id=1, source_target_pairs={{0,8},{4,20},{8,24},{12,4},{16,0},{20,28},{24,16},{28,12},{1,9},{5... | collective-permute-start | bytes 688136 | tf_op jit(solution)/shard_map/ppermute | solution.py:108
  111.1 7.3 %collective-permute-start.3 = (bf16[64,1792]{1,0:T(8,128)(2,1)S(1)}, bf16[64,1792]{1,0:T(8,128)(2,1)S(1)}, u32[]{:S(2)}, u32[]{:S(2)}) collective-permute-start(bf16[64,1792]{1,0:T(8,128)(2,1)S(1)} %add_convert_fusion.23), channel_id=1, source_target_pairs={{0,8},{4,20},{8,24},{12,4},{16,0},{20,28},{24,16},{28,12},{1,9},{5... | collective-permute-start | bytes 688136 | tf_op jit(solution)/shard_map/ppermute | solution.py:108
  113.6 7.3 %collective-permute-start.11 = (bf16[64,1792]{1,0:T(8,128)(2,1)S(1)}, bf16[64,1792]{1,0:T(8,128)(2,1)S(1)}, u32[]{:S(2)}, u32[]{:S(2)}) collective-permute-start(bf16[64,1792]{1,0:T(8,128)(2,1)S(1)} %add_convert_fusion.19), channel_id=1, source_target_pairs={{0,8},{4,20},{8,24},{12,4},{16,0},{20,28},{24,16},{28,12},{1,9},{5... | collective-permute-start | bytes 688136 | tf_op jit(solution)/shard_map/ppermute | solution.py:108
  116.0 7.3 %collective-permute-start.7 = (bf16[64,1792]{1,0:T(8,128)(2,1)S(1)}, bf16[64,1792]{1,0:T(8,128)(2,1)S(1)}, u32[]{:S(2)}, u32[]{:S(2)}) collective-permute-start(bf16[64,1792]{1,0:T(8,128)(2,1)S(1)} %add_convert_fusion.21), channel_id=1, source_target_pairs={{0,8},{4,20},{8,24},{12,4},{16,0},{20,28},{24,16},{28,12},{1,9},{5... | collective-permute-start | bytes 688136 | tf_op jit(solution)/shard_map/ppermute | solution.py:108
  125.0 29.7 %collective-permute-start.28 = (bf16[256,1792]{1,0:T(8,128)(2,1)S(1)}, bf16[256,1792]{1,0:T(8,128)(2,1)S(1)}, u32[]{:S(2)}, u32[]{:S(2)}) collective-permute-start(bf16[256,1792]{1,0:T(8,128)(2,1)S(1)} %constant_dynamic-slice_fusion.8), channel_id=1, source_target_pairs={{0,4},{4,0},{8,12},{12,8},{16,20},{20,16},{24,28},{28,24},{1,5},{5... | collective-permute-start | bytes 2752520 | tf_op jit(solution)/shard_map/ppermute | solution.py:103
  125.0 30.2 %collective-permute-start.24 = (bf16[256,1792]{1,0:T(8,128)(2,1)S(1)}, bf16[256,1792]{1,0:T(8,128)(2,1)S(1)}, u32[]{:S(2)}, u32[]{:S(2)}) collective-permute-start(bf16[256,1792]{1,0:T(8,128)(2,1)S(1)} %constant_dynamic-slice_fusion.7), channel_id=1, source_target_pairs={{0,4},{4,0},{8,12},{12,8},{16,20},{20,16},{24,28},{28,24},{1,5},{5... | collective-permute-start | bytes 2752520 | tf_op jit(solution)/shard_map/ppermute | solution.py:103
  125.5 29.7 %collective-permute-start.20 = (bf16[256,1792]{1,0:T(8,128)(2,1)S(1)}, bf16[256,1792]{1,0:T(8,128)(2,1)S(1)}, u32[]{:S(2)}, u32[]{:S(2)}) collective-permute-start(bf16[256,1792]{1,0:T(8,128)(2,1)S(1)} %constant_dynamic-slice_fusion.6), channel_id=1, source_target_pairs={{0,4},{4,0},{8,12},{12,8},{16,20},{20,16},{24,28},{28,24},{1,5},{5... | collective-permute-start | bytes 2752520 | tf_op jit(solution)/shard_map/ppermute | solution.py:103
  150.5 64.6 %collective-permute-start.43 = (bf16[256,1792]{1,0:T(8,128)(2,1)S(1)}, bf16[256,1792]{1,0:T(8,128)(2,1)S(1)}, u32[]{:S(2)}, u32[]{:S(2)}) collective-permute-start(bf16[256,1792]{1,0:T(8,128)(2,1)S(1)} %constant_dynamic-update-slice_fusion.47), channel_id=1, source_target_pairs={{0,4},{4,0},{8,12},{12,8},{16,20},{20,16},{24,28},{28,24},{1,5},{5... | collective-permute-start | bytes 2752520 | tf_op jit(solution)/shard_map/ppermute | solution.py:119
  154.0 53.3 %collective-permute-start.15 = (bf16[256,1792]{1,0:T(8,128)(2,1)S(1)}, bf16[256,1792]{1,0:T(8,128)(2,1)S(1)}, u32[]{:S(2)}, u32[]{:S(2)}) collective-permute-start(bf16[256,1792]{1,0:T(8,128)(2,1)S(1)} %constant_dynamic-update-slice_fusion.71), channel_id=1, source_target_pairs={{0,4},{4,0},{8,12},{12,8},{16,20},{20,16},{24,28},{28,24},{1,5},{5... | collective-permute-start | bytes 2752520 | tf_op jit(solution)/shard_map/ppermute | solution.py:119
  154.7 46.3 %collective-permute-start.19 = (bf16[256,1792]{1,0:T(8,128)(2,1)S(1)}, bf16[256,1792]{1,0:T(8,128)(2,1)S(1)}, u32[]{:S(2)}, u32[]{:S(2)}) collective-permute-start(bf16[256,1792]{1,0:T(8,128)(2,1)S(1)} %constant_dynamic-update-slice_fusion.65), channel_id=1, source_target_pairs={{0,4},{4,0},{8,12},{12,8},{16,20},{20,16},{24,28},{28,24},{1,5},{5... | collective-permute-start | bytes 2752520 | tf_op jit(solution)/shard_map/ppermute | solution.py:119
  199.9 40.0 %collective-permute-start.64 = (bf16[64,1792]{1,0:T(8,128)(2,1)S(1)}, bf16[64,1792]{1,0:T(8,128)(2,1)}, u32[]{:S(2)}, u32[]{:S(2)}) collective-permute-start(bf16[64,1792]{1,0:T(8,128)(2,1)S(1)} %get-tuple-element.57), channel_id=1, source_target_pairs={{0,8},{4,20},{8,24},{12,4},{16,0},{20,28},{24,16},{28,12},{1,9},{5... | collective-permute-start | bytes 688136 | tf_op jit(solution)/shard_map/ppermute | solution.py:117
  217.2 47.5 %collective-permute-start.52 = (bf16[256,1792]{1,0:T(8,128)(2,1)}, bf16[256,1792]{1,0:T(8,128)(2,1)S(1)}, u32[]{:S(2)}, u32[]{:S(2)}) collective-permute-start(bf16[256,1792]{1,0:T(8,128)(2,1)} %constant_dynamic-slice_fusion.5), channel_id=1, source_target_pairs={{0,4},{4,0},{8,12},{12,8},{16,20},{20,16},{24,28},{28,24},{1,5},{5... | collective-permute-start | bytes 2752520 | tf_op jit(solution)/shard_map/ppermute | solution.py:103
  217.3 48.0 %collective-permute-start.48 = (bf16[256,1792]{1,0:T(8,128)(2,1)S(1)}, bf16[256,1792]{1,0:T(8,128)(2,1)S(1)}, u32[]{:S(2)}, u32[]{:S(2)}) collective-permute-start(bf16[256,1792]{1,0:T(8,128)(2,1)S(1)} %constant_dynamic-slice_fusion.4), channel_id=1, source_target_pairs={{0,4},{4,0},{8,12},{12,8},{16,20},{20,16},{24,28},{28,24},{1,5},{5... | collective-permute-start | bytes 2752520 | tf_op jit(solution)/shard_map/ppermute | solution.py:103
  217.8 48.8 %collective-permute-start.44 = (bf16[256,1792]{1,0:T(8,128)(2,1)S(1)}, bf16[256,1792]{1,0:T(8,128)(2,1)}, u32[]{:S(2)}, u32[]{:S(2)}) collective-permute-start(bf16[256,1792]{1,0:T(8,128)(2,1)S(1)} %constant_dynamic-slice_fusion.3), channel_id=1, source_target_pairs={{0,4},{4,0},{8,12},{12,8},{16,20},{20,16},{24,28},{28,24},{1,5},{5... | collective-permute-start | bytes 2752520 | tf_op jit(solution)/shard_map/ppermute | solution.py:103
  231.5 10.1 %collective-permute-start.32 = (bf16[64,1792]{1,0:T(8,128)(2,1)S(1)}, bf16[64,1792]{1,0:T(8,128)(2,1)S(1)}, u32[]{:S(2)}, u32[]{:S(2)}) collective-permute-start(bf16[64,1792]{1,0:T(8,128)(2,1)S(1)} %get-tuple-element.54), channel_id=1, source_target_pairs={{0,8},{4,20},{8,24},{12,4},{16,0},{20,28},{24,16},{28,12},{1,9},{5... | collective-permute-start | bytes 688136 | tf_op jit(solution)/shard_map/ppermute | solution.py:117
  260.4 72.8 %collective-permute-start.67 = (bf16[256,1792]{1,0:T(8,128)(2,1)S(1)}, bf16[256,1792]{1,0:T(8,128)(2,1)}, u32[]{:S(2)}, u32[]{:S(2)}) collective-permute-start(bf16[256,1792]{1,0:T(8,128)(2,1)S(1)} %constant_dynamic-update-slice_fusion.29), channel_id=1, source_target_pairs={{0,4},{4,0},{8,12},{12,8},{16,20},{20,16},{24,28},{28,24},{1,5},{5... | collective-permute-start | bytes 2752520 | tf_op jit(solution)/shard_map/ppermute | solution.py:119
  264.0 51.3 %collective-permute-start.35 = (bf16[256,1792]{1,0:T(8,128)(2,1)S(1)}, bf16[256,1792]{1,0:T(8,128)(2,1)}, u32[]{:S(2)}, u32[]{:S(2)}) collective-permute-start(bf16[256,1792]{1,0:T(8,128)(2,1)S(1)} %constant_dynamic-update-slice_fusion.59), channel_id=1, source_target_pairs={{0,4},{4,0},{8,12},{12,8},{16,20},{20,16},{24,28},{28,24},{1,5},{5... | collective-permute-start | bytes 2752520 | tf_op jit(solution)/shard_map/ppermute | solution.py:119
  264.7 60.6 %collective-permute-start.39 = (bf16[256,1792]{1,0:T(8,128)(2,1)S(1)}, bf16[256,1792]{1,0:T(8,128)(2,1)}, u32[]{:S(2)}, u32[]{:S(2)}) collective-permute-start(bf16[256,1792]{1,0:T(8,128)(2,1)S(1)} %constant_dynamic-update-slice_fusion.53), channel_id=1, source_target_pairs={{0,4},{4,0},{8,12},{12,8},{16,20},{20,16},{24,28},{28,24},{1,5},{5... | collective-permute-start | bytes 2752520 | tf_op jit(solution)/shard_map/ppermute | solution.py:119
  283.5 7.4 %collective-permute-start.53 = (bf16[64,1792]{1,0:T(8,128)(2,1)S(1)}, bf16[64,1792]{1,0:T(8,128)(2,1)S(1)}, u32[]{:S(2)}, u32[]{:S(2)}) collective-permute-start(bf16[64,1792]{1,0:T(8,128)(2,1)S(1)} %dynamic-slice_convert_fusion.3), channel_id=1, source_target_pairs={{0,8},{4,20},{8,24},{12,4},{16,0},{20,28},{24,16},{28,12},{1,9},{5... | collective-permute-start | bytes 688136 | tf_op jit(solution)/shard_map/ppermute | solution.py:108
  313.0 30.0 %collective-permute-start.60 = (bf16[64,1792]{1,0:T(8,128)(2,1)S(1)}, bf16[64,1792]{1,0:T(8,128)(2,1)S(1)}, u32[]{:S(2)}, u32[]{:S(2)}) collective-permute-start(bf16[64,1792]{1,0:T(8,128)(2,1)S(1)} %get-tuple-element.44), channel_id=1, source_target_pairs={{0,8},{4,20},{8,24},{12,4},{16,0},{20,28},{24,16},{28,12},{1,9},{5... | collective-permute-start | bytes 688136 | tf_op jit(solution)/shard_map/ppermute | solution.py:117
  313.8 29.2 %collective-permute-start.56 = (bf16[64,1792]{1,0:T(8,128)(2,1)S(1)}, bf16[64,1792]{1,0:T(8,128)(2,1)S(1)}, u32[]{:S(2)}, u32[]{:S(2)}) collective-permute-start(bf16[64,1792]{1,0:T(8,128)(2,1)S(1)} %get-tuple-element.41), channel_id=1, source_target_pairs={{0,8},{4,20},{8,24},{12,4},{16,0},{20,28},{24,16},{28,12},{1,9},{5... | collective-permute-start | bytes 688136 | tf_op jit(solution)/shard_map/ppermute | solution.py:117
  315.2 28.6 %collective-permute-start.88 = (bf16[64,1792]{1,0:T(8,128)(2,1)S(1)}, bf16[64,1792]{1,0:T(8,128)(2,1)S(1)}, u32[]{:S(2)}, u32[]{:S(2)}) collective-permute-start(bf16[64,1792]{1,0:T(8,128)(2,1)S(1)} %get-tuple-element.37), channel_id=1, source_target_pairs={{0,8},{4,20},{8,24},{12,4},{16,0},{20,28},{24,16},{28,12},{1,9},{5... | collective-permute-start | bytes 688136 | tf_op jit(solution)/shard_map/ppermute | solution.py:117
  342.4 21.8 %collective-permute-start.76 = (bf16[256,1792]{1,0:T(8,128)(2,1)S(1)}, bf16[256,1792]{1,0:T(8,128)(2,1)S(1)}, u32[]{:S(2)}, u32[]{:S(2)}) collective-permute-start(bf16[256,1792]{1,0:T(8,128)(2,1)S(1)} %constant_dynamic-slice_fusion.2), channel_id=1, source_target_pairs={{0,4},{4,0},{8,12},{12,8},{16,20},{20,16},{24,28},{28,24},{1,5},{5... | collective-permute-start | bytes 2752520 | tf_op jit(solution)/shard_map/ppermute | solution.py:103
  342.4 23.3 %collective-permute-start.72 = (bf16[256,1792]{1,0:T(8,128)(2,1)S(1)}, bf16[256,1792]{1,0:T(8,128)(2,1)S(1)}, u32[]{:S(2)}, u32[]{:S(2)}) collective-permute-start(bf16[256,1792]{1,0:T(8,128)(2,1)S(1)} %constant_dynamic-slice_fusion.1), channel_id=1, source_target_pairs={{0,4},{4,0},{8,12},{12,8},{16,20},{20,16},{24,28},{28,24},{1,5},{5... | collective-permute-start | bytes 2752520 | tf_op jit(solution)/shard_map/ppermute | solution.py:103
  342.9 23.9 %collective-permute-start.68 = (bf16[256,1792]{1,0:T(8,128)(2,1)S(1)}, bf16[256,1792]{1,0:T(8,128)(2,1)S(1)}, u32[]{:S(2)}, u32[]{:S(2)}) collective-permute-start(bf16[256,1792]{1,0:T(8,128)(2,1)S(1)} %constant_dynamic-slice_fusion), channel_id=1, source_target_pairs={{0,4},{4,0},{8,12},{12,8},{16,20},{20,16},{24,28},{28,24},{1,5},{5... | collective-permute-start | bytes 2752520 | tf_op jit(solution)/shard_map/ppermute | solution.py:103
  343.9 7.6 %collective-permute-start.57 = (bf16[64,1792]{1,0:T(8,128)(2,1)S(1)}, bf16[64,1792]{1,0:T(8,128)(2,1)S(1)}, u32[]{:S(2)}, u32[]{:S(2)}) collective-permute-start(bf16[64,1792]{1,0:T(8,128)(2,1)S(1)} %collective-permute-done.56), channel_id=1, source_target_pairs={{0,8},{4,20},{8,24},{12,4},{16,0},{20,28},{24,16},{28,12},{1,9},{5... | collective-permute-start | bytes 688136 | tf_op jit(solution)/shard_map/ppermute | solution.py:117
  361.1 26.3 %collective-permute-start.63 = (bf16[256,1792]{1,0:T(8,128)(2,1)S(1)}, bf16[256,1792]{1,0:T(8,128)(2,1)S(1)}, u32[]{:S(2)}, u32[]{:S(2)}) collective-permute-start(bf16[256,1792]{1,0:T(8,128)(2,1)S(1)} %constant_dynamic-update-slice_fusion.35), channel_id=1, source_target_pairs={{0,4},{4,0},{8,12},{12,8},{16,20},{20,16},{24,28},{28,24},{1,5},{5... | collective-permute-start | bytes 2752520 | tf_op jit(solution)/shard_map/ppermute | solution.py:119
  363.6 29.6 %collective-permute-start.59 = (bf16[256,1792]{1,0:T(8,128)(2,1)S(1)}, bf16[256,1792]{1,0:T(8,128)(2,1)S(1)}, u32[]{:S(2)}, u32[]{:S(2)}) collective-permute-start(bf16[256,1792]{1,0:T(8,128)(2,1)S(1)} %constant_dynamic-update-slice_fusion.41), channel_id=1, source_target_pairs={{0,4},{4,0},{8,12},{12,8},{16,20},{20,16},{24,28},{28,24},{1,5},{5... | collective-permute-start | bytes 2752520 | tf_op jit(solution)/shard_map/ppermute | solution.py:119
  364.3 33.1 %collective-permute-start.91 = (bf16[256,1792]{1,0:T(8,128)(2,1)S(1)}, bf16[256,1792]{1,0:T(8,128)(2,1)S(1)}, u32[]{:S(2)}, u32[]{:S(2)}) collective-permute-start(bf16[256,1792]{1,0:T(8,128)(2,1)S(1)} %constant_dynamic-update-slice_fusion.8), channel_id=1, source_target_pairs={{0,4},{4,0},{8,12},{12,8},{16,20},{20,16},{24,28},{28,24},{1,5},{5... | collective-permute-start | bytes 2752520 | tf_op jit(solution)/shard_map/ppermute | solution.py:119
  366.9 7.4 %collective-permute-start.73 = (bf16[64,1792]{1,0:T(8,128)(2,1)S(1)}, bf16[64,1792]{1,0:T(8,128)(2,1)S(1)}, u32[]{:S(2)}, u32[]{:S(2)}) collective-permute-start(bf16[64,1792]{1,0:T(8,128)(2,1)S(1)} %dynamic-slice_convert_fusion.1), channel_id=1, source_target_pairs={{0,8},{4,20},{8,24},{12,4},{16,0},{20,28},{24,16},{28,12},{1,9},{5... | collective-permute-start | bytes 688136 | tf_op jit(solution)/shard_map/ppermute | solution.py:108
  383.9 19.7 %collective-permute-start.79 = (bf16[64,1792]{1,0:T(8,128)(2,1)S(1)}, bf16[64,1792]{1,0:T(8,128)(2,1)S(1)}, u32[]{:S(2)}, u32[]{:S(2)}) collective-permute-start(bf16[64,1792]{1,0:T(8,128)(2,1)S(1)} %add_convert_fusion.1), channel_id=1, source_target_pairs={{0,8},{4,20},{8,24},{12,4},{16,0},{20,28},{24,16},{28,12},{1,9},{5... | collective-permute-start | bytes 688136 | tf_op jit(solution)/shard_map/ppermute | solution.py:108
  386.6 17.0 %collective-permute-start.75 = (bf16[64,1792]{1,0:T(8,128)(2,1)S(1)}, bf16[64,1792]{1,0:T(8,128)(2,1)S(1)}, u32[]{:S(2)}, u32[]{:S(2)}) collective-permute-start(bf16[64,1792]{1,0:T(8,128)(2,1)S(1)} %add_convert_fusion.3), channel_id=1, source_target_pairs={{0,8},{4,20},{8,24},{12,4},{16,0},{20,28},{24,16},{28,12},{1,9},{5... | collective-permute-start | bytes 688136 | tf_op jit(solution)/shard_map/ppermute | solution.py:108
  387.4 16.2 %collective-permute-start.71 = (bf16[64,1792]{1,0:T(8,128)(2,1)S(1)}, bf16[64,1792]{1,0:T(8,128)(2,1)S(1)}, u32[]{:S(2)}, u32[]{:S(2)}) collective-permute-start(bf16[64,1792]{1,0:T(8,128)(2,1)S(1)} %add_convert_fusion.5), channel_id=1, source_target_pairs={{0,8},{4,20},{8,24},{12,4},{16,0},{20,28},{24,16},{28,12},{1,9},{5... | collective-permute-start | bytes 688136 | tf_op jit(solution)/shard_map/ppermute | solution.py:108
  407.0 7.9 %collective-permute-start.92 = (bf16[64,1792]{1,0:T(8,128)(2,1)S(1)}, bf16[64,1792]{1,0:T(8,128)(2,1)S(1)}, u32[]{:S(2)}, u32[]{:S(2)}) collective-permute-start(bf16[64,1792]{1,0:T(8,128)(2,1)S(1)} %get-tuple-element.35), channel_id=1, source_target_pairs={{0,8},{4,20},{8,24},{12,4},{16,0},{20,28},{24,16},{28,12},{1,9},{5... | collective-permute-start | bytes 688136 | tf_op jit(solution)/shard_map/ppermute | solution.py:117
  410.0 7.4 %collective-permute-start.81 = (bf16[64,1792]{1,0:T(8,128)(2,1)S(1)}, bf16[64,1792]{1,0:T(8,128)(2,1)S(1)}, u32[]{:S(2)}, u32[]{:S(2)}) collective-permute-start(bf16[64,1792]{1,0:T(8,128)(2,1)S(1)} %collective-permute-done.80), channel_id=1, source_target_pairs={{0,8},{4,20},{8,24},{12,4},{16,0},{20,28},{24,16},{28,12},{1,9},{5... | collective-permute-start | bytes 688136 | tf_op jit(solution)/shard_map/ppermute | solution.py:117
  412.5 7.4 %collective-permute-start.85 = (bf16[64,1792]{1,0:T(8,128)(2,1)S(1)}, bf16[64,1792]{1,0:T(8,128)(2,1)S(1)}, u32[]{:S(2)}, u32[]{:S(2)}) collective-permute-start(bf16[64,1792]{1,0:T(8,128)(2,1)S(1)} %collective-permute-done.84), channel_id=1, source_target_pairs={{0,8},{4,20},{8,24},{12,4},{16,0},{20,28},{24,16},{28,12},{1,9},{5... | collective-permute-start | bytes 688136 | tf_op jit(solution)/shard_map/ppermute | solution.py:117
  415.0 7.4 %collective-permute-start.93 = (bf16[64,1792]{1,0:T(8,128)(2,1)S(1)}, bf16[64,1792]{1,0:T(8,128)(2,1)S(1)}, u32[]{:S(2)}, u32[]{:S(2)}) collective-permute-start(bf16[64,1792]{1,0:T(8,128)(2,1)S(1)} %collective-permute-done.92), channel_id=1, source_target_pairs={{0,8},{4,20},{8,24},{12,4},{16,0},{20,28},{24,16},{28,12},{1,9},{5... | collective-permute-start | bytes 688136 | tf_op jit(solution)/shard_map/ppermute | solution.py:117
  417.4 7.4 %collective-permute-start.82 = (bf16[64,1792]{1,0:T(8,128)(2,1)S(1)}, bf16[64,1792]{1,0:T(8,128)(2,1)S(1)}, u32[]{:S(2)}, u32[]{:S(2)}) collective-permute-start(bf16[64,1792]{1,0:T(8,128)(2,1)S(1)} %collective-permute-done.81), channel_id=1, source_target_pairs={{0,8},{4,20},{8,24},{12,4},{16,0},{20,28},{24,16},{28,12},{1,9},{5... | collective-permute-start | bytes 688136 | tf_op jit(solution)/shard_map/ppermute | solution.py:117
  419.9 7.4 %collective-permute-start.86 = (bf16[64,1792]{1,0:T(8,128)(2,1)S(1)}, bf16[64,1792]{1,0:T(8,128)(2,1)S(1)}, u32[]{:S(2)}, u32[]{:S(2)}) collective-permute-start(bf16[64,1792]{1,0:T(8,128)(2,1)S(1)} %collective-permute-done.85), channel_id=1, source_target_pairs={{0,8},{4,20},{8,24},{12,4},{16,0},{20,28},{24,16},{28,12},{1,9},{5... | collective-permute-start | bytes 688136 | tf_op jit(solution)/shard_map/ppermute | solution.py:117
  422.3 7.4 %collective-permute-start.94 = (bf16[64,1792]{1,0:T(8,128)(2,1)S(1)}, bf16[64,1792]{1,0:T(8,128)(2,1)S(1)}, u32[]{:S(2)}, u32[]{:S(2)}) collective-permute-start(bf16[64,1792]{1,0:T(8,128)(2,1)S(1)} %collective-permute-done.93), channel_id=1, source_target_pairs={{0,8},{4,20},{8,24},{12,4},{16,0},{20,28},{24,16},{28,12},{1,9},{5... | collective-permute-start | bytes 688136 | tf_op jit(solution)/shard_map/ppermute | solution.py:117
  427.3 7.5 %collective-permute-start.87 = (bf16[256,1792]{1,0:T(8,128)(2,1)S(1)}, bf16[256,1792]{1,0:T(8,128)(2,1)S(1)}, u32[]{:S(2)}, u32[]{:S(2)}) collective-permute-start(bf16[256,1792]{1,0:T(8,128)(2,1)S(1)} %constant_dynamic-update-slice_fusion.17), channel_id=1, source_target_pairs={{0,4},{4,0},{8,12},{12,8},{16,20},{20,16},{24,28},{28,24},{1,5},{5... | collective-permute-start | bytes 2752520 | tf_op jit(solution)/shard_map/ppermute | solution.py:119
  429.7 17.5 %collective-permute-start.95 = (bf16[256,1792]{1,0:T(8,128)(2,1)S(1)}, bf16[256,1792]{1,0:T(8,128)(2,1)}, u32[]{:S(2)}, u32[]{:S(2)}) collective-permute-start(bf16[256,1792]{1,0:T(8,128)(2,1)S(1)} %constant_dynamic-update-slice_fusion.2), channel_id=1, source_target_pairs={{0,4},{4,0},{8,12},{12,8},{16,20},{20,16},{24,28},{28,24},{1,5},{5... | collective-permute-start | bytes 2752520 | tf_op jit(solution)/shard_map/ppermute | solution.py:119
  (73 other events, 460.9 us)
Sparse Core Ops, SparseCore 0:
  10.1 48.6 all-gather.1
  441.7 25.5 reduce-scatter.1
where the time goes:
time: 484 us; the launch traced here: 475 us
  waiting for transfers between devices  188 us (39%)
  matrix products  132 us (27%)
  starting transfers between devices  77.8 us (16%)
  local copies, waits for them, and re-layouts  45.8 us (9%)
  between operations  19.2 us (4%)
  other arithmetic  12.3 us (3%)
    ppermute x36, waiting for transfers between devices, per_device(): got = lax.ppermute(tuple((a.astype(BF16) for a in acc)), 'row', ring_pairs)  67.5 us
    ppermute x36, waiting for transfers between devices, per_device(): cur = lax.ppermute(cur, 'row', ring_pairs)  64.3 us
    dot_general x12, matrix products, contract_cols(): lax.dot_general(left, right, (((1,), (1,)), ((), ())), preferred_element_...  57.5 us
    all_gather x1, waiting for transfers between devices, per_device(): lax.all_gather(jnp.concatenate([tokens, cotangent], axis=1), 'col', axis=...  49.6 us
    dot_general x12, matrix products, contract_rows(): lax.dot_general(left, right, (((0,), (0,)), ((), ())), preferred_element_...  39.8 us
    ppermute x36, starting transfers between devices, per_device(): cur = lax.ppermute(cur, 'row', ring_pairs)  38.6 us
    ppermute x36, starting transfers between devices, per_device(): got = lax.ppermute(tuple((a.astype(BF16) for a in acc)), 'row', ring_pairs)  34.9 us
    dot_general x4, matrix products, per_device(): jnp.dot(x_chunk, gw, preferred_element_type=F32).astype(BF16)  17.2 us
  transfers between devices with their start and end apart: 98, of which 65 were waited for; matrix products, arithmetic and copies ran while one was open for 33% of the time, Pallas kernels for 0%

commit v1 on v0

--- a/solution.py
+++ b/solution.py
@@ -4,6 +4,7 @@
 from jax.sharding import PartitionSpec as P
 
 N_CHUNKS = 4
+GROUP = 2
 F32 = jnp.float32
 BF16 = jnp.bfloat16
 
@@ -86,6 +87,7 @@
         x_chunk, dy_chunk = x_panel, dy_panel
         reduced = {}
         grads = {}
+        exchanged = {}
         for j in range(N_CHUNKS):
             cols = slice(j * w, (j + 1) * w)
             gw = gate_weight[:, cols]
@@ -97,11 +99,16 @@
             )
             own = rows(parts, core * half, half)
             other = rows(parts, (1 - core) * half, half)
-            waits = tuple(reduced.get(j - 1, ())) + tuple(grads.get(j - 2, ()))
-            if waits:
-                other, _ = lax.optimization_barrier((other, waits))
+            g = j // GROUP
+            before = [i for i in range(N_CHUNKS) if i // GROUP == g - 1]
+            if before:
+                other, _ = lax.optimization_barrier((other, [reduced[i] for i in before]))
             got = lax.ppermute(other, "row", core_pairs)
-            x_chunk, dy_chunk, _ = lax.optimization_barrier((x_panel, dy_panel, got))
+            exchanged[j] = got
+            if j % GROUP == GROUP - 1:
+                x_chunk, dy_chunk, _ = lax.optimization_barrier(
+                    (x_panel, dy_panel, [exchanged[i] for i in range(j - GROUP + 1, j + 1)])
+                )
             summed = tuple(a.astype(F32) + b.astype(F32) for a, b in zip(own, got))
             acc = rows(summed, ((pos - 1) % chips) * block, block)
             for s in range(chips - 1):
@@ -109,6 +116,8 @@
                 mine = rows(summed, ((pos - s - 2) % chips) * block, block)
                 acc = tuple(a.astype(F32) + b for a, b in zip(got, mine))
             reduced[j] = acc
+            if before:
+                acc, _ = lax.optimization_barrier((acc, [grads[i] for i in before]))
             act = activations(*acc)
             held = tuple(jnp.zeros((half, w), BF16) for _ in act)
             held = put(held, act, pos * block)

time: 484 us -> 533 us (1.10)
  starting transfers between devices: 77.8 us -> 94.4 us
  local copies, waits for them, and re-layouts: 45.8 us -> 59.3 us
  other arithmetic: 12.3 us -> 24.7 us
    ppermute x36, waiting for transfers between devices: 64.3 us -> 80.1 us  [per_device(): cur = lax.ppermute(cur, 'row', ring_pairs)]
    ppermute x36, starting transfers between devices: 34.9 us -> 48.1 us  [per_device(): got = lax.ppermute(tuple((a.astype(BF16) for a in acc)), 'row', ring_pairs)]
    dynamic_update_slice x60, local copies, waits for them, and re-layouts: 8.46 us -> 19.7 us  [put(): lax.dynamic_update_slice_in_dim(a, p, start, 0)]
    reduce_scatter x1, waiting for transfers between devices: 6.51 us -> 0.01 us  [per_device(): lax.psum_scatter(input_acc.astype(BF16), 'col', scatter_dimension=0, tile...]
    ppermute x36, waiting for transfers between devices: 67.5 us -> 61.3 us  [per_device(): got = lax.ppermute(tuple((a.astype(BF16) for a in acc)), 'row', ring_pairs)]
    add x0 -> x6, other arithmetic: none -> 5.59 us  [per_device(): acc = tuple((a.astype(F32) + b for a, b in zip(got, mine)))]
  transfers between devices with their start and end apart: 98 -> 98, of which waited for: 65 -> 57; matrix products, arithmetic and copies ran while one was open for 33% -> 34% of each run, Pallas kernels for 0% -> 0%
where the time goes in v1:
time: 533 us; the launch traced here: 523 us
  waiting for transfers between devices  193 us (36%)
  matrix products  132 us (25%)
  starting transfers between devices  94.4 us (18%)
  local copies, waits for them, and re-layouts  59.3 us (11%)
  other arithmetic  24.7 us (5%)
  between operations  19.4 us (4%)
    ppermute x36, waiting for transfers between devices, per_device(): cur = lax.ppermute(cur, 'row', ring_pairs)  80.1 us
    ppermute x36, waiting for transfers between devices, per_device(): got = lax.ppermute(tuple((a.astype(BF16) for a in acc)), 'row', ring_pairs)  61.3 us
    dot_general x12, matrix products, contract_cols(): lax.dot_general(left, right, (((1,), (1,)), ((), ())), preferred_element_...  54 us
    all_gather x1, waiting for transfers between devices, per_device(): lax.all_gather(jnp.concatenate([tokens, cotangent], axis=1), 'col', axis=...  49.6 us
    ppermute x36, starting transfers between devices, per_device(): got = lax.ppermute(tuple((a.astype(BF16) for a in acc)), 'row', ring_pairs)  48.1 us
    dot_general x12, matrix products, contract_rows(): lax.dot_general(left, right, (((0,), (0,)), ((), ())), preferred_element_...  44.3 us
    ppermute x36, starting transfers between devices, per_device(): cur = lax.ppermute(cur, 'row', ring_pairs)  41.9 us
    dynamic_update_slice x60, local copies, waits for them, and re-layouts, put(): lax.dynamic_update_slice_in_dim(a, p, start, 0)  19.7 us
  transfers between devices with their start and end apart: 98, of which 57 were waited for; matrix products, arithmetic and copies ran while one was open for 34% of the time, Pallas kernels for 0%

profile of v1, /device:TPU:0, one launch (start us, length us, event | category | flops | bytes accessed | tf_op | source)
XLA Modules:
  0.0 522.9 jit_solution(11754270235611317096)
XLA Ops:
  9.2 49.6 %all-gather.2.cloned.1.call-done = bf16[512,2048]{1,0:T(8,128)(2,1)} async-done(((bf16[128,2048]{1,0:T(8,128)(2,1)}), bf16[512,2048]{1,0:T(8,128)(2,1)}) %all-gather.2.cloned.1.call-update) | async-done | bytes 2097168 | tf_op jit(solution)/shard_map/all_gather | solution.py:72
  58.8 4.6 fusion.73
  63.6 4.6 fusion.55
  69.5 4.1 fusion.52
  75.7 4.1 fusion.49
  81.3 4.1 fusion.70
  87.1 4.1 fusion.46
  98.6 4.5 fusion.67
  103.1 4.3 fusion.64
  111.7 4.1 fusion.61
  115.8 4.3 fusion.58
  187.5 3.9 collective-permute-done.37
  193.5 3.9 collective-permute-done.33
  198.8 4.5 collective-permute-done.17
  204.9 4.5 collective-permute-done.13
  210.9 4.5 collective-permute-done.57
  217.6 3.9 collective-permute-done.53
  223.6 3.9 collective-permute-done.38
  235.2 4.3 collective-permute-done.18
  241.2 4.3 collective-permute-done.14
  247.0 4.5 collective-permute-done.58
  253.7 3.9 collective-permute-done.54
  267.2 4.3 collective-permute-done.77
  273.0 4.5 collective-permute-done.73
  279.1 4.5 collective-permute-done.69
  285.1 4.5 collective-permute-done.49
  291.1 4.5 collective-permute-done.45
  297.1 4.5 collective-permute-done.41
  303.1 4.5 collective-permute-done.78
  309.9 3.8 collective-permute-done.74
  321.9 3.8 collective-permute-done.50
  327.9 3.9 collective-permute-done.46
  346.2 6.1 %fusion.30 = f32[512,1024]{1,0:T(8,128)} fusion(bf16[512,1792]{1,0:T(8,128)(2,1)S(1)} %constant_dynamic-update-slice_fusion.57, bf16[1024,7168]{1,0:T(8,128)(2,1)} %param.8), kind=kOutput, calls=%fused_computation.42 | convolution fusion | flops 1879048192 | bytes 7602176 | tf_op jit(solution)/shard_map/dot_general | solution.py:28
  360.2 3.9 constant_dynamic-update-slice_fusion.14
  364.2 10.1 %fusion.42 = f32[512,1024]{1,0:T(8,128)} fusion(bf16[512,1792]{1,0:T(8,128)(2,1)} %copy-done.11, bf16[1024,7168]{1,0:T(8,128)(2,1)} %param.9), kind=kOutput, calls=%fused_computation.54 | convolution fusion | flops 1879048192 | bytes 7602176 | tf_op jit(solution)/shard_map/dot_general | solution.py:28
  377.5 4.1 constant_dynamic-update-slice_fusion.13
  390.4 5.6 %fusion.82 = f32[512,1024]{1,0:T(8,128)} fusion(f32[512,1024]{1,0:T(8,128)S(1)} %copy-done.45, bf16[512,1792]{1,0:T(8,128)(2,1)S(1)} %copy-done.13, bf16[1024,7168]{1,0:T(8,128)(2,1)} %param.8), kind=kOutput, calls=%fused_computation.84 | convolution fusion | flops 1879572480 | bytes 9699328 | tf_op jit(solution)/shard_map/dot_general | solution.py:28
  399.5 10.6 %dynamic_update_slice.320 = bf16[7168,1024]{1,0:T(8,128)(2,1)} pad(bf16[1792,1024]{1,0:T(8,128)(2,1)S(1)} %convolution_convert_fusion.11, bf16[]{:T(256)} %constant.117.clone.1), padding=0_5376x0_0 | pad | bytes 18350082 | tf_op jit(solution)/shard_map/dynamic_update_slice | solution.py:144
  410.1 4.8 add_add_fusion
  416.3 4.0 constant_dynamic-update-slice_fusion.12
  473.3 4.8 fusion.22
  481.7 5.3 %add_convert_fusion = bf16[512,1024]{1,0:T(8,128)(2,1)} fusion(f32[512,1024]{1,0:T(8,128)S(1)} %fusion.18, f32[512,1024]{1,0:T(8,128)S(1)} %fusion.22, f32[512,1024]{1,0:T(8,128)S(1)} %add_add_fusion, f32[512,1024]{1,0:T(8,128)S(1)} %fusion.26, bf16[512,1792]{1,0:T(8,128)(2,1)S(1)} %constant_dynamic-update-slice_fusion.15, bf16[1024,7168]{1,0:T(8,128)(2,1)} %param.9), kind=kOutput, calls=%fused_computation.70 | convolution fusion | flops 1881669632 | bytes 14942208 | tf_op jit(solution)/shard_map/dot_general | solution.py:28
  487.1 5.9 %fusion.3 = bf16[1024,7168]{1,0:T(8,128)(2,1)} fusion(bf16[1024,7168]{1,0:T(8,128)(2,1)} %copy-done, bf16[512,1792]{1,0:T(8,128)(2,1)} %copy-done.22, bf16[512,2048]{1,0:T(8,128)(2,1)} %all-gather.2.cloned.1.call-done), kind=kOutput, calls=%fused_computation.7 | convolution fusion | flops 1880883200 | bytes 6553600 | tf_op jit(solution)/shard_map/dot_general | solution.py:22
  493.0 4.2 fusion.2
  500.0 4.0 fusion.5
  504.0 4.0 fusion.4
  508.0 3.9 fusion.1
  511.9 3.9 fusion
  (464 shorter events, 236.7 us)
Async XLA Ops:
  7.2 51.6 %all-gather.2.cloned.1.call-start = ((), (), s32[]{:S(2)}) async-start(), calls=%async_computation.1 | async-start | bytes 2621440 | tf_op jit(solution)/shard_map/all_gather | solution.py:72
  9.1 506.8 %reduce-scatter.2.cloned.1.call-start = ((), (), s32[]{:S(2)}) async-start(), calls=%async_computation.2 | async-start | bytes 1310720 | tf_op jit(solution)/shard_map/reduce_scatter | solution.py:145
  63.5 30.0 %collective-permute-start.20 = (bf16[256,1792]{1,0:T(8,128)(2,1)S(1)}, bf16[256,1792]{1,0:T(8,128)(2,1)S(1)}, u32[]{:S(2)}, u32[]{:S(2)}) collective-permute-start(bf16[256,1792]{1,0:T(8,128)(2,1)S(1)} %constant_dynamic-slice_fusion.8), channel_id=1, source_target_pairs={{0,4},{4,0},{8,12},{12,8},{16,20},{20,16},{24,28},{28,24},{1,5},{5... | collective-permute-start | bytes 2752520 | tf_op jit(solution)/shard_map/ppermute | solution.py:106
  69.5 29.1 %collective-permute-start.28 = (bf16[256,1792]{1,0:T(8,128)(2,1)S(1)}, bf16[256,1792]{1,0:T(8,128)(2,1)}, u32[]{:S(2)}, u32[]{:S(2)}) collective-permute-start(bf16[256,1792]{1,0:T(8,128)(2,1)S(1)} %constant_dynamic-slice_fusion.6), channel_id=1, source_target_pairs={{0,4},{4,0},{8,12},{12,8},{16,20},{20,16},{24,28},{28,24},{1,5},{5... | collective-permute-start | bytes 2752520 | tf_op jit(solution)/shard_map/ppermute | solution.py:106
  75.2 23.4 %collective-permute-start.24 = (bf16[256,1792]{1,0:T(8,128)(2,1)}, bf16[256,1792]{1,0:T(8,128)(2,1)}, u32[]{:S(2)}, u32[]{:S(2)}) collective-permute-start(bf16[256,1792]{1,0:T(8,128)(2,1)} %constant_dynamic-slice_fusion.7), channel_id=1, source_target_pairs={{0,4},{4,0},{8,12},{12,8},{16,20},{20,16},{24,28},{28,24},{1,5},{5... | collective-permute-start | bytes 2752520 | tf_op jit(solution)/shard_map/ppermute | solution.py:106
  81.3 17.2 %collective-permute-start.8 = (bf16[256,1792]{1,0:T(8,128)(2,1)}, bf16[256,1792]{1,0:T(8,128)(2,1)}, u32[]{:S(2)}, u32[]{:S(2)}) collective-permute-start(bf16[256,1792]{1,0:T(8,128)(2,1)} %constant_dynamic-slice_fusion.9), channel_id=1, source_target_pairs={{0,4},{4,0},{8,12},{12,8},{16,20},{20,16},{24,28},{28,24},{1,5},{5... | collective-permute-start | bytes 2752520 | tf_op jit(solution)/shard_map/ppermute | solution.py:106
  120.3 14.7 %collective-permute-start.21 = (bf16[64,1792]{1,0:T(8,128)(2,1)S(1)}, bf16[64,1792]{1,0:T(8,128)(2,1)S(1)}, u32[]{:S(2)}, u32[]{:S(2)}) collective-permute-start(bf16[64,1792]{1,0:T(8,128)(2,1)S(1)} %dynamic-slice_convert_fusion.8), channel_id=1, source_target_pairs={{0,8},{4,20},{8,24},{12,4},{16,0},{20,28},{24,16},{28,12},{1,9},{5... | collective-permute-start | bytes 688136 | tf_op jit(solution)/shard_map/ppermute | solution.py:115
  123.3 13.3 %collective-permute-start.29 = (bf16[64,1792]{1,0:T(8,128)(2,1)S(1)}, bf16[64,1792]{1,0:T(8,128)(2,1)S(1)}, u32[]{:S(2)}, u32[]{:S(2)}) collective-permute-start(bf16[64,1792]{1,0:T(8,128)(2,1)S(1)} %dynamic-slice_convert_fusion.6), channel_id=1, source_target_pairs={{0,8},{4,20},{8,24},{12,4},{16,0},{20,28},{24,16},{28,12},{1,9},{5... | collective-permute-start | bytes 688136 | tf_op jit(solution)/shard_map/ppermute | solution.py:115
  141.1 12.3 %collective-permute-start.2 = (bf16[64,1792]{1,0:T(8,128)(2,1)S(1)}, bf16[64,1792]{1,0:T(8,128)(2,1)S(1)}, u32[]{:S(2)}, u32[]{:S(2)}) collective-permute-start(bf16[64,1792]{1,0:T(8,128)(2,1)S(1)} %add_convert_fusion.24), channel_id=1, source_target_pairs={{0,8},{4,20},{8,24},{12,4},{16,0},{20,28},{24,16},{28,12},{1,9},{5... | collective-permute-start | bytes 688136 | tf_op jit(solution)/shard_map/ppermute | solution.py:115
  143.5 12.3 %collective-permute-start.6 = (bf16[64,1792]{1,0:T(8,128)(2,1)S(1)}, bf16[64,1792]{1,0:T(8,128)(2,1)S(1)}, u32[]{:S(2)}, u32[]{:S(2)}) collective-permute-start(bf16[64,1792]{1,0:T(8,128)(2,1)S(1)} %add_convert_fusion.22), channel_id=1, source_target_pairs={{0,8},{4,20},{8,24},{12,4},{16,0},{20,28},{24,16},{28,12},{1,9},{5... | collective-permute-start | bytes 688136 | tf_op jit(solution)/shard_map/ppermute | solution.py:115
  146.0 12.3 %collective-permute-start.23 = (bf16[64,1792]{1,0:T(8,128)(2,1)S(1)}, bf16[64,1792]{1,0:T(8,128)(2,1)S(1)}, u32[]{:S(2)}, u32[]{:S(2)}) collective-permute-start(bf16[64,1792]{1,0:T(8,128)(2,1)S(1)} %add_convert_fusion.17), channel_id=1, source_target_pairs={{0,8},{4,20},{8,24},{12,4},{16,0},{20,28},{24,16},{28,12},{1,9},{5... | collective-permute-start | bytes 688136 | tf_op jit(solution)/shard_map/ppermute | solution.py:115
  148.5 12.3 %collective-permute-start.31 = (bf16[64,1792]{1,0:T(8,128)(2,1)S(1)}, bf16[64,1792]{1,0:T(8,128)(2,1)S(1)}, u32[]{:S(2)}, u32[]{:S(2)}) collective-permute-start(bf16[64,1792]{1,0:T(8,128)(2,1)S(1)} %add_convert_fusion.13), channel_id=1, source_target_pairs={{0,8},{4,20},{8,24},{12,4},{16,0},{20,28},{24,16},{28,12},{1,9},{5... | collective-permute-start | bytes 688136 | tf_op jit(solution)/shard_map/ppermute | solution.py:115
  150.9 13.1 %collective-permute-start.27 = (bf16[64,1792]{1,0:T(8,128)(2,1)S(1)}, bf16[64,1792]{1,0:T(8,128)(2,1)S(1)}, u32[]{:S(2)}, u32[]{:S(2)}) collective-permute-start(bf16[64,1792]{1,0:T(8,128)(2,1)S(1)} %add_convert_fusion.15), channel_id=1, source_target_pairs={{0,8},{4,20},{8,24},{12,4},{16,0},{20,28},{24,16},{28,12},{1,9},{5... | collective-permute-start | bytes 688136 | tf_op jit(solution)/shard_map/ppermute | solution.py:115
  153.4 12.3 %collective-permute-start.11 = (bf16[64,1792]{1,0:T(8,128)(2,1)S(1)}, bf16[64,1792]{1,0:T(8,128)(2,1)S(1)}, u32[]{:S(2)}, u32[]{:S(2)}) collective-permute-start(bf16[64,1792]{1,0:T(8,128)(2,1)S(1)} %add_convert_fusion.19), channel_id=1, source_target_pairs={{0,8},{4,20},{8,24},{12,4},{16,0},{20,28},{24,16},{28,12},{1,9},{5... | collective-permute-start | bytes 688136 | tf_op jit(solution)/shard_map/ppermute | solution.py:115
  155.8 12.3 %collective-permute-start.3 = (bf16[64,1792]{1,0:T(8,128)(2,1)S(1)}, bf16[64,1792]{1,0:T(8,128)(2,1)S(1)}, u32[]{:S(2)}, u32[]{:S(2)}) collective-permute-start(bf16[64,1792]{1,0:T(8,128)(2,1)S(1)} %add_convert_fusion.23), channel_id=1, source_target_pairs={{0,8},{4,20},{8,24},{12,4},{16,0},{20,28},{24,16},{28,12},{1,9},{5... | collective-permute-start | bytes 688136 | tf_op jit(solution)/shard_map/ppermute | solution.py:115
  158.3 12.3 %collective-permute-start.7 = (bf16[64,1792]{1,0:T(8,128)(2,1)S(1)}, bf16[64,1792]{1,0:T(8,128)(2,1)S(1)}, u32[]{:S(2)}, u32[]{:S(2)}) collective-permute-start(bf16[64,1792]{1,0:T(8,128)(2,1)S(1)} %add_convert_fusion.21), channel_id=1, source_target_pairs={{0,8},{4,20},{8,24},{12,4},{16,0},{20,28},{24,16},{28,12},{1,9},{5... | collective-permute-start | bytes 688136 | tf_op jit(solution)/shard_map/ppermute | solution.py:115
  162.6 14.6 %collective-permute-start.36 = (bf16[64,1792]{1,0:T(8,128)(2,1)S(1)}, bf16[64,1792]{1,0:T(8,128)(2,1)S(1)}, u32[]{:S(2)}, u32[]{:S(2)}) collective-permute-start(bf16[64,1792]{1,0:T(8,128)(2,1)S(1)} %get-tuple-element.45), channel_id=1, source_target_pairs={{0,8},{4,20},{8,24},{12,4},{16,0},{20,28},{24,16},{28,12},{1,9},{5... | collective-permute-start | bytes 688136 | tf_op jit(solution)/shard_map/ppermute | solution.py:126
  164.4 14.2 %collective-permute-start.32 = (bf16[64,1792]{1,0:T(8,128)(2,1)S(1)}, bf16[64,1792]{1,0:T(8,128)(2,1)S(1)}, u32[]{:S(2)}, u32[]{:S(2)}) collective-permute-start(bf16[64,1792]{1,0:T(8,128)(2,1)S(1)} %get-tuple-element.49), channel_id=1, source_target_pairs={{0,8},{4,20},{8,24},{12,4},{16,0},{20,28},{24,16},{28,12},{1,9},{5... | collective-permute-start | bytes 688136 | tf_op jit(solution)/shard_map/ppermute | solution.py:126
  178.5 83.3 %collective-permute-start.76 = (bf16[256,1792]{1,0:T(8,128)(2,1)S(1)}, bf16[256,1792]{1,0:T(8,128)(2,1)S(1)}, u32[]{:S(2)}, u32[]{:S(2)}) collective-permute-start(bf16[256,1792]{1,0:T(8,128)(2,1)S(1)} %constant_dynamic-slice_fusion), channel_id=1, source_target_pairs={{0,4},{4,0},{8,12},{12,8},{16,20},{20,16},{24,28},{28,24},{1,5},{5... | collective-permute-start | bytes 2752520 | tf_op jit(solution)/shard_map/ppermute | solution.py:106
  178.6 84.6 %collective-permute-start.72 = (bf16[256,1792]{1,0:T(8,128)(2,1)S(1)}, bf16[256,1792]{1,0:T(8,128)(2,1)S(1)}, u32[]{:S(2)}, u32[]{:S(2)}) collective-permute-start(bf16[256,1792]{1,0:T(8,128)(2,1)S(1)} %constant_dynamic-slice_fusion.1), channel_id=1, source_target_pairs={{0,4},{4,0},{8,12},{12,8},{16,20},{20,16},{24,28},{28,24},{1,5},{5... | collective-permute-start | bytes 2752520 | tf_op jit(solution)/shard_map/ppermute | solution.py:106
  180.4 83.6 %collective-permute-start.68 = (bf16[256,1792]{1,0:T(8,128)(2,1)S(1)}, bf16[256,1792]{1,0:T(8,128)(2,1)S(1)}, u32[]{:S(2)}, u32[]{:S(2)}) collective-permute-start(bf16[256,1792]{1,0:T(8,128)(2,1)S(1)} %constant_dynamic-slice_fusion.2), channel_id=1, source_target_pairs={{0,4},{4,0},{8,12},{12,8},{16,20},{20,16},{24,28},{28,24},{1,5},{5... | collective-permute-start | bytes 2752520 | tf_op jit(solution)/shard_map/ppermute | solution.py:106
  182.9 81.5 %collective-permute-start.48 = (bf16[256,1792]{1,0:T(8,128)(2,1)S(1)}, bf16[256,1792]{1,0:T(8,128)(2,1)S(1)}, u32[]{:S(2)}, u32[]{:S(2)}) collective-permute-start(bf16[256,1792]{1,0:T(8,128)(2,1)S(1)} %constant_dynamic-slice_fusion.3), channel_id=1, source_target_pairs={{0,4},{4,0},{8,12},{12,8},{16,20},{20,16},{24,28},{28,24},{1,5},{5... | collective-permute-start | bytes 2752520 | tf_op jit(solution)/shard_map/ppermute | solution.py:106
  263.2 111.1 %collective-permute-start.39 = (bf16[256,1792]{1,0:T(8,128)(2,1)}, bf16[256,1792]{1,0:T(8,128)(2,1)}, u32[]{:S(2)}, u32[]{:S(2)}) collective-permute-start(bf16[256,1792]{1,0:T(8,128)(2,1)} %constant_dynamic-update-slice_fusion.53), channel_id=1, source_target_pairs={{0,4},{4,0},{8,12},{12,8},{16,20},{20,16},{24,28},{28,24},{1,5},{5... | collective-permute-start | bytes 2752520 | tf_op jit(solution)/shard_map/ppermute | solution.py:128
  264.0 80.6 %collective-permute-start.35 = (bf16[256,1792]{1,0:T(8,128)(2,1)S(1)}, bf16[256,1792]{1,0:T(8,128)(2,1)S(1)}, u32[]{:S(2)}, u32[]{:S(2)}) collective-permute-start(bf16[256,1792]{1,0:T(8,128)(2,1)S(1)} %constant_dynamic-update-slice_fusion.59), channel_id=1, source_target_pairs={{0,4},{4,0},{8,12},{12,8},{16,20},{20,16},{24,28},{28,24},{1,5},{5... | collective-permute-start | bytes 2752520 | tf_op jit(solution)/shard_map/ppermute | solution.py:128
  264.3 74.3 %collective-permute-start.19 = (bf16[256,1792]{1,0:T(8,128)(2,1)S(1)}, bf16[256,1792]{1,0:T(8,128)(2,1)S(1)}, u32[]{:S(2)}, u32[]{:S(2)}) collective-permute-start(bf16[256,1792]{1,0:T(8,128)(2,1)S(1)} %constant_dynamic-update-slice_fusion.65), channel_id=1, source_target_pairs={{0,4},{4,0},{8,12},{12,8},{16,20},{20,16},{24,28},{28,24},{1,5},{5... | collective-permute-start | bytes 2752520 | tf_op jit(solution)/shard_map/ppermute | solution.py:128
  265.1 87.2 %collective-permute-start.15 = (bf16[256,1792]{1,0:T(8,128)(2,1)S(1)}, bf16[256,1792]{1,0:T(8,128)(2,1)S(1)}, u32[]{:S(2)}, u32[]{:S(2)}) collective-permute-start(bf16[256,1792]{1,0:T(8,128)(2,1)S(1)} %constant_dynamic-update-slice_fusion.71), channel_id=1, source_target_pairs={{0,4},{4,0},{8,12},{12,8},{16,20},{20,16},{24,28},{28,24},{1,5},{5... | collective-permute-start | bytes 2752520 | tf_op jit(solution)/shard_map/ppermute | solution.py:128
  337.9 77.1 %collective-permute-start.59 = (bf16[256,1792]{1,0:T(8,128)(2,1)}, bf16[256,1792]{1,0:T(8,128)(2,1)}, u32[]{:S(2)}, u32[]{:S(2)}) collective-permute-start(bf16[256,1792]{1,0:T(8,128)(2,1)} %constant_dynamic-update-slice_fusion.41), channel_id=1, source_target_pairs={{0,4},{4,0},{8,12},{12,8},{16,20},{20,16},{24,28},{28,24},{1,5},{5... | collective-permute-start | bytes 2752520 | tf_op jit(solution)/shard_map/ppermute | solution.py:128
  338.7 57.4 %collective-permute-start.55 = (bf16[256,1792]{1,0:T(8,128)(2,1)}, bf16[256,1792]{1,0:T(8,128)(2,1)}, u32[]{:S(2)}, u32[]{:S(2)}) collective-permute-start(bf16[256,1792]{1,0:T(8,128)(2,1)} %constant_dynamic-update-slice_fusion.47), channel_id=1, source_target_pairs={{0,4},{4,0},{8,12},{12,8},{16,20},{20,16},{24,28},{28,24},{1,5},{5... | collective-permute-start | bytes 2752520 | tf_op jit(solution)/shard_map/ppermute | solution.py:128
  344.6 37.0 %collective-permute-start.79 = (bf16[64,1792]{1,0:T(8,128)(2,1)}, bf16[64,1792]{1,0:T(8,128)(2,1)}, u32[]{:S(2)}, u32[]{:S(2)}) collective-permute-start(bf16[64,1792]{1,0:T(8,128)(2,1)} %add_convert_fusion.1), channel_id=1, source_target_pairs={{0,8},{4,20},{8,24},{12,4},{16,0},{20,28},{24,16},{28,12},{1,9},{5... | collective-permute-start | bytes 688136 | tf_op jit(solution)/shard_map/ppermute | solution.py:115
  352.4 32.8 %collective-permute-start.75 = (bf16[64,1792]{1,0:T(8,128)(2,1)}, bf16[64,1792]{1,0:T(8,128)(2,1)}, u32[]{:S(2)}, u32[]{:S(2)}) collective-permute-start(bf16[64,1792]{1,0:T(8,128)(2,1)} %add_convert_fusion.3), channel_id=1, source_target_pairs={{0,8},{4,20},{8,24},{12,4},{16,0},{20,28},{24,16},{28,12},{1,9},{5... | collective-permute-start | bytes 688136 | tf_op jit(solution)/shard_map/ppermute | solution.py:115
  374.3 13.5 %collective-permute-start.71 = (bf16[64,1792]{1,0:T(8,128)(2,1)}, bf16[64,1792]{1,0:T(8,128)(2,1)S(1)}, u32[]{:S(2)}, u32[]{:S(2)}) collective-permute-start(bf16[64,1792]{1,0:T(8,128)(2,1)} %add_convert_fusion.5), channel_id=1, source_target_pairs={{0,8},{4,20},{8,24},{12,4},{16,0},{20,28},{24,16},{28,12},{1,9},{5... | collective-permute-start | bytes 688136 | tf_op jit(solution)/shard_map/ppermute | solution.py:115
  381.6 39.7 %collective-permute-start.51 = (bf16[64,1792]{1,0:T(8,128)(2,1)S(1)}, bf16[64,1792]{1,0:T(8,128)(2,1)S(1)}, u32[]{:S(2)}, u32[]{:S(2)}) collective-permute-start(bf16[64,1792]{1,0:T(8,128)(2,1)S(1)} %copy-done.41), channel_id=1, source_target_pairs={{0,8},{4,20},{8,24},{12,4},{16,0},{20,28},{24,16},{28,12},{1,9},{5... | collective-permute-start | bytes 688136 | tf_op jit(solution)/shard_map/ppermute | solution.py:115
  385.2 36.2 %collective-permute-start.47 = (bf16[64,1792]{1,0:T(8,128)(2,1)S(1)}, bf16[64,1792]{1,0:T(8,128)(2,1)S(1)}, u32[]{:S(2)}, u32[]{:S(2)}) collective-permute-start(bf16[64,1792]{1,0:T(8,128)(2,1)S(1)} %copy-done.42), channel_id=1, source_target_pairs={{0,8},{4,20},{8,24},{12,4},{16,0},{20,28},{24,16},{28,12},{1,9},{5... | collective-permute-start | bytes 688136 | tf_op jit(solution)/shard_map/ppermute | solution.py:115
  387.8 33.7 %collective-permute-start.43 = (bf16[64,1792]{1,0:T(8,128)(2,1)S(1)}, bf16[64,1792]{1,0:T(8,128)(2,1)S(1)}, u32[]{:S(2)}, u32[]{:S(2)}) collective-permute-start(bf16[64,1792]{1,0:T(8,128)(2,1)S(1)} %copy-done.43), channel_id=1, source_target_pairs={{0,8},{4,20},{8,24},{12,4},{16,0},{20,28},{24,16},{28,12},{1,9},{5... | collective-permute-start | bytes 688136 | tf_op jit(solution)/shard_map/ppermute | solution.py:115
  429.0 12.3 %collective-permute-start.93 = (bf16[64,1792]{1,0:T(8,128)(2,1)S(1)}, bf16[64,1792]{1,0:T(8,128)(2,1)S(1)}, u32[]{:S(2)}, u32[]{:S(2)}) collective-permute-start(bf16[64,1792]{1,0:T(8,128)(2,1)S(1)} %collective-permute-done.92), channel_id=1, source_target_pairs={{0,8},{4,20},{8,24},{12,4},{16,0},{20,28},{24,16},{28,12},{1,9},{5... | collective-permute-start | bytes 688136 | tf_op jit(solution)/shard_map/ppermute | solution.py:126
  431.4 12.3 %collective-permute-start.89 = (bf16[64,1792]{1,0:T(8,128)(2,1)S(1)}, bf16[64,1792]{1,0:T(8,128)(2,1)S(1)}, u32[]{:S(2)}, u32[]{:S(2)}) collective-permute-start(bf16[64,1792]{1,0:T(8,128)(2,1)S(1)} %collective-permute-done.88), channel_id=1, source_target_pairs={{0,8},{4,20},{8,24},{12,4},{16,0},{20,28},{24,16},{28,12},{1,9},{5... | collective-permute-start | bytes 688136 | tf_op jit(solution)/shard_map/ppermute | solution.py:126
  433.9 12.3 %collective-permute-start.65 = (bf16[64,1792]{1,0:T(8,128)(2,1)S(1)}, bf16[64,1792]{1,0:T(8,128)(2,1)S(1)}, u32[]{:S(2)}, u32[]{:S(2)}) collective-permute-start(bf16[64,1792]{1,0:T(8,128)(2,1)S(1)} %collective-permute-done.64), channel_id=1, source_target_pairs={{0,8},{4,20},{8,24},{12,4},{16,0},{20,28},{24,16},{28,12},{1,9},{5... | collective-permute-start | bytes 688136 | tf_op jit(solution)/shard_map/ppermute | solution.py:126
  436.3 12.3 %collective-permute-start.85 = (bf16[64,1792]{1,0:T(8,128)(2,1)S(1)}, bf16[64,1792]{1,0:T(8,128)(2,1)S(1)}, u32[]{:S(2)}, u32[]{:S(2)}) collective-permute-start(bf16[64,1792]{1,0:T(8,128)(2,1)S(1)} %collective-permute-done.84), channel_id=1, source_target_pairs={{0,8},{4,20},{8,24},{12,4},{16,0},{20,28},{24,16},{28,12},{1,9},{5... | collective-permute-start | bytes 688136 | tf_op jit(solution)/shard_map/ppermute | solution.py:126
  438.8 12.3 %collective-permute-start.61 = (bf16[64,1792]{1,0:T(8,128)(2,1)S(1)}, bf16[64,1792]{1,0:T(8,128)(2,1)S(1)}, u32[]{:S(2)}, u32[]{:S(2)}) collective-permute-start(bf16[64,1792]{1,0:T(8,128)(2,1)S(1)} %collective-permute-done.60), channel_id=1, source_target_pairs={{0,8},{4,20},{8,24},{12,4},{16,0},{20,28},{24,16},{28,12},{1,9},{5... | collective-permute-start | bytes 688136 | tf_op jit(solution)/shard_map/ppermute | solution.py:126
  441.3 12.3 %collective-permute-start.81 = (bf16[64,1792]{1,0:T(8,128)(2,1)S(1)}, bf16[64,1792]{1,0:T(8,128)(2,1)S(1)}, u32[]{:S(2)}, u32[]{:S(2)}) collective-permute-start(bf16[64,1792]{1,0:T(8,128)(2,1)S(1)} %collective-permute-done.80), channel_id=1, source_target_pairs={{0,8},{4,20},{8,24},{12,4},{16,0},{20,28},{24,16},{28,12},{1,9},{5... | collective-permute-start | bytes 688136 | tf_op jit(solution)/shard_map/ppermute | solution.py:126
  443.7 12.3 %collective-permute-start.94 = (bf16[64,1792]{1,0:T(8,128)(2,1)S(1)}, bf16[64,1792]{1,0:T(8,128)(2,1)S(1)}, u32[]{:S(2)}, u32[]{:S(2)}) collective-permute-start(bf16[64,1792]{1,0:T(8,128)(2,1)S(1)} %collective-permute-done.93), channel_id=1, source_target_pairs={{0,8},{4,20},{8,24},{12,4},{16,0},{20,28},{24,16},{28,12},{1,9},{5... | collective-permute-start | bytes 688136 | tf_op jit(solution)/shard_map/ppermute | solution.py:126
  448.6 12.3 %collective-permute-start.66 = (bf16[64,1792]{1,0:T(8,128)(2,1)S(1)}, bf16[64,1792]{1,0:T(8,128)(2,1)S(1)}, u32[]{:S(2)}, u32[]{:S(2)}) collective-permute-start(bf16[64,1792]{1,0:T(8,128)(2,1)S(1)} %collective-permute-done.65), channel_id=1, source_target_pairs={{0,8},{4,20},{8,24},{12,4},{16,0},{20,28},{24,16},{28,12},{1,9},{5... | collective-permute-start | bytes 688136 | tf_op jit(solution)/shard_map/ppermute | solution.py:126
  451.1 12.3 %collective-permute-start.86 = (bf16[64,1792]{1,0:T(8,128)(2,1)S(1)}, bf16[64,1792]{1,0:T(8,128)(2,1)S(1)}, u32[]{:S(2)}, u32[]{:S(2)}) collective-permute-start(bf16[64,1792]{1,0:T(8,128)(2,1)S(1)} %collective-permute-done.85), channel_id=1, source_target_pairs={{0,8},{4,20},{8,24},{12,4},{16,0},{20,28},{24,16},{28,12},{1,9},{5... | collective-permute-start | bytes 688136 | tf_op jit(solution)/shard_map/ppermute | solution.py:126
  453.5 12.3 %collective-permute-start.62 = (bf16[64,1792]{1,0:T(8,128)(2,1)S(1)}, bf16[64,1792]{1,0:T(8,128)(2,1)S(1)}, u32[]{:S(2)}, u32[]{:S(2)}) collective-permute-start(bf16[64,1792]{1,0:T(8,128)(2,1)S(1)} %collective-permute-done.61), channel_id=1, source_target_pairs={{0,8},{4,20},{8,24},{12,4},{16,0},{20,28},{24,16},{28,12},{1,9},{5... | collective-permute-start | bytes 688136 | tf_op jit(solution)/shard_map/ppermute | solution.py:126
  456.0 12.3 %collective-permute-start.82 = (bf16[64,1792]{1,0:T(8,128)(2,1)S(1)}, bf16[64,1792]{1,0:T(8,128)(2,1)S(1)}, u32[]{:S(2)}, u32[]{:S(2)}) collective-permute-start(bf16[64,1792]{1,0:T(8,128)(2,1)S(1)} %collective-permute-done.81), channel_id=1, source_target_pairs={{0,8},{4,20},{8,24},{12,4},{16,0},{20,28},{24,16},{28,12},{1,9},{5... | collective-permute-start | bytes 688136 | tf_op jit(solution)/shard_map/ppermute | solution.py:126
  458.5 38.8 %collective-permute-start.95 = (bf16[256,1792]{1,0:T(8,128)(2,1)S(1)}, bf16[256,1792]{1,0:T(8,128)(2,1)S(1)}, u32[]{:S(2)}, u32[]{:S(2)}) collective-permute-start(bf16[256,1792]{1,0:T(8,128)(2,1)S(1)} %constant_dynamic-update-slice_fusion.2), channel_id=1, source_target_pairs={{0,4},{4,0},{8,12},{12,8},{16,20},{20,16},{24,28},{28,24},{1,5},{5... | collective-permute-start | bytes 2752520 | tf_op jit(solution)/shard_map/ppermute | solution.py:128
  460.9 36.4 %collective-permute-start.91 = (bf16[256,1792]{1,0:T(8,128)(2,1)S(1)}, bf16[256,1792]{1,0:T(8,128)(2,1)}, u32[]{:S(2)}, u32[]{:S(2)}) collective-permute-start(bf16[256,1792]{1,0:T(8,128)(2,1)S(1)} %constant_dynamic-update-slice_fusion.8), channel_id=1, source_target_pairs={{0,4},{4,0},{8,12},{12,8},{16,20},{20,16},{24,28},{28,24},{1,5},{5... | collective-permute-start | bytes 2752520 | tf_op jit(solution)/shard_map/ppermute | solution.py:128
  465.8 14.5 %collective-permute-start.87 = (bf16[256,1792]{1,0:T(8,128)(2,1)S(1)}, bf16[256,1792]{1,0:T(8,128)(2,1)S(1)}, u32[]{:S(2)}, u32[]{:S(2)}) collective-permute-start(bf16[256,1792]{1,0:T(8,128)(2,1)S(1)} %constant_dynamic-update-slice_fusion.17), channel_id=1, source_target_pairs={{0,4},{4,0},{8,12},{12,8},{16,20},{20,16},{24,28},{28,24},{1,5},{5... | collective-permute-start | bytes 2752520 | tf_op jit(solution)/shard_map/ppermute | solution.py:128
  (106 other events, 790.4 us)
Sparse Core Ops, SparseCore 0:
  10.1 48.6 all-gather.1
  487.2 24.7 reduce-scatter.1

commit v2 on v1

--- a/solution.py
+++ b/solution.py
@@ -5,6 +5,7 @@
 
 N_CHUNKS = 4
 GROUP = 2
+FWD_GATE = -1
 F32 = jnp.float32
 BF16 = jnp.bfloat16
 
@@ -56,13 +57,11 @@
     chips, position, ring_pairs = ring_plan(n_row)
     core_pairs = [(r, r ^ 1) for r in range(n_row)]
 
-    def rows(arrays, start, size):
-        return tuple(lax.dynamic_slice_in_dim(a, start, size, 0) for a in arrays)
+    def rows(array, start, size):
+        return lax.dynamic_slice_in_dim(array, start, size, 1)
 
-    def put(arrays, pieces, start):
-        return tuple(
-            lax.dynamic_update_slice_in_dim(a, p, start, 0) for a, p in zip(arrays, pieces)
-        )
+    def put(array, piece, start):
+        return lax.dynamic_update_slice_in_dim(array, piece, start, 1)
 
     def per_device(tokens, cotangent, gate_weight, up_weight, down_weight):
         r = lax.axis_index("row")
@@ -85,17 +84,17 @@
         up_out = jnp.zeros((width, columns), BF16)
         down_out = jnp.zeros((columns, width), BF16)
         x_chunk, dy_chunk = x_panel, dy_panel
-        reduced = {}
-        grads = {}
-        exchanged = {}
+        reduced, grads, exchanged = {}, {}, {}
         for j in range(N_CHUNKS):
             cols = slice(j * w, (j + 1) * w)
             gw = gate_weight[:, cols]
             uw = up_weight[:, cols]
-            parts = (
-                jnp.dot(x_chunk, gw, preferred_element_type=F32).astype(BF16),
-                jnp.dot(x_chunk, uw, preferred_element_type=F32).astype(BF16),
-                contract_cols(dy_chunk, down_weight[cols, :]).astype(BF16),
+            parts = jnp.stack(
+                [
+                    jnp.dot(x_chunk, gw, preferred_element_type=F32).astype(BF16),
+                    jnp.dot(x_chunk, uw, preferred_element_type=F32).astype(BF16),
+                    contract_cols(dy_chunk, down_weight[cols, :]).astype(BF16),
+                ]
             )
             own = rows(parts, core * half, half)
             other = rows(parts, (1 - core) * half, half)
@@ -104,32 +103,31 @@
             if before:
                 other, _ = lax.optimization_barrier((other, [reduced[i] for i in before]))
             got = lax.ppermute(other, "row", core_pairs)
-            exchanged[j] = got
-            if j % GROUP == GROUP - 1:
+            summed = own.astype(F32) + got.astype(F32)
+            acc = rows(summed, ((pos - 1) % chips) * block, block)
+            steps = [got]
+            for s in range(chips - 1):
+                got = lax.ppermute(acc.astype(BF16), "row", ring_pairs)
+                acc = got.astype(F32) + rows(summed, ((pos - s - 2) % chips) * block, block)
+                steps.append(got)
+            exchanged[j] = steps[min(FWD_GATE, len(steps) - 1)]
+            if FWD_GATE >= 0 and j % GROUP == GROUP - 1 and j + 1 < N_CHUNKS:
                 x_chunk, dy_chunk, _ = lax.optimization_barrier(
                     (x_panel, dy_panel, [exchanged[i] for i in range(j - GROUP + 1, j + 1)])
                 )
-            summed = tuple(a.astype(F32) + b.astype(F32) for a, b in zip(own, got))
-            acc = rows(summed, ((pos - 1) % chips) * block, block)
-            for s in range(chips - 1):
-                got = lax.ppermute(tuple(a.astype(BF16) for a in acc), "row", ring_pairs)
-                mine = rows(summed, ((pos - s - 2) % chips) * block, block)
-                acc = tuple(a.astype(F32) + b for a, b in zip(got, mine))
             reduced[j] = acc
             if before:
                 acc, _ = lax.optimization_barrier((acc, [grads[i] for i in before]))
-            act = activations(*acc)
-            held = tuple(jnp.zeros((half, w), BF16) for _ in act)
-            held = put(held, act, pos * block)
+            act = jnp.stack(activations(acc[0], acc[1], acc[2]))
+            held = put(jnp.zeros((3, half, w), BF16), act, pos * block)
             cur = act
             for s in range(chips - 1):
                 cur = lax.ppermute(cur, "row", ring_pairs)
                 held = put(held, cur, ((pos - s - 1) % chips) * block)
             partner = lax.ppermute(held, "row", core_pairs)
-            full = tuple(jnp.zeros((n_tok, w), BF16) for _ in act)
-            full = put(full, held, core * half)
+            full = put(jnp.zeros((3, n_tok, w), BF16), held, core * half)
             full = put(full, partner, (1 - core) * half)
-            hidden, grad_gate_act, grad_up_act = full
+            hidden, grad_gate_act, grad_up_act = full[0], full[1], full[2]
             down_piece = contract_rows(hidden, dy_panel).astype(BF16)
             gate_piece = contract_rows(x_panel, grad_gate_act).astype(BF16)
             up_piece = contract_rows(x_panel, grad_up_act).astype(BF16)

time: 533 us -> 446 us (0.84)
  starting transfers between devices: 94.4 us -> 36.3 us
  local copies, waits for them, and re-layouts: 59.3 us -> 38.4 us
  matrix products: 132 us -> 147 us
  waiting for transfers between devices: 193 us -> 178 us
    ppermute x36 -> x12, starting transfers between devices: 48.1 us -> 18.3 us  [per_device(): got = lax.ppermute(acc.astype(BF16), 'row', ring_pairs)]
    ppermute x36 -> x12, starting transfers between devices: 41.9 us -> 17 us  [per_device(): cur = lax.ppermute(cur, 'row', ring_pairs)]
    ppermute x36 -> x12, waiting for transfers between devices: 61.3 us -> 48.3 us  [per_device(): got = lax.ppermute(acc.astype(BF16), 'row', ring_pairs)]
    dynamic_update_slice x60 -> x20, local copies, waits for them, and re-layouts: 19.7 us -> 6.67 us  [put(): return lax.dynamic_update_slice_in_dim(array, piece, start, 1)]
    dot_general x12, matrix products: 54 us -> 64.1 us  [contract_cols(): lax.dot_general(left, right, (((1,), (1,)), ((), ())), preferred_element_...]
    another operation x0 -> x8, other arithmetic: none -> 8.42 us  [the longest x4 8.04 us: per_device(): jnp.stack([jnp.dot(x_chunk, gw, preferred_element_type=F32).astype(BF16),...]
    unnamed x112 -> x34, local copies, waits for them, and re-layouts: 10.3 us -> 2.11 us
    add x18 -> x8, other arithmetic: 13.7 us -> 6.66 us  [the longest x4 6.16 us: per_device(): summed = own.astype(F32) + got.astype(F32)]
  transfers between devices with their start and end apart: 98 -> 34, of which waited for: 57 -> 23; matrix products, arithmetic and copies ran while one was open for 34% -> 40% of each run, Pallas kernels for 0% -> 0%
where the time goes in v2:
time: 446 us; the launch traced here: 441 us
  waiting for transfers between devices  178 us (40%)
  matrix products  147 us (33%)
  local copies, waits for them, and re-layouts  38.4 us (9%)
  starting transfers between devices  36.3 us (8%)
  other arithmetic  22.8 us (5%)
  between operations  18.4 us (4%)
    ppermute x12, waiting for transfers between devices, per_device(): cur = lax.ppermute(cur, 'row', ring_pairs)  84.3 us
    dot_general x12, matrix products, contract_cols(): lax.dot_general(left, right, (((1,), (1,)), ((), ())), preferred_element_...  64.1 us
    ppermute x12, waiting for transfers between devices, per_device(): got = lax.ppermute(acc.astype(BF16), 'row', ring_pairs)  48.3 us
    dot_general x12, matrix products, contract_rows(): lax.dot_general(left, right, (((0,), (0,)), ((), ())), preferred_element_...  47.5 us
    all_gather x1, waiting for transfers between devices, per_device(): lax.all_gather(jnp.concatenate([tokens, cotangent], axis=1), 'col', axis=...  45.1 us
    ppermute x12, starting transfers between devices, per_device(): got = lax.ppermute(acc.astype(BF16), 'row', ring_pairs)  18.3 us
    dot_general x4, matrix products, per_device(): jnp.dot(x_chunk, uw, preferred_element_type=F32).astype(BF16)  18.2 us
    dot_general x4, matrix products, per_device(): jnp.dot(x_chunk, gw, preferred_element_type=F32).astype(BF16)  17.6 us
  transfers between devices with their start and end apart: 34, of which 23 were waited for; matrix products, arithmetic and copies ran while one was open for 40% of the time, Pallas kernels for 0%

profile of v2, /device:TPU:0, one launch (start us, length us, event | category | flops | bytes accessed | tf_op | source)
XLA Modules:
  0.0 441.1 jit_solution(1002091704831609441)
XLA Ops:
  13.7 45.1 %all-gather.2.cloned.1.call-done = bf16[512,2048]{1,0:T(8,128)(2,1)} async-done(((bf16[128,2048]{1,0:T(8,128)(2,1)}), bf16[512,2048]{1,0:T(8,128)(2,1)}) %all-gather.2.cloned.1.call-update) | async-done | bytes 2097168 | tf_op jit(solution)/shard_map/all_gather | solution.py:71
  58.8 4.6 %fusion.106 = bf16[1,512,1792]{2,1,0:T(8,128)(2,1)S(1)} fusion(bf16[1024,7168]{1,0:T(8,128)(2,1)} %param.9, bf16[512,2048]{1,0:T(8,128)(2,1)} %all-gather.2.cloned.1.call-done), kind=kOutput, calls=%fused_computation.86 | convolution fusion | flops 1879965696 | bytes 6553600 | tf_op jit(solution)/shard_map/dot_general | solution.py:95
  63.4 4.1 fusion.109
  67.5 4.2 fusion.88
  72.9 4.1 fusion.112
  77.0 4.1 fusion.115
  81.1 4.2 fusion.91
  88.2 4.2 fusion.100
  92.5 4.1 fusion.103
  96.6 5.4 %fusion.85 = bf16[1,512,1792]{2,1,0:T(8,128)(2,1)} fusion(bf16[7168,1024]{1,0:T(8,128)(2,1)} %param.10, bf16[512,2048]{1,0:T(8,128)(2,1)S(1)} %copy-done.7), kind=kOutput, calls=%fused_computation.79 | convolution fusion | flops 1879965696 | bytes 6553600 | tf_op jit(solution)/shard_map/dot_general | solution.py:29
  105.0 4.6 %fusion.82 = bf16[1,512,1792]{2,1,0:T(8,128)(2,1)S(1)} fusion(bf16[7168,1024]{1,0:T(8,128)(2,1)} %param.10, bf16[512,2048]{1,0:T(8,128)(2,1)} %all-gather.2.cloned.1.call-done), kind=kOutput, calls=%fused_computation.78 | convolution fusion | flops 1879965696 | bytes 6553600 | tf_op jit(solution)/shard_map/dot_general | solution.py:29
  109.6 5.3 %fusion.94 = bf16[1,512,1792]{2,1,0:T(8,128)(2,1)} fusion(bf16[1024,7168]{1,0:T(8,128)(2,1)} %param.9, bf16[512,2048]{1,0:T(8,128)(2,1)S(1)} %copy-done.8), kind=kOutput, calls=%fused_computation.82 | convolution fusion | flops 1879965696 | bytes 6553600 | tf_op jit(solution)/shard_map/dot_general | solution.py:95
  115.0 5.3 %fusion.97 = bf16[1,512,1792]{2,1,0:T(8,128)(2,1)} fusion(bf16[1024,7168]{1,0:T(8,128)(2,1)} %param.8, bf16[512,2048]{1,0:T(8,128)(2,1)S(1)} %copy-done.8), kind=kOutput, calls=%fused_computation.83 | convolution fusion | flops 1879965696 | bytes 6553600 | tf_op jit(solution)/shard_map/dot_general | solution.py:94
  129.4 4.5 %collective-permute-done.9 = bf16[3,64,1792]{2,1,0:T(8,128)(2,1)S(1)} collective-permute-done((bf16[3,64,1792]{2,1,0:T(8,128)(2,1)S(1)}, bf16[3,64,1792]{2,1,0:T(8,128)(2,1)S(1)}, u32[]{:S(2)}, u32[]{:S(2)}) %collective-permute-start.9) | collective-permute-done | bytes 688160 | tf_op jit(solution)/shard_map/ppermute | solution.py:110
  144.1 4.6 %collective-permute-done.10 = bf16[3,64,1792]{2,1,0:T(8,128)(2,1)} collective-permute-done((bf16[3,64,1792]{2,1,0:T(8,128)(2,1)}, bf16[3,64,1792]{2,1,0:T(8,128)(2,1)}, u32[]{:S(2)}, u32[]{:S(2)}) %collective-permute-start.10) | collective-permute-done | bytes 688160 | tf_op jit(solution)/shard_map/ppermute | solution.py:110
  157.6 5.7 %collective-permute-done.11 = bf16[3,64,1792]{2,1,0:T(8,128)(2,1)S(1)} collective-permute-done((bf16[3,64,1792]{2,1,0:T(8,128)(2,1)S(1)}, bf16[3,64,1792]{2,1,0:T(8,128)(2,1)S(1)}, u32[]{:S(2)}, u32[]{:S(2)}) %collective-permute-start.11) | collective-permute-done | bytes 688160 | tf_op jit(solution)/shard_map/ppermute | solution.py:110
  163.7 7.0 %collective-permute-done.3 = bf16[3,64,1792]{2,1,0:T(8,128)(2,1)S(1)} collective-permute-done((bf16[3,64,1792]{2,1,0:T(8,128)(2,1)S(1)}, bf16[3,64,1792]{2,1,0:T(8,128)(2,1)S(1)}, u32[]{:S(2)}, u32[]{:S(2)}) %collective-permute-start.3) | collective-permute-done | bytes 688160 | tf_op jit(solution)/shard_map/ppermute | solution.py:110
  174.8 7.7 %collective-permute-done.12 = bf16[3,64,1792]{2,1,0:T(8,128)(2,1)S(1)} collective-permute-done((bf16[3,64,1792]{2,1,0:T(8,128)(2,1)S(1)}, bf16[3,64,1792]{2,1,0:T(8,128)(2,1)S(1)}, u32[]{:S(2)}, u32[]{:S(2)}) %collective-permute-start.12) | collective-permute-done | bytes 688160 | tf_op jit(solution)/shard_map/ppermute | solution.py:125
  183.9 5.9 %collective-permute-done.4 = bf16[3,64,1792]{2,1,0:T(8,128)(2,1)S(1)} collective-permute-done((bf16[3,64,1792]{2,1,0:T(8,128)(2,1)S(1)}, bf16[3,64,1792]{2,1,0:T(8,128)(2,1)S(1)}, u32[]{:S(2)}, u32[]{:S(2)}) %collective-permute-start.4) | collective-permute-done | bytes 688160 | tf_op jit(solution)/shard_map/ppermute | solution.py:125
  191.4 5.8 %collective-permute-done.13 = bf16[3,64,1792]{2,1,0:T(8,128)(2,1)S(1)} collective-permute-done((bf16[3,64,1792]{2,1,0:T(8,128)(2,1)S(1)}, bf16[3,64,1792]{2,1,0:T(8,128)(2,1)S(1)}, u32[]{:S(2)}, u32[]{:S(2)}) %collective-permute-start.13) | collective-permute-done | bytes 688160 | tf_op jit(solution)/shard_map/ppermute | solution.py:125
  198.7 5.8 %collective-permute-done.5 = bf16[3,64,1792]{2,1,0:T(8,128)(2,1)S(1)} collective-permute-done((bf16[3,64,1792]{2,1,0:T(8,128)(2,1)S(1)}, bf16[3,64,1792]{2,1,0:T(8,128)(2,1)S(1)}, u32[]{:S(2)}, u32[]{:S(2)}) %collective-permute-start.5) | collective-permute-done | bytes 688160 | tf_op jit(solution)/shard_map/ppermute | solution.py:125
  206.2 5.8 %collective-permute-done.14 = bf16[3,64,1792]{2,1,0:T(8,128)(2,1)S(1)} collective-permute-done((bf16[3,64,1792]{2,1,0:T(8,128)(2,1)S(1)}, bf16[3,64,1792]{2,1,0:T(8,128)(2,1)S(1)}, u32[]{:S(2)}, u32[]{:S(2)}) %collective-permute-start.14) | collective-permute-done | bytes 688160 | tf_op jit(solution)/shard_map/ppermute | solution.py:125
  212.1 7.2 %collective-permute-done.6 = bf16[3,64,1792]{2,1,0:T(8,128)(2,1)S(1)} collective-permute-done((bf16[3,64,1792]{2,1,0:T(8,128)(2,1)S(1)}, bf16[3,64,1792]{2,1,0:T(8,128)(2,1)S(1)}, u32[]{:S(2)}, u32[]{:S(2)}) %collective-permute-start.6) | collective-permute-done | bytes 688160 | tf_op jit(solution)/shard_map/ppermute | solution.py:125
  224.8 6.6 %collective-permute-done.17 = bf16[3,64,1792]{2,1,0:T(8,128)(2,1)S(1)} collective-permute-done((bf16[3,64,1792]{2,1,0:T(8,128)(2,1)S(1)}, bf16[3,64,1792]{2,1,0:T(8,128)(2,1)S(1)}, u32[]{:S(2)}, u32[]{:S(2)}) %collective-permute-start.17) | collective-permute-done | bytes 688160 | tf_op jit(solution)/shard_map/ppermute | solution.py:110
  233.0 5.7 %collective-permute-done.25 = bf16[3,64,1792]{2,1,0:T(8,128)(2,1)S(1)} collective-permute-done((bf16[3,64,1792]{2,1,0:T(8,128)(2,1)S(1)}, bf16[3,64,1792]{2,1,0:T(8,128)(2,1)S(1)}, u32[]{:S(2)}, u32[]{:S(2)}) %collective-permute-start.25) | collective-permute-done | bytes 688160 | tf_op jit(solution)/shard_map/ppermute | solution.py:110
  241.0 5.0 %collective-permute-done.18 = bf16[3,64,1792]{2,1,0:T(8,128)(2,1)S(1)} collective-permute-done((bf16[3,64,1792]{2,1,0:T(8,128)(2,1)S(1)}, bf16[3,64,1792]{2,1,0:T(8,128)(2,1)S(1)}, u32[]{:S(2)}, u32[]{:S(2)}) %collective-permute-start.18) | collective-permute-done | bytes 688160 | tf_op jit(solution)/shard_map/ppermute | solution.py:110
  248.5 4.9 %collective-permute-done.26 = bf16[3,64,1792]{2,1,0:T(8,128)(2,1)S(1)} collective-permute-done((bf16[3,64,1792]{2,1,0:T(8,128)(2,1)S(1)}, bf16[3,64,1792]{2,1,0:T(8,128)(2,1)S(1)}, u32[]{:S(2)}, u32[]{:S(2)}) %collective-permute-start.26) | collective-permute-done | bytes 688160 | tf_op jit(solution)/shard_map/ppermute | solution.py:110
  257.2 5.5 %fusion.34 = f32[512,1024]{1,0:T(8,128)} fusion(bf16[1024,7168]{1,0:T(8,128)(2,1)} %param.8, bf16[3,512,1792]{2,1,0:T(8,128)(2,1)S(1)} %constant_dynamic-update-slice_fusion.15), kind=kOutput, calls=%fused_computation.54 | convolution fusion | flops 1879048192 | bytes 7602176 | tf_op jit(solution)/shard_map/dot_general | solution.py:29
  264.8 6.1 %fusion.38 = f32[512,1024]{1,0:T(8,128)S(1)} fusion(bf16[1024,7168]{1,0:T(8,128)(2,1)} %param.9, bf16[3,512,1792]{2,1,0:T(8,128)(2,1)S(1)} %constant_dynamic-update-slice_fusion.21), kind=kOutput, calls=%fused_computation.58 | convolution fusion | flops 1879048192 | bytes 7602176 | tf_op jit(solution)/shard_map/dot_general | solution.py:29
  270.9 5.6 %fusion.118 = f32[512,1024]{1,0:T(8,128)} fusion(f32[512,1024]{1,0:T(8,128)S(1)} %fusion.38, bf16[1024,7168]{1,0:T(8,128)(2,1)} %param.8, bf16[3,512,1792]{2,1,0:T(8,128)(2,1)S(1)} %constant_dynamic-update-slice_fusion.21), kind=kOutput, calls=%fused_computation.104 | convolution fusion | flops 1879572480 | bytes 9699328 | tf_op jit(solution)/shard_map/dot_general | solution.py:29
  285.8 7.1 %dynamic_update_slice.132 = bf16[1024,7168]{1,0:T(8,128)(2,1)} pad(bf16[1024,1792]{1,0:T(8,128)(2,1)S(1)} %convolution_convert_fusion.10, bf16[]{:T(256)} %constant.117.clone.1), padding=0_0x0_5376 | pad | bytes 18350082 | tf_op jit(solution)/shard_map/dynamic_update_slice | solution.py:140
  296.7 10.9 %dynamic_update_slice.140 = bf16[7168,1024]{1,0:T(8,128)(2,1)} pad(bf16[1792,1024]{1,0:T(8,128)(2,1)S(1)} %convolution_convert_fusion.11, bf16[]{:T(256)} %constant.117.clone.1), padding=0_5376x0_0 | pad | bytes 18350082 | tf_op jit(solution)/shard_map/dynamic_update_slice | solution.py:142
  307.6 6.7 %add_add_fusion = f32[512,1024]{1,0:T(8,128)} fusion(f32[512,1024]{1,0:T(8,128)} %fusion.118, f32[512,1024]{1,0:T(8,128)} %fusion.34, bf16[1024,7168]{1,0:T(8,128)(2,1)} %param.9, bf16[3,512,1792]{2,1,0:T(8,128)(2,1)S(1)} %constant_dynamic-update-slice_fusion.15), kind=kOutput, calls=%fused_computation.91 | convolution fusion | flops 1880096768 | bytes 11796480 | tf_op jit(solution)/shard_map/dot_general | solution.py:29
  318.0 4.5 %constant_dynamic-update-slice_fusion.2 = bf16[1024,7168]{1,0:T(8,128)(2,1)} fusion(bf16[1024,7168]{1,0:T(8,128)(2,1)} %dynamic_update_slice.132, bf16[3,512,1792]{2,1,0:T(8,128)(2,1)S(1)} %constant_dynamic-update-slice_fusion.15, bf16[512,2048]{1,0:T(8,128)(2,1)S(1)} %copy-done.10), kind=kOutput, calls=%fused_computation.156 | convolution fusion | flops 1880883200 | bytes 6553600 | tf_op jit(solution)/shard_map/dot_general | solution.py:23
  331.0 9.1 %collective-permute-done.20 = bf16[3,64,1792]{2,1,0:T(8,128)(2,1)S(1)} collective-permute-done((bf16[3,64,1792]{2,1,0:T(8,128)(2,1)S(1)}, bf16[3,64,1792]{2,1,0:T(8,128)(2,1)S(1)}, u32[]{:S(2)}, u32[]{:S(2)}) %collective-permute-start.20) | collective-permute-done | bytes 688160 | tf_op jit(solution)/shard_map/ppermute | solution.py:125
  342.4 8.6 %collective-permute-done.21 = bf16[3,64,1792]{2,1,0:T(8,128)(2,1)S(1)} collective-permute-done((bf16[3,64,1792]{2,1,0:T(8,128)(2,1)S(1)}, bf16[3,64,1792]{2,1,0:T(8,128)(2,1)S(1)}, u32[]{:S(2)}, u32[]{:S(2)}) %collective-permute-start.21) | collective-permute-done | bytes 688160 | tf_op jit(solution)/shard_map/ppermute | solution.py:125
  352.5 5.9 %collective-permute-done.28 = bf16[3,64,1792]{2,1,0:T(8,128)(2,1)S(1)} collective-permute-done((bf16[3,64,1792]{2,1,0:T(8,128)(2,1)S(1)}, bf16[3,64,1792]{2,1,0:T(8,128)(2,1)S(1)}, u32[]{:S(2)}, u32[]{:S(2)}) %collective-permute-start.28) | collective-permute-done | bytes 688160 | tf_op jit(solution)/shard_map/ppermute | solution.py:125
  359.9 5.8 %collective-permute-done.22 = bf16[3,64,1792]{2,1,0:T(8,128)(2,1)S(1)} collective-permute-done((bf16[3,64,1792]{2,1,0:T(8,128)(2,1)S(1)}, bf16[3,64,1792]{2,1,0:T(8,128)(2,1)S(1)}, u32[]{:S(2)}, u32[]{:S(2)}) %collective-permute-start.22) | collective-permute-done | bytes 688160 | tf_op jit(solution)/shard_map/ppermute | solution.py:125
  365.9 7.2 %collective-permute-done.29 = bf16[3,64,1792]{2,1,0:T(8,128)(2,1)S(1)} collective-permute-done((bf16[3,64,1792]{2,1,0:T(8,128)(2,1)S(1)}, bf16[3,64,1792]{2,1,0:T(8,128)(2,1)S(1)}, u32[]{:S(2)}, u32[]{:S(2)}) %collective-permute-start.29) | collective-permute-done | bytes 688160 | tf_op jit(solution)/shard_map/ppermute | solution.py:125
  374.8 9.4 %collective-permute-done.30 = bf16[3,64,1792]{2,1,0:T(8,128)(2,1)S(1)} collective-permute-done((bf16[3,64,1792]{2,1,0:T(8,128)(2,1)S(1)}, bf16[3,64,1792]{2,1,0:T(8,128)(2,1)S(1)}, u32[]{:S(2)}, u32[]{:S(2)}) %collective-permute-start.30) | collective-permute-done | bytes 688160 | tf_op jit(solution)/shard_map/ppermute | solution.py:125
  386.1 6.1 %fusion.22 = f32[512,1024]{1,0:T(8,128)S(1)} fusion(bf16[1024,7168]{1,0:T(8,128)(2,1)} %param.9, bf16[3,512,1792]{2,1,0:T(8,128)(2,1)S(1)} %constant_dynamic-update-slice_fusion.9), kind=kOutput, calls=%fused_computation.42 | convolution fusion | flops 1879048192 | bytes 7602176 | tf_op jit(solution)/shard_map/dot_general | solution.py:29
  392.2 4.1 fusion.26
  396.7 6.1 %fusion.18 = f32[512,1024]{1,0:T(8,128)S(1)} fusion(bf16[1024,7168]{1,0:T(8,128)(2,1)} %param.8, bf16[3,512,1792]{2,1,0:T(8,128)(2,1)S(1)} %constant_dynamic-update-slice_fusion.3), kind=kOutput, calls=%fused_computation.38 | convolution fusion | flops 1879048192 | bytes 7602176 | tf_op jit(solution)/shard_map/dot_general | solution.py:29
  402.9 5.5 %add_convert_fusion = bf16[512,1024]{1,0:T(8,128)(2,1)} fusion(f32[512,1024]{1,0:T(8,128)S(1)} %fusion.18, f32[512,1024]{1,0:T(8,128)S(1)} %fusion.22, f32[512,1024]{1,0:T(8,128)S(1)} %copy-done.12, f32[512,1024]{1,0:T(8,128)S(1)} %fusion.26, bf16[1024,7168]{1,0:T(8,128)(2,1)} %param.9, bf16[3,512,1792]{2,1,0:T(8,128)(2,1)S(1)} %constant_dynamic-update-slice_fusion.3), kind=kOutput, calls=%fused_computation.90 | convolution fusion | flops 1881669632 | bytes 14942208 | tf_op jit(solution)/shard_map/dot_general | solution.py:29
  408.4 5.6 %fusion.3 = bf16[1024,7168]{1,0:T(8,128)(2,1)} fusion(bf16[1024,7168]{1,0:T(8,128)(2,1)} %copy-done.2, bf16[3,512,1792]{2,1,0:T(8,128)(2,1)} %copy-done.5, bf16[512,2048]{1,0:T(8,128)(2,1)S(1)} %copy-done.11), kind=kOutput, calls=%fused_computation.15 | convolution fusion | flops 1880883200 | bytes 6553600 | tf_op jit(solution)/shard_map/dot_general | solution.py:23
  414.0 4.0 fusion.2
  418.0 4.2 fusion.5
  422.2 4.0 fusion.4
  (158 shorter events, 109.2 us)
Async XLA Ops:
  7.2 51.6 %all-gather.2.cloned.1.call-start = ((), (), s32[]{:S(2)}) async-start(), calls=%async_computation.1 | async-start | bytes 2621440 | tf_op jit(solution)/shard_map/all_gather | solution.py:71
  9.1 424.9 %reduce-scatter.2.cloned.1.call-start = ((), (), s32[]{:S(2)}) async-start(), calls=%async_computation.2 | async-start | bytes 1310720 | tf_op jit(solution)/shard_map/reduce_scatter | solution.py:143
  72.8 47.5 %collective-permute-start.8 = (bf16[3,256,1792]{2,1,0:T(8,128)(2,1)S(1)}, bf16[3,256,1792]{2,1,0:T(8,128)(2,1)}, u32[]{:S(2)}, u32[]{:S(2)}) collective-permute-start(bf16[3,256,1792]{2,1,0:T(8,128)(2,1)S(1)} %constant_dynamic-slice_fusion.2), channel_id=1, source_target_pairs={{0,4},{4,0},{8,12},{12,8},{16,20},{20,16},{24,28},{28,24},{1,5},{5... | collective-permute-start | bytes 8257544 | tf_op jit(solution)/shard_map/ppermute | solution.py:105
  87.7 4.7 %copy-start.7 = (bf16[512,2048]{1,0:T(8,128)(2,1)S(1)}, bf16[512,2048]{1,0:T(8,128)(2,1)}, u32[]{:S(2)}) copy-start(bf16[512,2048]{1,0:T(8,128)(2,1)} %all-gather.2.cloned.1.call-done) | copy-start | bytes 6291460
  87.7 36.7 %collective-permute-start = (bf16[3,256,1792]{2,1,0:T(8,128)(2,1)}, bf16[3,256,1792]{2,1,0:T(8,128)(2,1)}, u32[]{:S(2)}, u32[]{:S(2)}) collective-permute-start(bf16[3,256,1792]{2,1,0:T(8,128)(2,1)} %constant_dynamic-slice_fusion.3), channel_id=1, source_target_pairs={{0,4},{4,0},{8,12},{12,8},{16,20},{20,16},{24,28},{28,24},{1,5},{5... | collective-permute-start | bytes 8257544 | tf_op jit(solution)/shard_map/ppermute | solution.py:105
  105.0 4.6 %copy-start.8 = (bf16[512,2048]{1,0:T(8,128)(2,1)S(1)}, bf16[512,2048]{1,0:T(8,128)(2,1)}, u32[]{:S(2)}) copy-start(bf16[512,2048]{1,0:T(8,128)(2,1)} %all-gather.2.cloned.1.call-done) | copy-start | bytes 6291460
  122.9 11.0 %collective-permute-start.9 = (bf16[3,64,1792]{2,1,0:T(8,128)(2,1)S(1)}, bf16[3,64,1792]{2,1,0:T(8,128)(2,1)S(1)}, u32[]{:S(2)}, u32[]{:S(2)}) collective-permute-start(bf16[3,64,1792]{2,1,0:T(8,128)(2,1)S(1)} %dynamic-slice_convert_fusion.2), channel_id=1, source_target_pairs={{0,8},{4,20},{8,24},{12,4},{16,0},{20,28},{24,16},{28,12},{1,9},{5... | collective-permute-start | bytes 2064392 | tf_op jit(solution)/shard_map/ppermute | solution.py:110
  126.9 7.9 %copy-start = (f32[3,256,1792]{2,1,0:T(8,128)}, f32[3,256,1792]{2,1,0:T(8,128)S(1)}, u32[]{:S(2)}) copy-start(f32[3,256,1792]{2,1,0:T(8,128)S(1)} %convert_add_fusion.3) | copy-start | bytes 16515076
  127.9 13.4 %collective-permute-start.1 = (bf16[3,64,1792]{2,1,0:T(8,128)(2,1)}, bf16[3,64,1792]{2,1,0:T(8,128)(2,1)}, u32[]{:S(2)}, u32[]{:S(2)}) collective-permute-start(bf16[3,64,1792]{2,1,0:T(8,128)(2,1)} %dynamic-slice_convert_fusion.3), channel_id=1, source_target_pairs={{0,8},{4,20},{8,24},{12,4},{16,0},{20,28},{24,16},{28,12},{1,9},{5... | collective-permute-start | bytes 2064392 | tf_op jit(solution)/shard_map/ppermute | solution.py:110
  134.8 13.9 %collective-permute-start.10 = (bf16[3,64,1792]{2,1,0:T(8,128)(2,1)}, bf16[3,64,1792]{2,1,0:T(8,128)(2,1)}, u32[]{:S(2)}, u32[]{:S(2)}) collective-permute-start(bf16[3,64,1792]{2,1,0:T(8,128)(2,1)} %add_convert_fusion.6), channel_id=1, source_target_pairs={{0,8},{4,20},{8,24},{12,4},{16,0},{20,28},{24,16},{28,12},{1,9},{5... | collective-permute-start | bytes 2064392 | tf_op jit(solution)/shard_map/ppermute | solution.py:110
  136.3 5.0 %copy-start.1 = (f32[3,256,1792]{2,1,0:T(8,128)S(1)}, f32[3,256,1792]{2,1,0:T(8,128)}, u32[]{:S(2)}) copy-start(f32[3,256,1792]{2,1,0:T(8,128)} %copy-done) | copy-start | bytes 16515076
  142.6 13.4 %collective-permute-start.2 = (bf16[3,64,1792]{2,1,0:T(8,128)(2,1)S(1)}, bf16[3,64,1792]{2,1,0:T(8,128)(2,1)S(1)}, u32[]{:S(2)}, u32[]{:S(2)}) collective-permute-start(bf16[3,64,1792]{2,1,0:T(8,128)(2,1)S(1)} %add_convert_fusion.8), channel_id=1, source_target_pairs={{0,8},{4,20},{8,24},{12,4},{16,0},{20,28},{24,16},{28,12},{1,9},{5... | collective-permute-start | bytes 2064392 | tf_op jit(solution)/shard_map/ppermute | solution.py:110
  150.0 13.4 %collective-permute-start.11 = (bf16[3,64,1792]{2,1,0:T(8,128)(2,1)S(1)}, bf16[3,64,1792]{2,1,0:T(8,128)(2,1)S(1)}, u32[]{:S(2)}, u32[]{:S(2)}) collective-permute-start(bf16[3,64,1792]{2,1,0:T(8,128)(2,1)S(1)} %add_convert_fusion.5), channel_id=1, source_target_pairs={{0,8},{4,20},{8,24},{12,4},{16,0},{20,28},{24,16},{28,12},{1,9},{5... | collective-permute-start | bytes 2064392 | tf_op jit(solution)/shard_map/ppermute | solution.py:110
  156.1 14.6 %collective-permute-start.3 = (bf16[3,64,1792]{2,1,0:T(8,128)(2,1)S(1)}, bf16[3,64,1792]{2,1,0:T(8,128)(2,1)S(1)}, u32[]{:S(2)}, u32[]{:S(2)}) collective-permute-start(bf16[3,64,1792]{2,1,0:T(8,128)(2,1)S(1)} %add_convert_fusion.7), channel_id=1, source_target_pairs={{0,8},{4,20},{8,24},{12,4},{16,0},{20,28},{24,16},{28,12},{1,9},{5... | collective-permute-start | bytes 2064392 | tf_op jit(solution)/shard_map/ppermute | solution.py:110
  171.1 48.4 %collective-permute-start.16 = (bf16[3,256,1792]{2,1,0:T(8,128)(2,1)S(1)}, bf16[3,256,1792]{2,1,0:T(8,128)(2,1)S(1)}, u32[]{:S(2)}, u32[]{:S(2)}) collective-permute-start(bf16[3,256,1792]{2,1,0:T(8,128)(2,1)S(1)} %get-tuple-element.8), channel_id=1, source_target_pairs={{0,4},{4,0},{8,12},{12,8},{16,20},{20,16},{24,28},{28,24},{1,5},{5... | collective-permute-start | bytes 8257544 | tf_op jit(solution)/shard_map/ppermute | solution.py:105
  171.5 11.0 %collective-permute-start.12 = (bf16[3,64,1792]{2,1,0:T(8,128)(2,1)S(1)}, bf16[3,64,1792]{2,1,0:T(8,128)(2,1)S(1)}, u32[]{:S(2)}, u32[]{:S(2)}) collective-permute-start(bf16[3,64,1792]{2,1,0:T(8,128)(2,1)S(1)} %get-tuple-element.28), channel_id=1, source_target_pairs={{0,8},{4,20},{8,24},{12,4},{16,0},{20,28},{24,16},{28,12},{1,9},{5... | collective-permute-start | bytes 2064392 | tf_op jit(solution)/shard_map/ppermute | solution.py:125
  173.3 16.5 %collective-permute-start.4 = (bf16[3,64,1792]{2,1,0:T(8,128)(2,1)S(1)}, bf16[3,64,1792]{2,1,0:T(8,128)(2,1)S(1)}, u32[]{:S(2)}, u32[]{:S(2)}) collective-permute-start(bf16[3,64,1792]{2,1,0:T(8,128)(2,1)S(1)} %get-tuple-element.30), channel_id=1, source_target_pairs={{0,8},{4,20},{8,24},{12,4},{16,0},{20,28},{24,16},{28,12},{1,9},{5... | collective-permute-start | bytes 2064392 | tf_op jit(solution)/shard_map/ppermute | solution.py:125
  182.5 14.7 %collective-permute-start.13 = (bf16[3,64,1792]{2,1,0:T(8,128)(2,1)S(1)}, bf16[3,64,1792]{2,1,0:T(8,128)(2,1)S(1)}, u32[]{:S(2)}, u32[]{:S(2)}) collective-permute-start(bf16[3,64,1792]{2,1,0:T(8,128)(2,1)S(1)} %collective-permute-done.12), channel_id=1, source_target_pairs={{0,8},{4,20},{8,24},{12,4},{16,0},{20,28},{24,16},{28,12},{1,9},{5... | collective-permute-start | bytes 2064392 | tf_op jit(solution)/shard_map/ppermute | solution.py:125
  183.9 37.9 %collective-permute-start.24 = (bf16[3,256,1792]{2,1,0:T(8,128)(2,1)}, bf16[3,256,1792]{2,1,0:T(8,128)(2,1)S(1)}, u32[]{:S(2)}, u32[]{:S(2)}) collective-permute-start(bf16[3,256,1792]{2,1,0:T(8,128)(2,1)} %get-tuple-element.10), channel_id=1, source_target_pairs={{0,4},{4,0},{8,12},{12,8},{16,20},{20,16},{24,28},{28,24},{1,5},{5... | collective-permute-start | bytes 8257544 | tf_op jit(solution)/shard_map/ppermute | solution.py:105
  189.8 14.7 %collective-permute-start.5 = (bf16[3,64,1792]{2,1,0:T(8,128)(2,1)S(1)}, bf16[3,64,1792]{2,1,0:T(8,128)(2,1)S(1)}, u32[]{:S(2)}, u32[]{:S(2)}) collective-permute-start(bf16[3,64,1792]{2,1,0:T(8,128)(2,1)S(1)} %collective-permute-done.4), channel_id=1, source_target_pairs={{0,8},{4,20},{8,24},{12,4},{16,0},{20,28},{24,16},{28,12},{1,9},{5... | collective-permute-start | bytes 2064392 | tf_op jit(solution)/shard_map/ppermute | solution.py:125
  197.2 14.7 %collective-permute-start.14 = (bf16[3,64,1792]{2,1,0:T(8,128)(2,1)S(1)}, bf16[3,64,1792]{2,1,0:T(8,128)(2,1)S(1)}, u32[]{:S(2)}, u32[]{:S(2)}) collective-permute-start(bf16[3,64,1792]{2,1,0:T(8,128)(2,1)S(1)} %collective-permute-done.13), channel_id=1, source_target_pairs={{0,8},{4,20},{8,24},{12,4},{16,0},{20,28},{24,16},{28,12},{1,9},{5... | collective-permute-start | bytes 2064392 | tf_op jit(solution)/shard_map/ppermute | solution.py:125
  204.6 14.7 %collective-permute-start.6 = (bf16[3,64,1792]{2,1,0:T(8,128)(2,1)S(1)}, bf16[3,64,1792]{2,1,0:T(8,128)(2,1)S(1)}, u32[]{:S(2)}, u32[]{:S(2)}) collective-permute-start(bf16[3,64,1792]{2,1,0:T(8,128)(2,1)S(1)} %collective-permute-done.5), channel_id=1, source_target_pairs={{0,8},{4,20},{8,24},{12,4},{16,0},{20,28},{24,16},{28,12},{1,9},{5... | collective-permute-start | bytes 2064392 | tf_op jit(solution)/shard_map/ppermute | solution.py:125
  212.0 43.1 %collective-permute-start.15 = (bf16[3,256,1792]{2,1,0:T(8,128)(2,1)S(1)}, bf16[3,256,1792]{2,1,0:T(8,128)(2,1)}, u32[]{:S(2)}, u32[]{:S(2)}) collective-permute-start(bf16[3,256,1792]{2,1,0:T(8,128)(2,1)S(1)} %constant_dynamic-update-slice_fusion.17), channel_id=1, source_target_pairs={{0,4},{4,0},{8,12},{12,8},{16,20},{20,16},{24,28},{28,24},{1,5},{5... | collective-permute-start | bytes 8257544 | tf_op jit(solution)/shard_map/ppermute | solution.py:127
  219.4 43.3 %collective-permute-start.7 = (bf16[3,256,1792]{2,1,0:T(8,128)(2,1)S(1)}, bf16[3,256,1792]{2,1,0:T(8,128)(2,1)}, u32[]{:S(2)}, u32[]{:S(2)}) collective-permute-start(bf16[3,256,1792]{2,1,0:T(8,128)(2,1)S(1)} %constant_dynamic-update-slice_fusion.23), channel_id=1, source_target_pairs={{0,4},{4,0},{8,12},{12,8},{16,20},{20,16},{24,28},{28,24},{1,5},{5... | collective-permute-start | bytes 8257544 | tf_op jit(solution)/shard_map/ppermute | solution.py:127
  220.2 11.2 %collective-permute-start.17 = (bf16[3,64,1792]{2,1,0:T(8,128)(2,1)S(1)}, bf16[3,64,1792]{2,1,0:T(8,128)(2,1)S(1)}, u32[]{:S(2)}, u32[]{:S(2)}) collective-permute-start(bf16[3,64,1792]{2,1,0:T(8,128)(2,1)S(1)} %dynamic-slice_convert_fusion.1), channel_id=1, source_target_pairs={{0,8},{4,20},{8,24},{12,4},{16,0},{20,28},{24,16},{28,12},{1,9},{5... | collective-permute-start | bytes 2064392 | tf_op jit(solution)/shard_map/ppermute | solution.py:110
  222.6 16.1 %collective-permute-start.25 = (bf16[3,64,1792]{2,1,0:T(8,128)(2,1)S(1)}, bf16[3,64,1792]{2,1,0:T(8,128)(2,1)S(1)}, u32[]{:S(2)}, u32[]{:S(2)}) collective-permute-start(bf16[3,64,1792]{2,1,0:T(8,128)(2,1)S(1)} %dynamic-slice_convert_fusion), channel_id=1, source_target_pairs={{0,8},{4,20},{8,24},{12,4},{16,0},{20,28},{24,16},{28,12},{1,9},{5... | collective-permute-start | bytes 2064392 | tf_op jit(solution)/shard_map/ppermute | solution.py:110
  231.5 14.6 %collective-permute-start.18 = (bf16[3,64,1792]{2,1,0:T(8,128)(2,1)S(1)}, bf16[3,64,1792]{2,1,0:T(8,128)(2,1)S(1)}, u32[]{:S(2)}, u32[]{:S(2)}) collective-permute-start(bf16[3,64,1792]{2,1,0:T(8,128)(2,1)S(1)} %add_convert_fusion.4), channel_id=1, source_target_pairs={{0,8},{4,20},{8,24},{12,4},{16,0},{20,28},{24,16},{28,12},{1,9},{5... | collective-permute-start | bytes 2064392 | tf_op jit(solution)/shard_map/ppermute | solution.py:110
  238.8 14.6 %collective-permute-start.26 = (bf16[3,64,1792]{2,1,0:T(8,128)(2,1)S(1)}, bf16[3,64,1792]{2,1,0:T(8,128)(2,1)S(1)}, u32[]{:S(2)}, u32[]{:S(2)}) collective-permute-start(bf16[3,64,1792]{2,1,0:T(8,128)(2,1)S(1)} %add_convert_fusion.2), channel_id=1, source_target_pairs={{0,8},{4,20},{8,24},{12,4},{16,0},{20,28},{24,16},{28,12},{1,9},{5... | collective-permute-start | bytes 2064392 | tf_op jit(solution)/shard_map/ppermute | solution.py:110
  247.1 67.3 %collective-permute-start.19 = (bf16[3,64,1792]{2,1,0:T(8,128)(2,1)}, bf16[3,64,1792]{2,1,0:T(8,128)(2,1)S(1)}, u32[]{:S(2)}, u32[]{:S(2)}) collective-permute-start(bf16[3,64,1792]{2,1,0:T(8,128)(2,1)} %add_convert_fusion.3), channel_id=1, source_target_pairs={{0,8},{4,20},{8,24},{12,4},{16,0},{20,28},{24,16},{28,12},{1,9},{5... | collective-permute-start | bytes 2064392 | tf_op jit(solution)/shard_map/ppermute | solution.py:110
  253.6 77.0 %collective-permute-start.27 = (bf16[3,64,1792]{2,1,0:T(8,128)(2,1)S(1)}, bf16[3,64,1792]{2,1,0:T(8,128)(2,1)S(1)}, u32[]{:S(2)}, u32[]{:S(2)}) collective-permute-start(bf16[3,64,1792]{2,1,0:T(8,128)(2,1)S(1)} %add_convert_fusion.1), channel_id=1, source_target_pairs={{0,8},{4,20},{8,24},{12,4},{16,0},{20,28},{24,16},{28,12},{1,9},{5... | collective-permute-start | bytes 2064392 | tf_op jit(solution)/shard_map/ppermute | solution.py:110
  264.8 11.7 %copy-start.4 = (bf16[3,512,1792]{2,1,0:T(8,128)(2,1)}, bf16[3,512,1792]{2,1,0:T(8,128)(2,1)S(1)}, u32[]{:S(2)}) copy-start(bf16[3,512,1792]{2,1,0:T(8,128)(2,1)S(1)} %constant_dynamic-update-slice_fusion.21) | copy-start | bytes 16515076
  270.9 5.6 %copy-start.9 = (bf16[512,2048]{1,0:T(8,128)(2,1)S(1)}, bf16[512,2048]{1,0:T(8,128)(2,1)}, u32[]{:S(2)}) copy-start(bf16[512,2048]{1,0:T(8,128)(2,1)} %all-gather.2.cloned.1.call-done) | copy-start | bytes 6291460
  318.0 6.6 %copy-start.2 = (bf16[1024,7168]{1,0:T(8,128)(2,1)}, bf16[1024,7168]{1,0:T(8,128)(2,1)S(1)}, u32[]{:S(2)}) copy-start(bf16[1024,7168]{1,0:T(8,128)(2,1)S(1)} %constant_dynamic-update-slice_fusion.1) | copy-start | bytes 44040196
  329.1 11.0 %collective-permute-start.20 = (bf16[3,64,1792]{2,1,0:T(8,128)(2,1)S(1)}, bf16[3,64,1792]{2,1,0:T(8,128)(2,1)S(1)}, u32[]{:S(2)}, u32[]{:S(2)}) collective-permute-start(bf16[3,64,1792]{2,1,0:T(8,128)(2,1)S(1)} %get-tuple-element.24), channel_id=1, source_target_pairs={{0,8},{4,20},{8,24},{12,4},{16,0},{20,28},{24,16},{28,12},{1,9},{5... | collective-permute-start | bytes 2064392 | tf_op jit(solution)/shard_map/ppermute | solution.py:125
  340.1 10.9 %collective-permute-start.21 = (bf16[3,64,1792]{2,1,0:T(8,128)(2,1)S(1)}, bf16[3,64,1792]{2,1,0:T(8,128)(2,1)S(1)}, u32[]{:S(2)}, u32[]{:S(2)}) collective-permute-start(bf16[3,64,1792]{2,1,0:T(8,128)(2,1)S(1)} %collective-permute-done.20), channel_id=1, source_target_pairs={{0,8},{4,20},{8,24},{12,4},{16,0},{20,28},{24,16},{28,12},{1,9},{5... | collective-permute-start | bytes 2064392 | tf_op jit(solution)/shard_map/ppermute | solution.py:125
  341.8 16.6 %collective-permute-start.28 = (bf16[3,64,1792]{2,1,0:T(8,128)(2,1)S(1)}, bf16[3,64,1792]{2,1,0:T(8,128)(2,1)S(1)}, u32[]{:S(2)}, u32[]{:S(2)}) collective-permute-start(bf16[3,64,1792]{2,1,0:T(8,128)(2,1)S(1)} %get-tuple-element.26), channel_id=1, source_target_pairs={{0,8},{4,20},{8,24},{12,4},{16,0},{20,28},{24,16},{28,12},{1,9},{5... | collective-permute-start | bytes 2064392 | tf_op jit(solution)/shard_map/ppermute | solution.py:125
  351.0 14.7 %collective-permute-start.22 = (bf16[3,64,1792]{2,1,0:T(8,128)(2,1)S(1)}, bf16[3,64,1792]{2,1,0:T(8,128)(2,1)S(1)}, u32[]{:S(2)}, u32[]{:S(2)}) collective-permute-start(bf16[3,64,1792]{2,1,0:T(8,128)(2,1)S(1)} %collective-permute-done.21), channel_id=1, source_target_pairs={{0,8},{4,20},{8,24},{12,4},{16,0},{20,28},{24,16},{28,12},{1,9},{5... | collective-permute-start | bytes 2064392 | tf_op jit(solution)/shard_map/ppermute | solution.py:125
  358.4 14.7 %collective-permute-start.29 = (bf16[3,64,1792]{2,1,0:T(8,128)(2,1)S(1)}, bf16[3,64,1792]{2,1,0:T(8,128)(2,1)S(1)}, u32[]{:S(2)}, u32[]{:S(2)}) collective-permute-start(bf16[3,64,1792]{2,1,0:T(8,128)(2,1)S(1)} %collective-permute-done.28), channel_id=1, source_target_pairs={{0,8},{4,20},{8,24},{12,4},{16,0},{20,28},{24,16},{28,12},{1,9},{5... | collective-permute-start | bytes 2064392 | tf_op jit(solution)/shard_map/ppermute | solution.py:125
  365.8 19.9 %collective-permute-start.23 = (bf16[3,256,1792]{2,1,0:T(8,128)(2,1)S(1)}, bf16[3,256,1792]{2,1,0:T(8,128)(2,1)S(1)}, u32[]{:S(2)}, u32[]{:S(2)}) collective-permute-start(bf16[3,256,1792]{2,1,0:T(8,128)(2,1)S(1)} %constant_dynamic-update-slice_fusion.11), channel_id=1, source_target_pairs={{0,4},{4,0},{8,12},{12,8},{16,20},{20,16},{24,28},{28,24},{1,5},{5... | collective-permute-start | bytes 8257544 | tf_op jit(solution)/shard_map/ppermute | solution.py:127
  373.1 11.1 %collective-permute-start.30 = (bf16[3,64,1792]{2,1,0:T(8,128)(2,1)S(1)}, bf16[3,64,1792]{2,1,0:T(8,128)(2,1)S(1)}, u32[]{:S(2)}, u32[]{:S(2)}) collective-permute-start(bf16[3,64,1792]{2,1,0:T(8,128)(2,1)S(1)} %collective-permute-done.29), channel_id=1, source_target_pairs={{0,8},{4,20},{8,24},{12,4},{16,0},{20,28},{24,16},{28,12},{1,9},{5... | collective-permute-start | bytes 2064392 | tf_op jit(solution)/shard_map/ppermute | solution.py:125
  384.3 12.1 %collective-permute-start.31 = (bf16[3,256,1792]{2,1,0:T(8,128)(2,1)S(1)}, bf16[3,256,1792]{2,1,0:T(8,128)(2,1)S(1)}, u32[]{:S(2)}, u32[]{:S(2)}) collective-permute-start(bf16[3,256,1792]{2,1,0:T(8,128)(2,1)S(1)} %constant_dynamic-update-slice_fusion.5), channel_id=1, source_target_pairs={{0,4},{4,0},{8,12},{12,8},{16,20},{20,16},{24,28},{28,24},{1,5},{5... | collective-permute-start | bytes 8257544 | tf_op jit(solution)/shard_map/ppermute | solution.py:127
  386.1 10.3 %copy-start.5 = (bf16[3,512,1792]{2,1,0:T(8,128)(2,1)}, bf16[3,512,1792]{2,1,0:T(8,128)(2,1)S(1)}, u32[]{:S(2)}) copy-start(bf16[3,512,1792]{2,1,0:T(8,128)(2,1)S(1)} %constant_dynamic-update-slice_fusion.9) | copy-start | bytes 16515076
  396.7 6.2 %copy-start.3 = (bf16[3,512,1792]{2,1,0:T(8,128)(2,1)}, bf16[3,512,1792]{2,1,0:T(8,128)(2,1)S(1)}, u32[]{:S(2)}) copy-start(bf16[3,512,1792]{2,1,0:T(8,128)(2,1)S(1)} %constant_dynamic-update-slice_fusion.3) | copy-start | bytes 16515076
  396.7 6.2 %copy-start.12 = (f32[512,1024]{1,0:T(8,128)S(1)}, f32[512,1024]{1,0:T(8,128)}, u32[]{:S(2)}) copy-start(f32[512,1024]{1,0:T(8,128)} %add_add_fusion) | copy-start | bytes 6291460
  402.9 5.5 %copy-start.11 = (bf16[512,2048]{1,0:T(8,128)(2,1)S(1)}, bf16[512,2048]{1,0:T(8,128)(2,1)}, u32[]{:S(2)}) copy-start(bf16[512,2048]{1,0:T(8,128)(2,1)} %all-gather.2.cloned.1.call-done) | copy-start | bytes 6291460
  408.3 5.7 %slice-start = ((s8[5505024]{0:T(1024)(128)(4,1)}), s8[1310720]{0:T(1024)(128)(4,1)S(1)}, s32[]{:S(2)}) async-start(s8[5505024]{0:T(1024)(128)(4,1)} %bitcast.85), calls=%async_computation.3 | async-start | bytes 2621440
  408.4 5.6 %slice-start.1 = ((s8[5505024]{0:T(1024)(128)(4,1)}), s8[4194304]{0:T(1024)(128)(4,1)S(1)}, s32[]{:S(2)}) async-start(s8[5505024]{0:T(1024)(128)(4,1)} %bitcast.85), calls=%async_computation.4 | async-start | bytes 8388608
  408.4 9.6 %slice-start.2 = ((s8[5505024]{0:T(1024)(128)(4,1)}), s8[4194304]{0:T(1024)(128)(4,1)S(1)}, s32[]{:S(2)}) async-start(s8[5505024]{0:T(1024)(128)(4,1)} %bitcast.87), calls=%async_computation.5 | async-start | bytes 8388608
  (3 other events, 12.1 us)
Sparse Core Ops, SparseCore 0:
  10.1 48.6 all-gather.1
  408.5 25.1 reduce-scatter.1

commit v3 on v2

--- a/solution.py
+++ b/solution.py
@@ -6,6 +6,9 @@
 N_CHUNKS = 4
 GROUP = 2
 FWD_GATE = -1
+GATE_BWD = 0
+FWD_IN_STEP = -1
+GATHER_AFTER_BWD = 0
 F32 = jnp.float32
 BF16 = jnp.bfloat16
 
@@ -79,45 +82,45 @@
         columns = gate_weight.shape[1]
         w = columns // N_CHUNKS
 
-        input_acc = jnp.zeros((n_tok, width), F32)
-        gate_out = jnp.zeros((width, columns), BF16)
-        up_out = jnp.zeros((width, columns), BF16)
-        down_out = jnp.zeros((columns, width), BF16)
-        x_chunk, dy_chunk = x_panel, dy_panel
-        reduced, grads, exchanged = {}, {}, {}
-        for j in range(N_CHUNKS):
-            cols = slice(j * w, (j + 1) * w)
-            gw = gate_weight[:, cols]
-            uw = up_weight[:, cols]
-            parts = jnp.stack(
-                [
-                    jnp.dot(x_chunk, gw, preferred_element_type=F32).astype(BF16),
-                    jnp.dot(x_chunk, uw, preferred_element_type=F32).astype(BF16),
-                    contract_cols(dy_chunk, down_weight[cols, :]).astype(BF16),
-                ]
-            )
+        state = {
+            "input": jnp.zeros((n_tok, width), F32),
+            "gate": jnp.zeros((width, columns), BF16),
+            "up": jnp.zeros((width, columns), BF16),
+            "down": jnp.zeros((columns, width), BF16),
+        }
+        made, first, reduced, grads = {}, {}, {}, {}
+        groups = [list(range(g, min(g + GROUP, N_CHUNKS))) for g in range(0, N_CHUNKS, GROUP)]
+
+        def forward(j):
+            if j not in made:
+                cols = slice(j * w, (j + 1) * w)
+                made[j] = jnp.stack(
+                    [
+                        jnp.dot(x_panel, gate_weight[:, cols], preferred_element_type=F32).astype(BF16),
+                        jnp.dot(x_panel, up_weight[:, cols], preferred_element_type=F32).astype(BF16),
+                        contract_cols(dy_panel, down_weight[cols, :]).astype(BF16),
+                    ]
+                )
+            return made[j]
+
+        def reduce_chunk(j, waits, later):
+            parts = forward(j)
             own = rows(parts, core * half, half)
             other = rows(parts, (1 - core) * half, half)
-            g = j // GROUP
-            before = [i for i in range(N_CHUNKS) if i // GROUP == g - 1]
-            if before:
-                other, _ = lax.optimization_barrier((other, [reduced[i] for i in before]))
+            if waits:
+                other, _ = lax.optimization_barrier((other, waits))
             got = lax.ppermute(other, "row", core_pairs)
+            first[j] = got
             summed = own.astype(F32) + got.astype(F32)
             acc = rows(summed, ((pos - 1) % chips) * block, block)
-            steps = [got]
             for s in range(chips - 1):
+                if s == FWD_IN_STEP and later is not None:
+                    acc, _ = lax.optimization_barrier((acc, forward(later)))
                 got = lax.ppermute(acc.astype(BF16), "row", ring_pairs)
                 acc = got.astype(F32) + rows(summed, ((pos - s - 2) % chips) * block, block)
-                steps.append(got)
-            exchanged[j] = steps[min(FWD_GATE, len(steps) - 1)]
-            if FWD_GATE >= 0 and j % GROUP == GROUP - 1 and j + 1 < N_CHUNKS:
-                x_chunk, dy_chunk, _ = lax.optimization_barrier(
-                    (x_panel, dy_panel, [exchanged[i] for i in range(j - GROUP + 1, j + 1)])
-                )
-            reduced[j] = acc
-            if before:
-                acc, _ = lax.optimization_barrier((acc, [grads[i] for i in before]))
+            return acc
+
+        def gather_chunk(acc):
             act = jnp.stack(activations(acc[0], acc[1], acc[2]))
             held = put(jnp.zeros((3, half, w), BF16), act, pos * block)
             cur = act
@@ -126,20 +129,45 @@
                 held = put(held, cur, ((pos - s - 1) % chips) * block)
             partner = lax.ppermute(held, "row", core_pairs)
             full = put(jnp.zeros((3, n_tok, w), BF16), held, core * half)
-            full = put(full, partner, (1 - core) * half)
+            return put(full, partner, (1 - core) * half)
+
+        def backward(j, full):
+            cols = slice(j * w, (j + 1) * w)
             hidden, grad_gate_act, grad_up_act = full[0], full[1], full[2]
             down_piece = contract_rows(hidden, dy_panel).astype(BF16)
             gate_piece = contract_rows(x_panel, grad_gate_act).astype(BF16)
             up_piece = contract_rows(x_panel, grad_up_act).astype(BF16)
-            input_acc = (
-                input_acc
-                + contract_cols(grad_gate_act, gw)
-                + contract_cols(grad_up_act, uw)
+            state["input"] = (
+                state["input"]
+                + contract_cols(grad_gate_act, gate_weight[:, cols])
+                + contract_cols(grad_up_act, up_weight[:, cols])
             )
-            grads[j] = (down_piece, gate_piece, up_piece, input_acc)
-            gate_out = lax.dynamic_update_slice(gate_out, gate_piece, (0, j * w))
-            up_out = lax.dynamic_update_slice(up_out, up_piece, (0, j * w))
-            down_out = lax.dynamic_update_slice(down_out, down_piece, (j * w, 0))
+            grads[j] = (down_piece, gate_piece, up_piece, state["input"])
+            state["gate"] = lax.dynamic_update_slice(state["gate"], gate_piece, (0, j * w))
+            state["up"] = lax.dynamic_update_slice(state["up"], up_piece, (0, j * w))
+            state["down"] = lax.dynamic_update_slice(state["down"], down_piece, (j * w, 0))
+
+        full_of = {}
+        for g, group in enumerate(groups):
+            nxt = groups[g + 1] if g + 1 < len(groups) else []
+            waits = [reduced[i] for i in groups[g - 1]] if g else []
+            for k, j in enumerate(group):
+                reduced[j] = reduce_chunk(j, waits, nxt[k] if k < len(nxt) else None)
+            if g:
+                for i in groups[g - 1]:
+                    full = full_of[i]
+                    if GATE_BWD:
+                        full, _ = lax.optimization_barrier((full, [first[j] for j in group]))
+                    backward(i, full)
+            for j in group:
+                acc = reduced[j]
+                if g and GATHER_AFTER_BWD:
+                    acc, _ = lax.optimization_barrier((acc, [grads[i] for i in groups[g - 1]]))
+                full_of[j] = gather_chunk(acc)
+        for j in groups[-1]:
+            backward(j, full_of[j])
+        input_acc = state["input"]
+        gate_out, up_out, down_out = state["gate"], state["up"], state["down"]
         input_sum = lax.psum_scatter(
             input_acc.astype(BF16), "col", scatter_dimension=0, tiled=True
         )

time: 446 us -> 420 us (0.942)
  waiting for transfers between devices: 178 us -> 157 us
  matrix products: 147 us -> 140 us
    ppermute x32, waiting for transfers between devices: 133 us -> 112 us  [the longest x12 60.5 us: reduce_chunk(): got = lax.ppermute(acc.astype(BF16), 'row', ring_pairs)]
    dynamic_update_slice x20, local copies, waits for them, and re-layouts: 6.67 us -> 11.9 us  [put(): return lax.dynamic_update_slice_in_dim(array, piece, start, 1)]
  transfers between devices with their start and end apart: 34 -> 34, of which waited for: 23 -> 21; matrix products, arithmetic and copies ran while one was open for 40% -> 39% of each run, Pallas kernels for 0% -> 0%
where the time goes in v3:
time: 420 us; the launch traced here: 415 us
  waiting for transfers between devices  157 us (37%)
  matrix products  140 us (33%)
  local copies, waits for them, and re-layouts  41.5 us (10%)
  starting transfers between devices  35.1 us (8%)
  other arithmetic  22.3 us (5%)
  between operations  18.6 us (4%)
    dot_general x12, matrix products, contract_cols(): lax.dot_general(left, right, (((1,), (1,)), ((), ())), preferred_element_...  61.9 us
    ppermute x12, waiting for transfers between devices, reduce_chunk(): got = lax.ppermute(acc.astype(BF16), 'row', ring_pairs)  60.5 us
    ppermute x12, waiting for transfers between devices, gather_chunk(): cur = lax.ppermute(cur, 'row', ring_pairs)  51.3 us
    all_gather x1, waiting for transfers between devices, per_device(): lax.all_gather(jnp.concatenate([tokens, cotangent], axis=1), 'col', axis=...  45.1 us
    dot_general x12, matrix products, contract_rows(): lax.dot_general(left, right, (((0,), (0,)), ((), ())), preferred_element_...  43.5 us
    ppermute x12, starting transfers between devices, reduce_chunk(): got = lax.ppermute(acc.astype(BF16), 'row', ring_pairs)  18.5 us
    dot_general x4, matrix products, forward(): jnp.dot(x_panel, up_weight[:, cols], preferred_element_type=F32)  18.1 us
    dot_general x4, matrix products, forward(): jnp.dot(x_panel, gate_weight[:, cols], preferred_element_type=F32)  16.9 us
  transfers between devices with their start and end apart: 34, of which 21 were waited for; matrix products, arithmetic and copies ran while one was open for 39% of the time, Pallas kernels for 0%

profile of v3, /device:TPU:0, one launch (start us, length us, event | category | flops | bytes accessed | tf_op | source)
XLA Modules:
  0.0 414.9 jit_solution(14922008290176898891)
XLA Ops:
  13.7 45.1 %all-gather.2.cloned.1.call-done = bf16[512,2048]{1,0:T(8,128)(2,1)} async-done(((bf16[128,2048]{1,0:T(8,128)(2,1)}), bf16[512,2048]{1,0:T(8,128)(2,1)}) %all-gather.2.cloned.1.call-update) | async-done | bytes 2097168 | tf_op jit(solution)/shard_map/all_gather | solution.py:74
  58.8 4.6 %fusion.115 = bf16[1,512,1792]{2,1,0:T(8,128)(2,1)S(1)} fusion(bf16[1024,7168]{1,0:T(8,128)(2,1)} %param.9, bf16[512,2048]{1,0:T(8,128)(2,1)} %all-gather.2.cloned.1.call-done), kind=kOutput, calls=%fused_computation.91 | convolution fusion | flops 1879965696 | bytes 6553600 | tf_op jit(solution)/shard_map/dot_general | solution.py:100
  63.4 4.2 %fusion.94 = bf16[1,512,1792]{2,1,0:T(8,128)(2,1)S(1)} fusion(bf16[7168,1024]{1,0:T(8,128)(2,1)} %param.10, bf16[512,2048]{1,0:T(8,128)(2,1)S(1)} %copy-done.6), kind=kOutput, calls=%fused_computation.84 | convolution fusion | flops 1879965696 | bytes 6553600 | tf_op jit(solution)/shard_map/dot_general | solution.py:32
  67.6 4.1 fusion.118
  74.3 4.1 fusion.112
  78.4 4.1 fusion.109
  82.5 4.2 %fusion.91 = bf16[1,512,1792]{2,1,0:T(8,128)(2,1)S(1)} fusion(bf16[7168,1024]{1,0:T(8,128)(2,1)} %param.10, bf16[512,2048]{1,0:T(8,128)(2,1)S(1)} %copy-done.6), kind=kOutput, calls=%fused_computation.83 | convolution fusion | flops 1879965696 | bytes 6553600 | tf_op jit(solution)/shard_map/dot_general | solution.py:32
  88.2 4.1 fusion.106
  92.4 4.1 fusion.103
  96.5 5.4 %fusion.88 = bf16[1,512,1792]{2,1,0:T(8,128)(2,1)} fusion(bf16[7168,1024]{1,0:T(8,128)(2,1)} %param.10, bf16[512,2048]{1,0:T(8,128)(2,1)S(1)} %copy-done.7), kind=kOutput, calls=%fused_computation.82 | convolution fusion | flops 1879965696 | bytes 6553600 | tf_op jit(solution)/shard_map/dot_general | solution.py:32
  104.7 4.6 %fusion.100 = bf16[1,512,1792]{2,1,0:T(8,128)(2,1)S(1)} fusion(bf16[1024,7168]{1,0:T(8,128)(2,1)} %param.8, bf16[512,2048]{1,0:T(8,128)(2,1)} %all-gather.2.cloned.1.call-done), kind=kOutput, calls=%fused_computation.86 | convolution fusion | flops 1879965696 | bytes 6553600 | tf_op jit(solution)/shard_map/dot_general | solution.py:99
  109.3 5.3 %fusion.97 = bf16[1,512,1792]{2,1,0:T(8,128)(2,1)} fusion(bf16[1024,7168]{1,0:T(8,128)(2,1)} %param.9, bf16[512,2048]{1,0:T(8,128)(2,1)S(1)} %copy-done.8), kind=kOutput, calls=%fused_computation.85 | convolution fusion | flops 1879965696 | bytes 6553600 | tf_op jit(solution)/shard_map/dot_general | solution.py:100
  114.6 5.4 %fusion.85 = bf16[1,512,1792]{2,1,0:T(8,128)(2,1)} fusion(bf16[7168,1024]{1,0:T(8,128)(2,1)} %param.10, bf16[512,2048]{1,0:T(8,128)(2,1)S(1)} %copy-done.8), kind=kOutput, calls=%fused_computation.81 | convolution fusion | flops 1879965696 | bytes 6553600 | tf_op jit(solution)/shard_map/dot_general | solution.py:32
  129.0 4.6 %collective-permute-done.9 = bf16[3,64,1792]{2,1,0:T(8,128)(2,1)S(1)} collective-permute-done((bf16[3,64,1792]{2,1,0:T(8,128)(2,1)S(1)}, bf16[3,64,1792]{2,1,0:T(8,128)(2,1)S(1)}, u32[]{:S(2)}, u32[]{:S(2)}) %collective-permute-start.9) | collective-permute-done | bytes 688160 | tf_op jit(solution)/shard_map/ppermute | solution.py:119
  143.8 4.6 %collective-permute-done.10 = bf16[3,64,1792]{2,1,0:T(8,128)(2,1)} collective-permute-done((bf16[3,64,1792]{2,1,0:T(8,128)(2,1)}, bf16[3,64,1792]{2,1,0:T(8,128)(2,1)}, u32[]{:S(2)}, u32[]{:S(2)}) %collective-permute-start.10) | collective-permute-done | bytes 688160 | tf_op jit(solution)/shard_map/ppermute | solution.py:119
  157.3 5.7 %collective-permute-done.11 = bf16[3,64,1792]{2,1,0:T(8,128)(2,1)S(1)} collective-permute-done((bf16[3,64,1792]{2,1,0:T(8,128)(2,1)S(1)}, bf16[3,64,1792]{2,1,0:T(8,128)(2,1)S(1)}, u32[]{:S(2)}, u32[]{:S(2)}) %collective-permute-start.11) | collective-permute-done | bytes 688160 | tf_op jit(solution)/shard_map/ppermute | solution.py:119
  163.5 7.0 %collective-permute-done.3 = bf16[3,64,1792]{2,1,0:T(8,128)(2,1)S(1)} collective-permute-done((bf16[3,64,1792]{2,1,0:T(8,128)(2,1)S(1)}, bf16[3,64,1792]{2,1,0:T(8,128)(2,1)S(1)}, u32[]{:S(2)}, u32[]{:S(2)}) %collective-permute-start.3) | collective-permute-done | bytes 688160 | tf_op jit(solution)/shard_map/ppermute | solution.py:119
  174.5 7.7 %collective-permute-done.12 = bf16[3,64,1792]{2,1,0:T(8,128)(2,1)S(1)} collective-permute-done((bf16[3,64,1792]{2,1,0:T(8,128)(2,1)S(1)}, bf16[3,64,1792]{2,1,0:T(8,128)(2,1)S(1)}, u32[]{:S(2)}, u32[]{:S(2)}) %collective-permute-start.12) | collective-permute-done | bytes 688160 | tf_op jit(solution)/shard_map/ppermute | solution.py:128
  183.7 5.9 %collective-permute-done.4 = bf16[3,64,1792]{2,1,0:T(8,128)(2,1)S(1)} collective-permute-done((bf16[3,64,1792]{2,1,0:T(8,128)(2,1)S(1)}, bf16[3,64,1792]{2,1,0:T(8,128)(2,1)S(1)}, u32[]{:S(2)}, u32[]{:S(2)}) %collective-permute-start.4) | collective-permute-done | bytes 688160 | tf_op jit(solution)/shard_map/ppermute | solution.py:128
  191.1 5.9 %collective-permute-done.13 = bf16[3,64,1792]{2,1,0:T(8,128)(2,1)S(1)} collective-permute-done((bf16[3,64,1792]{2,1,0:T(8,128)(2,1)S(1)}, bf16[3,64,1792]{2,1,0:T(8,128)(2,1)S(1)}, u32[]{:S(2)}, u32[]{:S(2)}) %collective-permute-start.13) | collective-permute-done | bytes 688160 | tf_op jit(solution)/shard_map/ppermute | solution.py:128
  198.4 5.9 %collective-permute-done.5 = bf16[3,64,1792]{2,1,0:T(8,128)(2,1)S(1)} collective-permute-done((bf16[3,64,1792]{2,1,0:T(8,128)(2,1)S(1)}, bf16[3,64,1792]{2,1,0:T(8,128)(2,1)S(1)}, u32[]{:S(2)}, u32[]{:S(2)}) %collective-permute-start.5) | collective-permute-done | bytes 688160 | tf_op jit(solution)/shard_map/ppermute | solution.py:128
  205.9 5.8 %collective-permute-done.14 = bf16[3,64,1792]{2,1,0:T(8,128)(2,1)S(1)} collective-permute-done((bf16[3,64,1792]{2,1,0:T(8,128)(2,1)S(1)}, bf16[3,64,1792]{2,1,0:T(8,128)(2,1)S(1)}, u32[]{:S(2)}, u32[]{:S(2)}) %collective-permute-start.14) | collective-permute-done | bytes 688160 | tf_op jit(solution)/shard_map/ppermute | solution.py:128
  211.8 7.2 %collective-permute-done.6 = bf16[3,64,1792]{2,1,0:T(8,128)(2,1)S(1)} collective-permute-done((bf16[3,64,1792]{2,1,0:T(8,128)(2,1)S(1)}, bf16[3,64,1792]{2,1,0:T(8,128)(2,1)S(1)}, u32[]{:S(2)}, u32[]{:S(2)}) %collective-permute-start.6) | collective-permute-done | bytes 688160 | tf_op jit(solution)/shard_map/ppermute | solution.py:128
  224.0 7.3 %collective-permute-done.17 = bf16[3,64,1792]{2,1,0:T(8,128)(2,1)S(1)} collective-permute-done((bf16[3,64,1792]{2,1,0:T(8,128)(2,1)S(1)}, bf16[3,64,1792]{2,1,0:T(8,128)(2,1)S(1)}, u32[]{:S(2)}, u32[]{:S(2)}) %collective-permute-start.17) | collective-permute-done | bytes 688160 | tf_op jit(solution)/shard_map/ppermute | solution.py:119
  233.6 5.0 %collective-permute-done.25 = bf16[3,64,1792]{2,1,0:T(8,128)(2,1)S(1)} collective-permute-done((bf16[3,64,1792]{2,1,0:T(8,128)(2,1)S(1)}, bf16[3,64,1792]{2,1,0:T(8,128)(2,1)S(1)}, u32[]{:S(2)}, u32[]{:S(2)}) %collective-permute-start.25) | collective-permute-done | bytes 688160 | tf_op jit(solution)/shard_map/ppermute | solution.py:119
  240.3 5.7 %collective-permute-done.18 = bf16[3,64,1792]{2,1,0:T(8,128)(2,1)S(1)} collective-permute-done((bf16[3,64,1792]{2,1,0:T(8,128)(2,1)S(1)}, bf16[3,64,1792]{2,1,0:T(8,128)(2,1)S(1)}, u32[]{:S(2)}, u32[]{:S(2)}) %collective-permute-start.18) | collective-permute-done | bytes 688160 | tf_op jit(solution)/shard_map/ppermute | solution.py:119
  248.4 5.0 %collective-permute-done.26 = bf16[3,64,1792]{2,1,0:T(8,128)(2,1)S(1)} collective-permute-done((bf16[3,64,1792]{2,1,0:T(8,128)(2,1)S(1)}, bf16[3,64,1792]{2,1,0:T(8,128)(2,1)S(1)}, u32[]{:S(2)}, u32[]{:S(2)}) %collective-permute-start.26) | collective-permute-done | bytes 688160 | tf_op jit(solution)/shard_map/ppermute | solution.py:119
  255.1 5.7 %collective-permute-done.19 = bf16[3,64,1792]{2,1,0:T(8,128)(2,1)S(1)} collective-permute-done((bf16[3,64,1792]{2,1,0:T(8,128)(2,1)S(1)}, bf16[3,64,1792]{2,1,0:T(8,128)(2,1)S(1)}, u32[]{:S(2)}, u32[]{:S(2)}) %collective-permute-start.19) | collective-permute-done | bytes 688160 | tf_op jit(solution)/shard_map/ppermute | solution.py:119
  263.0 5.2 %collective-permute-done.27 = bf16[3,64,1792]{2,1,0:T(8,128)(2,1)S(1)} collective-permute-done((bf16[3,64,1792]{2,1,0:T(8,128)(2,1)S(1)}, bf16[3,64,1792]{2,1,0:T(8,128)(2,1)S(1)}, u32[]{:S(2)}, u32[]{:S(2)}) %collective-permute-start.27) | collective-permute-done | bytes 688160 | tf_op jit(solution)/shard_map/ppermute | solution.py:119
  273.2 4.1 fusion.33
  281.9 10.5 %dynamic_update_slice.140 = bf16[7168,1024]{1,0:T(8,128)(2,1)} pad(bf16[1792,1024]{1,0:T(8,128)(2,1)S(1)} %convolution_convert_fusion.3, bf16[]{:T(256)} %constant.117.clone.1), padding=0_5376x0_0 | pad | bytes 18350082 | tf_op jit(solution)/shard_map/dynamic_update_slice | solution.py:148
  292.4 4.0 fusion.2
  296.4 5.4 %fusion.37 = f32[512,1024]{1,0:T(8,128)} fusion(bf16[1024,7168]{1,0:T(8,128)(2,1)} %param.8, bf16[3,512,1792]{2,1,0:T(8,128)(2,1)S(1)} %constant_dynamic-update-slice_fusion.12), kind=kOutput, calls=%fused_computation.57 | convolution fusion | flops 1879048192 | bytes 7602176 | tf_op jit(solution)/shard_map/dot_general | solution.py:32
  308.8 5.6 %fusion.41 = f32[512,1024]{1,0:T(8,128)} fusion(bf16[1024,7168]{1,0:T(8,128)(2,1)} %param.9, bf16[3,512,1792]{2,1,0:T(8,128)(2,1)S(1)} %constant_dynamic-update-slice_fusion.18), kind=kOutput, calls=%fused_computation.61 | convolution fusion | flops 1879048192 | bytes 7602176 | tf_op jit(solution)/shard_map/dot_general | solution.py:32
  319.3 6.3 %collective-permute-done.29 = bf16[3,64,1792]{2,1,0:T(8,128)(2,1)} collective-permute-done((bf16[3,64,1792]{2,1,0:T(8,128)(2,1)}, bf16[3,64,1792]{2,1,0:T(8,128)(2,1)}, u32[]{:S(2)}, u32[]{:S(2)}) %collective-permute-start.29) | collective-permute-done | bytes 688160 | tf_op jit(solution)/shard_map/ppermute | solution.py:128
  326.3 6.6 %collective-permute-done.22 = bf16[3,64,1792]{2,1,0:T(8,128)(2,1)S(1)} collective-permute-done((bf16[3,64,1792]{2,1,0:T(8,128)(2,1)S(1)}, bf16[3,64,1792]{2,1,0:T(8,128)(2,1)S(1)}, u32[]{:S(2)}, u32[]{:S(2)}) %collective-permute-start.22) | collective-permute-done | bytes 688160 | tf_op jit(solution)/shard_map/ppermute | solution.py:128
  336.4 7.3 %dynamic_update_slice.136 = bf16[1024,7168]{1,0:T(8,128)(2,1)} pad(bf16[1024,1792]{1,0:T(8,128)(2,1)S(1)} %convolution_convert_fusion.7, bf16[]{:T(256)} %constant.117.clone.1), padding=0_0x0_5376 | pad | bytes 18350082 | tf_op jit(solution)/shard_map/dynamic_update_slice | solution.py:147
  347.9 4.0 fusion.5
  351.8 5.4 %fusion.45 = f32[512,1024]{1,0:T(8,128)} fusion(bf16[1024,7168]{1,0:T(8,128)(2,1)} %param.8, bf16[3,512,1792]{2,1,0:T(8,128)(2,1)S(1)} %constant_dynamic-update-slice_fusion.18), kind=kOutput, calls=%fused_computation.65 | convolution fusion | flops 1879048192 | bytes 7602176 | tf_op jit(solution)/shard_map/dot_general | solution.py:32
  359.0 6.1 %fusion.25 = f32[512,1024]{1,0:T(8,128)S(1)} fusion(bf16[1024,7168]{1,0:T(8,128)(2,1)} %param.9, bf16[3,512,1792]{2,1,0:T(8,128)(2,1)S(1)} %constant_dynamic-update-slice_fusion.6), kind=kOutput, calls=%fused_computation.45 | convolution fusion | flops 1879048192 | bytes 7602176 | tf_op jit(solution)/shard_map/dot_general | solution.py:32
  365.1 4.1 fusion.29
  369.6 6.1 %fusion.21 = f32[512,1024]{1,0:T(8,128)S(1)} fusion(bf16[1024,7168]{1,0:T(8,128)(2,1)} %param.8, bf16[3,512,1792]{2,1,0:T(8,128)(2,1)S(1)} %constant_dynamic-update-slice_fusion), kind=kOutput, calls=%fused_computation.41 | convolution fusion | flops 1879048192 | bytes 7602176 | tf_op jit(solution)/shard_map/dot_general | solution.py:32
  375.8 5.8 %add_convert_fusion = bf16[512,1024]{1,0:T(8,128)(2,1)} fusion(f32[512,1024]{1,0:T(8,128)S(1)} %fusion.21, f32[512,1024]{1,0:T(8,128)S(1)} %fusion.25, f32[512,1024]{1,0:T(8,128)S(1)} %fusion.29, f32[512,1024]{1,0:T(8,128)S(1)} %fusion.33, f32[512,1024]{1,0:T(8,128)S(1)} %copy-done.3, f32[512,1024]{1,0:T(8,128)S(1)} %copy-done.5, ...), kind=kOutput, calls=%fused_computation.93 | convolution fusion | flops 1883242496 | bytes 21233664 | tf_op jit(solution)/shard_map/dot_general | solution.py:32
  381.7 6.2 %fusion.7 = bf16[1024,7168]{1,0:T(8,128)(2,1)} fusion(bf16[1024,7168]{1,0:T(8,128)(2,1)} %copy-done, bf16[3,512,1792]{2,1,0:T(8,128)(2,1)} %copy-done.2, bf16[512,2048]{1,0:T(8,128)(2,1)} %all-gather.2.cloned.1.call-done), kind=kOutput, calls=%fused_computation.25 | convolution fusion | flops 1880883200 | bytes 6553600 | tf_op jit(solution)/shard_map/dot_general | solution.py:26
  387.9 4.0 fusion.6
  391.8 4.0 fusion.4
  395.8 4.0 fusion.3
  399.8 3.9 fusion.1
  (158 shorter events, 99.5 us)
Async XLA Ops:
  7.2 51.6 %all-gather.2.cloned.1.call-start = ((), (), s32[]{:S(2)}) async-start(), calls=%async_computation.1 | async-start | bytes 2621440 | tf_op jit(solution)/shard_map/all_gather | solution.py:74
  9.1 398.5 %reduce-scatter.2.cloned.1.call-start = ((), (), s32[]{:S(2)}) async-start(), calls=%async_computation.2 | async-start | bytes 1310720 | tf_op jit(solution)/shard_map/reduce_scatter | solution.py:171
  58.8 4.6 %copy-start.6 = (bf16[512,2048]{1,0:T(8,128)(2,1)S(1)}, bf16[512,2048]{1,0:T(8,128)(2,1)}, u32[]{:S(2)}) copy-start(bf16[512,2048]{1,0:T(8,128)(2,1)} %all-gather.2.cloned.1.call-done) | copy-start | bytes 6291460
  87.6 4.7 %copy-start.7 = (bf16[512,2048]{1,0:T(8,128)(2,1)S(1)}, bf16[512,2048]{1,0:T(8,128)(2,1)}, u32[]{:S(2)}) copy-start(bf16[512,2048]{1,0:T(8,128)(2,1)} %all-gather.2.cloned.1.call-done) | copy-start | bytes 6291460
  87.7 32.4 %collective-permute-start.8 = (bf16[3,256,1792]{2,1,0:T(8,128)(2,1)S(1)}, bf16[3,256,1792]{2,1,0:T(8,128)(2,1)}, u32[]{:S(2)}, u32[]{:S(2)}) collective-permute-start(bf16[3,256,1792]{2,1,0:T(8,128)(2,1)S(1)} %constant_dynamic-slice_fusion.2), channel_id=1, source_target_pairs={{0,4},{4,0},{8,12},{12,8},{16,20},{20,16},{24,28},{28,24},{1,5},{5... | collective-permute-start | bytes 8257544 | tf_op jit(solution)/shard_map/ppermute | solution.py:112
  87.7 36.4 %collective-permute-start = (bf16[3,256,1792]{2,1,0:T(8,128)(2,1)}, bf16[3,256,1792]{2,1,0:T(8,128)(2,1)}, u32[]{:S(2)}, u32[]{:S(2)}) collective-permute-start(bf16[3,256,1792]{2,1,0:T(8,128)(2,1)} %constant_dynamic-slice_fusion.3), channel_id=1, source_target_pairs={{0,4},{4,0},{8,12},{12,8},{16,20},{20,16},{24,28},{28,24},{1,5},{5... | collective-permute-start | bytes 8257544 | tf_op jit(solution)/shard_map/ppermute | solution.py:112
  104.7 4.6 %copy-start.8 = (bf16[512,2048]{1,0:T(8,128)(2,1)S(1)}, bf16[512,2048]{1,0:T(8,128)(2,1)}, u32[]{:S(2)}) copy-start(bf16[512,2048]{1,0:T(8,128)(2,1)} %all-gather.2.cloned.1.call-done) | copy-start | bytes 6291460
  122.6 11.0 %collective-permute-start.9 = (bf16[3,64,1792]{2,1,0:T(8,128)(2,1)S(1)}, bf16[3,64,1792]{2,1,0:T(8,128)(2,1)S(1)}, u32[]{:S(2)}, u32[]{:S(2)}) collective-permute-start(bf16[3,64,1792]{2,1,0:T(8,128)(2,1)S(1)} %dynamic-slice_convert_fusion.2), channel_id=1, source_target_pairs={{0,8},{4,20},{8,24},{12,4},{16,0},{20,28},{24,16},{28,12},{1,9},{5... | collective-permute-start | bytes 2064392 | tf_op jit(solution)/shard_map/ppermute | solution.py:119
  127.5 13.5 %collective-permute-start.1 = (bf16[3,64,1792]{2,1,0:T(8,128)(2,1)}, bf16[3,64,1792]{2,1,0:T(8,128)(2,1)}, u32[]{:S(2)}, u32[]{:S(2)}) collective-permute-start(bf16[3,64,1792]{2,1,0:T(8,128)(2,1)} %dynamic-slice_convert_fusion.3), channel_id=1, source_target_pairs={{0,8},{4,20},{8,24},{12,4},{16,0},{20,28},{24,16},{28,12},{1,9},{5... | collective-permute-start | bytes 2064392 | tf_op jit(solution)/shard_map/ppermute | solution.py:119
  134.5 13.9 %collective-permute-start.10 = (bf16[3,64,1792]{2,1,0:T(8,128)(2,1)}, bf16[3,64,1792]{2,1,0:T(8,128)(2,1)}, u32[]{:S(2)}, u32[]{:S(2)}) collective-permute-start(bf16[3,64,1792]{2,1,0:T(8,128)(2,1)} %add_convert_fusion.6), channel_id=1, source_target_pairs={{0,8},{4,20},{8,24},{12,4},{16,0},{20,28},{24,16},{28,12},{1,9},{5... | collective-permute-start | bytes 2064392 | tf_op jit(solution)/shard_map/ppermute | solution.py:119
  142.3 13.4 %collective-permute-start.2 = (bf16[3,64,1792]{2,1,0:T(8,128)(2,1)S(1)}, bf16[3,64,1792]{2,1,0:T(8,128)(2,1)S(1)}, u32[]{:S(2)}, u32[]{:S(2)}) collective-permute-start(bf16[3,64,1792]{2,1,0:T(8,128)(2,1)S(1)} %add_convert_fusion.8), channel_id=1, source_target_pairs={{0,8},{4,20},{8,24},{12,4},{16,0},{20,28},{24,16},{28,12},{1,9},{5... | collective-permute-start | bytes 2064392 | tf_op jit(solution)/shard_map/ppermute | solution.py:119
  149.7 13.4 %collective-permute-start.11 = (bf16[3,64,1792]{2,1,0:T(8,128)(2,1)S(1)}, bf16[3,64,1792]{2,1,0:T(8,128)(2,1)S(1)}, u32[]{:S(2)}, u32[]{:S(2)}) collective-permute-start(bf16[3,64,1792]{2,1,0:T(8,128)(2,1)S(1)} %add_convert_fusion.5), channel_id=1, source_target_pairs={{0,8},{4,20},{8,24},{12,4},{16,0},{20,28},{24,16},{28,12},{1,9},{5... | collective-permute-start | bytes 2064392 | tf_op jit(solution)/shard_map/ppermute | solution.py:119
  155.8 14.6 %collective-permute-start.3 = (bf16[3,64,1792]{2,1,0:T(8,128)(2,1)S(1)}, bf16[3,64,1792]{2,1,0:T(8,128)(2,1)S(1)}, u32[]{:S(2)}, u32[]{:S(2)}) collective-permute-start(bf16[3,64,1792]{2,1,0:T(8,128)(2,1)S(1)} %add_convert_fusion.7), channel_id=1, source_target_pairs={{0,8},{4,20},{8,24},{12,4},{16,0},{20,28},{24,16},{28,12},{1,9},{5... | collective-permute-start | bytes 2064392 | tf_op jit(solution)/shard_map/ppermute | solution.py:119
  170.8 48.4 %collective-permute-start.16 = (bf16[3,256,1792]{2,1,0:T(8,128)(2,1)S(1)}, bf16[3,256,1792]{2,1,0:T(8,128)(2,1)S(1)}, u32[]{:S(2)}, u32[]{:S(2)}) collective-permute-start(bf16[3,256,1792]{2,1,0:T(8,128)(2,1)S(1)} %get-tuple-element.6), channel_id=1, source_target_pairs={{0,4},{4,0},{8,12},{12,8},{16,20},{20,16},{24,28},{28,24},{1,5},{5... | collective-permute-start | bytes 8257544 | tf_op jit(solution)/shard_map/ppermute | solution.py:112
  171.2 11.0 %collective-permute-start.12 = (bf16[3,64,1792]{2,1,0:T(8,128)(2,1)S(1)}, bf16[3,64,1792]{2,1,0:T(8,128)(2,1)S(1)}, u32[]{:S(2)}, u32[]{:S(2)}) collective-permute-start(bf16[3,64,1792]{2,1,0:T(8,128)(2,1)S(1)} %get-tuple-element.22), channel_id=1, source_target_pairs={{0,8},{4,20},{8,24},{12,4},{16,0},{20,28},{24,16},{28,12},{1,9},{5... | collective-permute-start | bytes 2064392 | tf_op jit(solution)/shard_map/ppermute | solution.py:128
  173.0 16.6 %collective-permute-start.4 = (bf16[3,64,1792]{2,1,0:T(8,128)(2,1)S(1)}, bf16[3,64,1792]{2,1,0:T(8,128)(2,1)S(1)}, u32[]{:S(2)}, u32[]{:S(2)}) collective-permute-start(bf16[3,64,1792]{2,1,0:T(8,128)(2,1)S(1)} %get-tuple-element.20), channel_id=1, source_target_pairs={{0,8},{4,20},{8,24},{12,4},{16,0},{20,28},{24,16},{28,12},{1,9},{5... | collective-permute-start | bytes 2064392 | tf_op jit(solution)/shard_map/ppermute | solution.py:128
  182.2 14.7 %collective-permute-start.13 = (bf16[3,64,1792]{2,1,0:T(8,128)(2,1)S(1)}, bf16[3,64,1792]{2,1,0:T(8,128)(2,1)S(1)}, u32[]{:S(2)}, u32[]{:S(2)}) collective-permute-start(bf16[3,64,1792]{2,1,0:T(8,128)(2,1)S(1)} %collective-permute-done.12), channel_id=1, source_target_pairs={{0,8},{4,20},{8,24},{12,4},{16,0},{20,28},{24,16},{28,12},{1,9},{5... | collective-permute-start | bytes 2064392 | tf_op jit(solution)/shard_map/ppermute | solution.py:128
  183.6 38.2 %collective-permute-start.24 = (bf16[3,256,1792]{2,1,0:T(8,128)(2,1)}, bf16[3,256,1792]{2,1,0:T(8,128)(2,1)S(1)}, u32[]{:S(2)}, u32[]{:S(2)}) collective-permute-start(bf16[3,256,1792]{2,1,0:T(8,128)(2,1)} %get-tuple-element.7), channel_id=1, source_target_pairs={{0,4},{4,0},{8,12},{12,8},{16,20},{20,16},{24,28},{28,24},{1,5},{5... | collective-permute-start | bytes 8257544 | tf_op jit(solution)/shard_map/ppermute | solution.py:112
  189.6 14.7 %collective-permute-start.5 = (bf16[3,64,1792]{2,1,0:T(8,128)(2,1)S(1)}, bf16[3,64,1792]{2,1,0:T(8,128)(2,1)S(1)}, u32[]{:S(2)}, u32[]{:S(2)}) collective-permute-start(bf16[3,64,1792]{2,1,0:T(8,128)(2,1)S(1)} %collective-permute-done.4), channel_id=1, source_target_pairs={{0,8},{4,20},{8,24},{12,4},{16,0},{20,28},{24,16},{28,12},{1,9},{5... | collective-permute-start | bytes 2064392 | tf_op jit(solution)/shard_map/ppermute | solution.py:128
  196.9 14.7 %collective-permute-start.14 = (bf16[3,64,1792]{2,1,0:T(8,128)(2,1)S(1)}, bf16[3,64,1792]{2,1,0:T(8,128)(2,1)S(1)}, u32[]{:S(2)}, u32[]{:S(2)}) collective-permute-start(bf16[3,64,1792]{2,1,0:T(8,128)(2,1)S(1)} %collective-permute-done.13), channel_id=1, source_target_pairs={{0,8},{4,20},{8,24},{12,4},{16,0},{20,28},{24,16},{28,12},{1,9},{5... | collective-permute-start | bytes 2064392 | tf_op jit(solution)/shard_map/ppermute | solution.py:128
  204.3 14.7 %collective-permute-start.6 = (bf16[3,64,1792]{2,1,0:T(8,128)(2,1)S(1)}, bf16[3,64,1792]{2,1,0:T(8,128)(2,1)S(1)}, u32[]{:S(2)}, u32[]{:S(2)}) collective-permute-start(bf16[3,64,1792]{2,1,0:T(8,128)(2,1)S(1)} %collective-permute-done.5), channel_id=1, source_target_pairs={{0,8},{4,20},{8,24},{12,4},{16,0},{20,28},{24,16},{28,12},{1,9},{5... | collective-permute-start | bytes 2064392 | tf_op jit(solution)/shard_map/ppermute | solution.py:128
  211.7 59.4 %collective-permute-start.15 = (bf16[3,256,1792]{2,1,0:T(8,128)(2,1)S(1)}, bf16[3,256,1792]{2,1,0:T(8,128)(2,1)}, u32[]{:S(2)}, u32[]{:S(2)}) collective-permute-start(bf16[3,256,1792]{2,1,0:T(8,128)(2,1)S(1)} %constant_dynamic-update-slice_fusion.14), channel_id=1, source_target_pairs={{0,4},{4,0},{8,12},{12,8},{16,20},{20,16},{24,28},{28,24},{1,5},{5... | collective-permute-start | bytes 8257544 | tf_op jit(solution)/shard_map/ppermute | solution.py:130
  219.1 58.3 %collective-permute-start.7 = (bf16[3,256,1792]{2,1,0:T(8,128)(2,1)S(1)}, bf16[3,256,1792]{2,1,0:T(8,128)(2,1)}, u32[]{:S(2)}, u32[]{:S(2)}) collective-permute-start(bf16[3,256,1792]{2,1,0:T(8,128)(2,1)S(1)} %constant_dynamic-update-slice_fusion.20), channel_id=1, source_target_pairs={{0,4},{4,0},{8,12},{12,8},{16,20},{20,16},{24,28},{28,24},{1,5},{5... | collective-permute-start | bytes 8257544 | tf_op jit(solution)/shard_map/ppermute | solution.py:130
  219.9 11.4 %collective-permute-start.17 = (bf16[3,64,1792]{2,1,0:T(8,128)(2,1)S(1)}, bf16[3,64,1792]{2,1,0:T(8,128)(2,1)S(1)}, u32[]{:S(2)}, u32[]{:S(2)}) collective-permute-start(bf16[3,64,1792]{2,1,0:T(8,128)(2,1)S(1)} %dynamic-slice_convert_fusion.1), channel_id=1, source_target_pairs={{0,8},{4,20},{8,24},{12,4},{16,0},{20,28},{24,16},{28,12},{1,9},{5... | collective-permute-start | bytes 2064392 | tf_op jit(solution)/shard_map/ppermute | solution.py:119
  222.5 16.1 %collective-permute-start.25 = (bf16[3,64,1792]{2,1,0:T(8,128)(2,1)S(1)}, bf16[3,64,1792]{2,1,0:T(8,128)(2,1)S(1)}, u32[]{:S(2)}, u32[]{:S(2)}) collective-permute-start(bf16[3,64,1792]{2,1,0:T(8,128)(2,1)S(1)} %dynamic-slice_convert_fusion), channel_id=1, source_target_pairs={{0,8},{4,20},{8,24},{12,4},{16,0},{20,28},{24,16},{28,12},{1,9},{5... | collective-permute-start | bytes 2064392 | tf_op jit(solution)/shard_map/ppermute | solution.py:119
  231.4 14.6 %collective-permute-start.18 = (bf16[3,64,1792]{2,1,0:T(8,128)(2,1)S(1)}, bf16[3,64,1792]{2,1,0:T(8,128)(2,1)S(1)}, u32[]{:S(2)}, u32[]{:S(2)}) collective-permute-start(bf16[3,64,1792]{2,1,0:T(8,128)(2,1)S(1)} %add_convert_fusion.4), channel_id=1, source_target_pairs={{0,8},{4,20},{8,24},{12,4},{16,0},{20,28},{24,16},{28,12},{1,9},{5... | collective-permute-start | bytes 2064392 | tf_op jit(solution)/shard_map/ppermute | solution.py:119
  238.8 14.6 %collective-permute-start.26 = (bf16[3,64,1792]{2,1,0:T(8,128)(2,1)S(1)}, bf16[3,64,1792]{2,1,0:T(8,128)(2,1)S(1)}, u32[]{:S(2)}, u32[]{:S(2)}) collective-permute-start(bf16[3,64,1792]{2,1,0:T(8,128)(2,1)S(1)} %add_convert_fusion.2), channel_id=1, source_target_pairs={{0,8},{4,20},{8,24},{12,4},{16,0},{20,28},{24,16},{28,12},{1,9},{5... | collective-permute-start | bytes 2064392 | tf_op jit(solution)/shard_map/ppermute | solution.py:119
  246.2 14.6 %collective-permute-start.19 = (bf16[3,64,1792]{2,1,0:T(8,128)(2,1)S(1)}, bf16[3,64,1792]{2,1,0:T(8,128)(2,1)S(1)}, u32[]{:S(2)}, u32[]{:S(2)}) collective-permute-start(bf16[3,64,1792]{2,1,0:T(8,128)(2,1)S(1)} %add_convert_fusion.3), channel_id=1, source_target_pairs={{0,8},{4,20},{8,24},{12,4},{16,0},{20,28},{24,16},{28,12},{1,9},{5... | collective-permute-start | bytes 2064392 | tf_op jit(solution)/shard_map/ppermute | solution.py:119
  253.6 14.6 %collective-permute-start.27 = (bf16[3,64,1792]{2,1,0:T(8,128)(2,1)S(1)}, bf16[3,64,1792]{2,1,0:T(8,128)(2,1)S(1)}, u32[]{:S(2)}, u32[]{:S(2)}) collective-permute-start(bf16[3,64,1792]{2,1,0:T(8,128)(2,1)S(1)} %add_convert_fusion.1), channel_id=1, source_target_pairs={{0,8},{4,20},{8,24},{12,4},{16,0},{20,28},{24,16},{28,12},{1,9},{5... | collective-permute-start | bytes 2064392 | tf_op jit(solution)/shard_map/ppermute | solution.py:119
  261.4 40.4 %collective-permute-start.20 = (bf16[3,64,1792]{2,1,0:T(8,128)(2,1)S(1)}, bf16[3,64,1792]{2,1,0:T(8,128)(2,1)}, u32[]{:S(2)}, u32[]{:S(2)}) collective-permute-start(bf16[3,64,1792]{2,1,0:T(8,128)(2,1)S(1)} %get-tuple-element.24), channel_id=1, source_target_pairs={{0,8},{4,20},{8,24},{12,4},{16,0},{20,28},{24,16},{28,12},{1,9},{5... | collective-permute-start | bytes 2064392 | tf_op jit(solution)/shard_map/ppermute | solution.py:128
  269.7 44.7 %collective-permute-start.28 = (bf16[3,64,1792]{2,1,0:T(8,128)(2,1)}, bf16[3,64,1792]{2,1,0:T(8,128)(2,1)}, u32[]{:S(2)}, u32[]{:S(2)}) collective-permute-start(bf16[3,64,1792]{2,1,0:T(8,128)(2,1)} %get-tuple-element.26), channel_id=1, source_target_pairs={{0,8},{4,20},{8,24},{12,4},{16,0},{20,28},{24,16},{28,12},{1,9},{5... | collective-permute-start | bytes 2064392 | tf_op jit(solution)/shard_map/ppermute | solution.py:128
  301.8 13.1 %collective-permute-start.21 = (bf16[3,64,1792]{2,1,0:T(8,128)(2,1)}, bf16[3,64,1792]{2,1,0:T(8,128)(2,1)S(1)}, u32[]{:S(2)}, u32[]{:S(2)}) collective-permute-start(bf16[3,64,1792]{2,1,0:T(8,128)(2,1)} %collective-permute-done.20), channel_id=1, source_target_pairs={{0,8},{4,20},{8,24},{12,4},{16,0},{20,28},{24,16},{28,12},{1,9},{5... | collective-permute-start | bytes 2064392 | tf_op jit(solution)/shard_map/ppermute | solution.py:128
  308.8 6.8 %copy-start.10 = (bf16[512,2048]{1,0:T(8,128)(2,1)S(1)}, bf16[512,2048]{1,0:T(8,128)(2,1)}, u32[]{:S(2)}) copy-start(bf16[512,2048]{1,0:T(8,128)(2,1)} %all-gather.2.cloned.1.call-done) | copy-start | bytes 6291460
  314.4 11.3 %collective-permute-start.29 = (bf16[3,64,1792]{2,1,0:T(8,128)(2,1)}, bf16[3,64,1792]{2,1,0:T(8,128)(2,1)}, u32[]{:S(2)}, u32[]{:S(2)}) collective-permute-start(bf16[3,64,1792]{2,1,0:T(8,128)(2,1)} %collective-permute-done.28), channel_id=1, source_target_pairs={{0,8},{4,20},{8,24},{12,4},{16,0},{20,28},{24,16},{28,12},{1,9},{5... | collective-permute-start | bytes 2064392 | tf_op jit(solution)/shard_map/ppermute | solution.py:128
  315.0 17.9 %collective-permute-start.22 = (bf16[3,64,1792]{2,1,0:T(8,128)(2,1)S(1)}, bf16[3,64,1792]{2,1,0:T(8,128)(2,1)S(1)}, u32[]{:S(2)}, u32[]{:S(2)}) collective-permute-start(bf16[3,64,1792]{2,1,0:T(8,128)(2,1)S(1)} %collective-permute-done.21), channel_id=1, source_target_pairs={{0,8},{4,20},{8,24},{12,4},{16,0},{20,28},{24,16},{28,12},{1,9},{5... | collective-permute-start | bytes 2064392 | tf_op jit(solution)/shard_map/ppermute | solution.py:128
  317.6 18.8 %copy-start = (bf16[1024,7168]{1,0:T(8,128)(2,1)}, bf16[1024,7168]{1,0:T(8,128)(2,1)S(1)}, u32[]{:S(2)}) copy-start(bf16[1024,7168]{1,0:T(8,128)(2,1)S(1)} %fusion.8) | copy-start | bytes 44040196
  325.6 20.5 %collective-permute-start.30 = (bf16[3,64,1792]{2,1,0:T(8,128)(2,1)}, bf16[3,64,1792]{2,1,0:T(8,128)(2,1)}, u32[]{:S(2)}, u32[]{:S(2)}) collective-permute-start(bf16[3,64,1792]{2,1,0:T(8,128)(2,1)} %collective-permute-done.29), channel_id=1, source_target_pairs={{0,8},{4,20},{8,24},{12,4},{16,0},{20,28},{24,16},{28,12},{1,9},{5... | collective-permute-start | bytes 2064392 | tf_op jit(solution)/shard_map/ppermute | solution.py:128
  332.9 25.7 %collective-permute-start.23 = (bf16[3,256,1792]{2,1,0:T(8,128)(2,1)S(1)}, bf16[3,256,1792]{2,1,0:T(8,128)(2,1)S(1)}, u32[]{:S(2)}, u32[]{:S(2)}) collective-permute-start(bf16[3,256,1792]{2,1,0:T(8,128)(2,1)S(1)} %constant_dynamic-update-slice_fusion.8), channel_id=1, source_target_pairs={{0,4},{4,0},{8,12},{12,8},{16,20},{20,16},{24,28},{28,24},{1,5},{5... | collective-permute-start | bytes 8257544 | tf_op jit(solution)/shard_map/ppermute | solution.py:130
  347.3 21.9 %collective-permute-start.31 = (bf16[3,256,1792]{2,1,0:T(8,128)(2,1)S(1)}, bf16[3,256,1792]{2,1,0:T(8,128)(2,1)S(1)}, u32[]{:S(2)}, u32[]{:S(2)}) collective-permute-start(bf16[3,256,1792]{2,1,0:T(8,128)(2,1)S(1)} %constant_dynamic-update-slice_fusion.2), channel_id=1, source_target_pairs={{0,4},{4,0},{8,12},{12,8},{16,20},{20,16},{24,28},{28,24},{1,5},{5... | collective-permute-start | bytes 8257544 | tf_op jit(solution)/shard_map/ppermute | solution.py:130
  359.0 10.3 %copy-start.2 = (bf16[3,512,1792]{2,1,0:T(8,128)(2,1)}, bf16[3,512,1792]{2,1,0:T(8,128)(2,1)S(1)}, u32[]{:S(2)}) copy-start(bf16[3,512,1792]{2,1,0:T(8,128)(2,1)S(1)} %constant_dynamic-update-slice_fusion.6) | copy-start | bytes 16515076
  369.6 6.2 %copy-start.1 = (bf16[3,512,1792]{2,1,0:T(8,128)(2,1)}, bf16[3,512,1792]{2,1,0:T(8,128)(2,1)S(1)}, u32[]{:S(2)}) copy-start(bf16[3,512,1792]{2,1,0:T(8,128)(2,1)S(1)} %constant_dynamic-update-slice_fusion) | copy-start | bytes 16515076
  369.6 6.2 %copy-start.3 = (f32[512,1024]{1,0:T(8,128)S(1)}, f32[512,1024]{1,0:T(8,128)}, u32[]{:S(2)}) copy-start(f32[512,1024]{1,0:T(8,128)} %fusion.37) | copy-start | bytes 6291460
  369.6 6.2 %copy-start.4 = (f32[512,1024]{1,0:T(8,128)S(1)}, f32[512,1024]{1,0:T(8,128)}, u32[]{:S(2)}) copy-start(f32[512,1024]{1,0:T(8,128)} %fusion.41) | copy-start | bytes 6291460
  369.6 6.2 %copy-start.5 = (f32[512,1024]{1,0:T(8,128)S(1)}, f32[512,1024]{1,0:T(8,128)}, u32[]{:S(2)}) copy-start(f32[512,1024]{1,0:T(8,128)} %fusion.45) | copy-start | bytes 6291460
  381.6 6.3 %slice-start = ((s8[5505024]{0:T(1024)(128)(4,1)}), s8[1310720]{0:T(1024)(128)(4,1)S(1)}, s32[]{:S(2)}) async-start(s8[5505024]{0:T(1024)(128)(4,1)} %bitcast.75), calls=%async_computation.3 | async-start | bytes 2621440
  381.6 6.2 %slice-start.1 = ((s8[5505024]{0:T(1024)(128)(4,1)}), s8[4194304]{0:T(1024)(128)(4,1)S(1)}, s32[]{:S(2)}) async-start(s8[5505024]{0:T(1024)(128)(4,1)} %bitcast.75), calls=%async_computation.4 | async-start | bytes 8388608
  381.6 6.2 %copy-start.12 = (bf16[512,2048]{1,0:T(8,128)(2,1)S(1)}, bf16[512,2048]{1,0:T(8,128)(2,1)}, u32[]{:S(2)}) copy-start(bf16[512,2048]{1,0:T(8,128)(2,1)} %all-gather.2.cloned.1.call-done) | copy-start | bytes 6291460
  381.6 10.2 %slice-start.2 = ((s8[5505024]{0:T(1024)(128)(4,1)}), s8[4194304]{0:T(1024)(128)(4,1)S(1)}, s32[]{:S(2)}) async-start(s8[5505024]{0:T(1024)(128)(4,1)} %bitcast.77), calls=%async_computation.5 | async-start | bytes 8388608
  (3 other events, 10.6 us)
Sparse Core Ops, SparseCore 0:
  10.1 48.6 all-gather.1
  381.7 24.0 reduce-scatter.1

commit v4 on v3

--- a/solution.py
+++ b/solution.py
@@ -4,7 +4,7 @@
 from jax.sharding import PartitionSpec as P
 
 N_CHUNKS = 4
-GROUP = 2
+GROUP = 1
 FWD_GATE = -1
 GATE_BWD = 0
 FWD_IN_STEP = -1

time: 420 us -> 418 us (level)
  waiting for transfers between devices: 157 us -> 167 us
  other arithmetic: 22.3 us -> 13.6 us
  matrix products: 140 us -> 132 us
    ppermute x12, waiting for transfers between devices: 51.3 us -> 38.8 us  [gather_chunk(): cur = lax.ppermute(cur, 'row', ring_pairs)]
    ppermute x4, waiting for transfers between devices: 0.01 us -> 9.13 us  [reduce_chunk(): got = lax.ppermute(other, 'row', core_pairs)]
    dot_general x12, matrix products: 61.9 us -> 53.2 us  [contract_cols(): lax.dot_general(left, right, (((1,), (1,)), ((), ())), preferred_element_...]
    dynamic_update_slice x20, local copies, waits for them, and re-layouts: 11.9 us -> 5.04 us  [put(): return lax.dynamic_update_slice_in_dim(array, piece, start, 1)]
    ppermute x12, waiting for transfers between devices: 60.5 us -> 67.3 us  [reduce_chunk(): got = lax.ppermute(acc.astype(BF16), 'row', ring_pairs)]
    unnamed x34 -> x32, local copies, waits for them, and re-layouts: 0.23 us -> 5.41 us
    another operation x4, other arithmetic: 7.5 us -> 2.9 us  [forward(): jnp.stack([jnp.dot(x_panel, gate_weight[:, cols], preferred_element_type=...]
    all_gather x1, waiting for transfers between devices: 45.1 us -> 49.6 us  [per_device(): lax.all_gather(jnp.concatenate([tokens, cotangent], axis=1), 'col', axis=...]
  transfers between devices with their start and end apart: 34 -> 34, of which waited for: 21 -> 27; matrix products, arithmetic and copies ran while one was open for 39% -> 36% of each run, Pallas kernels for 0% -> 0%
where the time goes in v4:
time: 418 us; the launch traced here: 411 us
  waiting for transfers between devices  167 us (40%)
  matrix products  132 us (32%)
  local copies, waits for them, and re-layouts  42.3 us (10%)
  starting transfers between devices  36.7 us (9%)
  between operations  18.4 us (4%)
  other arithmetic  13.6 us (3%)
    ppermute x12, waiting for transfers between devices, reduce_chunk(): got = lax.ppermute(acc.astype(BF16), 'row', ring_pairs)  67.3 us
    dot_general x12, matrix products, contract_cols(): lax.dot_general(left, right, (((1,), (1,)), ((), ())), preferred_element_...  53.2 us
    all_gather x1, waiting for transfers between devices, per_device(): lax.all_gather(jnp.concatenate([tokens, cotangent], axis=1), 'col', axis=...  49.6 us
    dot_general x12, matrix products, contract_rows(): lax.dot_general(left, right, (((0,), (0,)), ((), ())), preferred_element_...  45.3 us
    ppermute x12, waiting for transfers between devices, gather_chunk(): cur = lax.ppermute(cur, 'row', ring_pairs)  38.8 us
    ppermute x12, starting transfers between devices, reduce_chunk(): got = lax.ppermute(acc.astype(BF16), 'row', ring_pairs)  18.3 us
    ppermute x12, starting transfers between devices, gather_chunk(): cur = lax.ppermute(cur, 'row', ring_pairs)  17.8 us
    dot_general x4, matrix products, forward(): jnp.dot(x_panel, up_weight[:, cols], preferred_element_type=F32)  17 us
  transfers between devices with their start and end apart: 34, of which 27 were waited for; matrix products, arithmetic and copies ran while one was open for 36% of the time, Pallas kernels for 0%

profile of v4, /device:TPU:0, one launch (start us, length us, event | category | flops | bytes accessed | tf_op | source)
XLA Modules:
  0.0 410.6 jit_solution(10589250979152631175)
XLA Ops:
  9.2 49.6 %all-gather.2.cloned.1.call-done = bf16[512,2048]{1,0:T(8,128)(2,1)} async-done(((bf16[128,2048]{1,0:T(8,128)(2,1)}), bf16[512,2048]{1,0:T(8,128)(2,1)}) %all-gather.2.cloned.1.call-update) | async-done | bytes 2097168 | tf_op jit(solution)/shard_map/all_gather | solution.py:74
  58.8 4.6 %fusion.115 = bf16[1,512,1792]{2,1,0:T(8,128)(2,1)S(1)} fusion(bf16[1024,7168]{1,0:T(8,128)(2,1)} %param.9, bf16[512,2048]{1,0:T(8,128)(2,1)} %all-gather.2.cloned.1.call-done), kind=kOutput, calls=%fused_computation.91 | convolution fusion | flops 1879965696 | bytes 6553600 | tf_op jit(solution)/shard_map/dot_general | solution.py:100
  63.4 4.2 %fusion.94 = bf16[1,512,1792]{2,1,0:T(8,128)(2,1)S(1)} fusion(bf16[7168,1024]{1,0:T(8,128)(2,1)} %param.10, bf16[512,2048]{1,0:T(8,128)(2,1)S(1)} %copy-done.6), kind=kOutput, calls=%fused_computation.84 | convolution fusion | flops 1879965696 | bytes 6553600 | tf_op jit(solution)/shard_map/dot_general | solution.py:32
  67.6 4.1 fusion.118
  77.0 4.0 collective-permute-done
  89.4 4.6 %fusion.112 = bf16[1,512,1792]{2,1,0:T(8,128)(2,1)S(1)} fusion(bf16[1024,7168]{1,0:T(8,128)(2,1)} %param.8, bf16[512,2048]{1,0:T(8,128)(2,1)} %all-gather.2.cloned.1.call-done), kind=kOutput, calls=%fused_computation.90 | convolution fusion | flops 1879965696 | bytes 6553600 | tf_op jit(solution)/shard_map/dot_general | solution.py:99
  98.7 4.1 fusion.109
  102.8 4.2 %fusion.91 = bf16[1,512,1792]{2,1,0:T(8,128)(2,1)S(1)} fusion(bf16[7168,1024]{1,0:T(8,128)(2,1)} %param.10, bf16[512,2048]{1,0:T(8,128)(2,1)S(1)} %copy-done.7), kind=kOutput, calls=%fused_computation.83 | convolution fusion | flops 1879965696 | bytes 6553600 | tf_op jit(solution)/shard_map/dot_general | solution.py:32
  110.7 8.6 %collective-permute-done.3 = bf16[3,64,1792]{2,1,0:T(8,128)(2,1)S(1)} collective-permute-done((bf16[3,64,1792]{2,1,0:T(8,128)(2,1)S(1)}, bf16[3,64,1792]{2,1,0:T(8,128)(2,1)S(1)}, u32[]{:S(2)}, u32[]{:S(2)}) %collective-permute-start.3) | collective-permute-done | bytes 688160 | tf_op jit(solution)/shard_map/ppermute | solution.py:119
  119.5 5.1 %collective-permute-done.8 = bf16[3,256,1792]{2,1,0:T(8,128)(2,1)S(1)} collective-permute-done((bf16[3,256,1792]{2,1,0:T(8,128)(2,1)S(1)}, bf16[3,256,1792]{2,1,0:T(8,128)(2,1)S(1)}, u32[]{:S(2)}, u32[]{:S(2)}) %collective-permute-start.8) | collective-permute-done | bytes 2752544 | tf_op jit(solution)/shard_map/ppermute | solution.py:112
  126.8 4.1 fusion.106
  130.9 5.4 %collective-permute-done.9 = bf16[3,64,1792]{2,1,0:T(8,128)(2,1)S(1)} collective-permute-done((bf16[3,64,1792]{2,1,0:T(8,128)(2,1)S(1)}, bf16[3,64,1792]{2,1,0:T(8,128)(2,1)S(1)}, u32[]{:S(2)}, u32[]{:S(2)}) %collective-permute-start.9) | collective-permute-done | bytes 688160 | tf_op jit(solution)/shard_map/ppermute | solution.py:119
  137.9 4.1 fusion.103
  142.0 4.2 %fusion.88 = bf16[1,512,1792]{2,1,0:T(8,128)(2,1)S(1)} fusion(bf16[7168,1024]{1,0:T(8,128)(2,1)} %param.10, bf16[512,2048]{1,0:T(8,128)(2,1)S(1)} %copy-done.8), kind=kOutput, calls=%fused_computation.82 | convolution fusion | flops 1879965696 | bytes 6553600 | tf_op jit(solution)/shard_map/dot_general | solution.py:32
  153.0 5.5 %collective-permute-done.11 = bf16[3,64,1792]{2,1,0:T(8,128)(2,1)S(1)} collective-permute-done((bf16[3,64,1792]{2,1,0:T(8,128)(2,1)S(1)}, bf16[3,64,1792]{2,1,0:T(8,128)(2,1)S(1)}, u32[]{:S(2)}, u32[]{:S(2)}) %collective-permute-start.11) | collective-permute-done | bytes 688160 | tf_op jit(solution)/shard_map/ppermute | solution.py:119
  161.8 4.1 fusion.100
  165.9 5.4 %collective-permute-done.4 = bf16[3,64,1792]{2,1,0:T(8,128)(2,1)S(1)} collective-permute-done((bf16[3,64,1792]{2,1,0:T(8,128)(2,1)S(1)}, bf16[3,64,1792]{2,1,0:T(8,128)(2,1)S(1)}, u32[]{:S(2)}, u32[]{:S(2)}) %collective-permute-start.4) | collective-permute-done | bytes 688160 | tf_op jit(solution)/shard_map/ppermute | solution.py:128
  172.8 4.2 %fusion.97 = bf16[1,512,1792]{2,1,0:T(8,128)(2,1)S(1)} fusion(bf16[1024,7168]{1,0:T(8,128)(2,1)} %param.9, bf16[512,2048]{1,0:T(8,128)(2,1)S(1)} %copy-done.9), kind=kOutput, calls=%fused_computation.85 | convolution fusion | flops 1879965696 | bytes 6553600 | tf_op jit(solution)/shard_map/dot_general | solution.py:100
  177.0 4.2 %fusion.85 = bf16[1,512,1792]{2,1,0:T(8,128)(2,1)S(1)} fusion(bf16[7168,1024]{1,0:T(8,128)(2,1)} %param.10, bf16[512,2048]{1,0:T(8,128)(2,1)S(1)} %copy-done.9), kind=kOutput, calls=%fused_computation.81 | convolution fusion | flops 1879965696 | bytes 6553600 | tf_op jit(solution)/shard_map/dot_general | solution.py:32
  187.9 5.3 %collective-permute-done.6 = bf16[3,64,1792]{2,1,0:T(8,128)(2,1)S(1)} collective-permute-done((bf16[3,64,1792]{2,1,0:T(8,128)(2,1)S(1)}, bf16[3,64,1792]{2,1,0:T(8,128)(2,1)S(1)}, u32[]{:S(2)}, u32[]{:S(2)}) %collective-permute-start.6) | collective-permute-done | bytes 688160 | tf_op jit(solution)/shard_map/ppermute | solution.py:128
  193.3 7.2 %collective-permute-done.17 = bf16[3,64,1792]{2,1,0:T(8,128)(2,1)S(1)} collective-permute-done((bf16[3,64,1792]{2,1,0:T(8,128)(2,1)S(1)}, bf16[3,64,1792]{2,1,0:T(8,128)(2,1)S(1)}, u32[]{:S(2)}, u32[]{:S(2)}) %collective-permute-start.17) | collective-permute-done | bytes 688160 | tf_op jit(solution)/shard_map/ppermute | solution.py:119
  203.8 7.9 %collective-permute-done.18 = bf16[3,64,1792]{2,1,0:T(8,128)(2,1)S(1)} collective-permute-done((bf16[3,64,1792]{2,1,0:T(8,128)(2,1)S(1)}, bf16[3,64,1792]{2,1,0:T(8,128)(2,1)S(1)}, u32[]{:S(2)}, u32[]{:S(2)}) %collective-permute-start.18) | collective-permute-done | bytes 688160 | tf_op jit(solution)/shard_map/ppermute | solution.py:119
  215.4 7.4 %collective-permute-done.19 = bf16[3,64,1792]{2,1,0:T(8,128)(2,1)S(1)} collective-permute-done((bf16[3,64,1792]{2,1,0:T(8,128)(2,1)S(1)}, bf16[3,64,1792]{2,1,0:T(8,128)(2,1)S(1)}, u32[]{:S(2)}, u32[]{:S(2)}) %collective-permute-start.19) | collective-permute-done | bytes 688160 | tf_op jit(solution)/shard_map/ppermute | solution.py:119
  233.9 4.1 %fusion.41 = f32[512,1024]{1,0:T(8,128)S(1)} fusion(bf16[1024,7168]{1,0:T(8,128)(2,1)} %param.9, bf16[3,512,1792]{2,1,0:T(8,128)(2,1)S(1)} %constant_dynamic-update-slice_fusion.18), kind=kOutput, calls=%fused_computation.61 | convolution fusion | flops 1879048192 | bytes 7602176 | tf_op jit(solution)/shard_map/dot_general | solution.py:32
  244.8 10.6 %dynamic_update_slice.140 = bf16[7168,1024]{1,0:T(8,128)(2,1)} pad(bf16[1792,1024]{1,0:T(8,128)(2,1)S(1)} %convolution_convert_fusion.3, bf16[]{:T(256)} %constant.117.clone.1), padding=0_5376x0_0 | pad | bytes 18350082 | tf_op jit(solution)/shard_map/dynamic_update_slice | solution.py:148
  255.5 7.1 %dynamic_update_slice.132 = bf16[1024,7168]{1,0:T(8,128)(2,1)} pad(bf16[1024,1792]{1,0:T(8,128)(2,1)S(1)} %convolution_convert_fusion.11, bf16[]{:T(256)} %constant.117.clone.1), padding=0_0x0_5376 | pad | bytes 18350082 | tf_op jit(solution)/shard_map/dynamic_update_slice | solution.py:146
  262.5 7.0 %dynamic_update_slice.136 = bf16[1024,7168]{1,0:T(8,128)(2,1)} pad(bf16[1024,1792]{1,0:T(8,128)(2,1)S(1)} %convolution_convert_fusion.7, bf16[]{:T(256)} %constant.117.clone.1), padding=0_0x0_5376 | pad | bytes 18350082 | tf_op jit(solution)/shard_map/dynamic_update_slice | solution.py:147
  273.2 8.3 %collective-permute-done.25 = bf16[3,64,1792]{2,1,0:T(8,128)(2,1)S(1)} collective-permute-done((bf16[3,64,1792]{2,1,0:T(8,128)(2,1)S(1)}, bf16[3,64,1792]{2,1,0:T(8,128)(2,1)S(1)}, u32[]{:S(2)}, u32[]{:S(2)}) %collective-permute-start.25) | collective-permute-done | bytes 688160 | tf_op jit(solution)/shard_map/ppermute | solution.py:119
  283.2 4.1 %fusion.45 = f32[512,1024]{1,0:T(8,128)S(1)} fusion(bf16[1024,7168]{1,0:T(8,128)(2,1)} %param.8, bf16[3,512,1792]{2,1,0:T(8,128)(2,1)S(1)} %constant_dynamic-update-slice_fusion.18), kind=kOutput, calls=%fused_computation.65 | convolution fusion | flops 1879048192 | bytes 7602176 | tf_op jit(solution)/shard_map/dot_general | solution.py:32
  290.4 5.9 %collective-permute-done.26 = bf16[3,64,1792]{2,1,0:T(8,128)(2,1)S(1)} collective-permute-done((bf16[3,64,1792]{2,1,0:T(8,128)(2,1)S(1)}, bf16[3,64,1792]{2,1,0:T(8,128)(2,1)S(1)}, u32[]{:S(2)}, u32[]{:S(2)}) %collective-permute-start.26) | collective-permute-done | bytes 688160 | tf_op jit(solution)/shard_map/ppermute | solution.py:119
  298.2 4.1 %fusion.33 = f32[512,1024]{1,0:T(8,128)S(1)} fusion(bf16[1024,7168]{1,0:T(8,128)(2,1)} %param.9, bf16[3,512,1792]{2,1,0:T(8,128)(2,1)S(1)} %constant_dynamic-update-slice_fusion.12), kind=kOutput, calls=%fused_computation.53 | convolution fusion | flops 1879048192 | bytes 7602176 | tf_op jit(solution)/shard_map/dot_general | solution.py:32
  305.1 5.9 %collective-permute-done.27 = bf16[3,64,1792]{2,1,0:T(8,128)(2,1)S(1)} collective-permute-done((bf16[3,64,1792]{2,1,0:T(8,128)(2,1)S(1)}, bf16[3,64,1792]{2,1,0:T(8,128)(2,1)S(1)}, u32[]{:S(2)}, u32[]{:S(2)}) %collective-permute-start.27) | collective-permute-done | bytes 688160 | tf_op jit(solution)/shard_map/ppermute | solution.py:119
  313.3 5.1 %collective-permute-done.22 = bf16[3,64,1792]{2,1,0:T(8,128)(2,1)S(1)} collective-permute-done((bf16[3,64,1792]{2,1,0:T(8,128)(2,1)S(1)}, bf16[3,64,1792]{2,1,0:T(8,128)(2,1)S(1)}, u32[]{:S(2)}, u32[]{:S(2)}) %collective-permute-start.22) | collective-permute-done | bytes 688160 | tf_op jit(solution)/shard_map/ppermute | solution.py:128
  318.5 7.2 %collective-permute-done.28 = bf16[3,64,1792]{2,1,0:T(8,128)(2,1)S(1)} collective-permute-done((bf16[3,64,1792]{2,1,0:T(8,128)(2,1)S(1)}, bf16[3,64,1792]{2,1,0:T(8,128)(2,1)S(1)}, u32[]{:S(2)}, u32[]{:S(2)}) %collective-permute-start.28) | collective-permute-done | bytes 688160 | tf_op jit(solution)/shard_map/ppermute | solution.py:128
  331.2 4.1 %fusion.37 = f32[512,1024]{1,0:T(8,128)S(1)} fusion(bf16[1024,7168]{1,0:T(8,128)(2,1)} %param.8, bf16[3,512,1792]{2,1,0:T(8,128)(2,1)S(1)} %constant_dynamic-update-slice_fusion.12), kind=kOutput, calls=%fused_computation.57 | convolution fusion | flops 1879048192 | bytes 7602176 | tf_op jit(solution)/shard_map/dot_general | solution.py:32
  338.6 4.0 fusion.8
  342.6 5.4 %collective-permute-done.30 = bf16[3,64,1792]{2,1,0:T(8,128)(2,1)S(1)} collective-permute-done((bf16[3,64,1792]{2,1,0:T(8,128)(2,1)S(1)}, bf16[3,64,1792]{2,1,0:T(8,128)(2,1)S(1)}, u32[]{:S(2)}, u32[]{:S(2)}) %collective-permute-start.30) | collective-permute-done | bytes 688160 | tf_op jit(solution)/shard_map/ppermute | solution.py:128
  348.2 4.0 fusion.5
  353.2 4.0 fusion.7
  357.2 4.1 %fusion.25 = f32[512,1024]{1,0:T(8,128)S(1)} fusion(bf16[1024,7168]{1,0:T(8,128)(2,1)} %param.9, bf16[3,512,1792]{2,1,0:T(8,128)(2,1)S(1)} %constant_dynamic-update-slice_fusion.6), kind=kOutput, calls=%fused_computation.45 | convolution fusion | flops 1879048192 | bytes 7602176 | tf_op jit(solution)/shard_map/dot_general | solution.py:32
  361.3 4.1 %fusion.29 = f32[512,1024]{1,0:T(8,128)S(1)} fusion(bf16[1024,7168]{1,0:T(8,128)(2,1)} %param.8, bf16[3,512,1792]{2,1,0:T(8,128)(2,1)S(1)} %constant_dynamic-update-slice_fusion.6), kind=kOutput, calls=%fused_computation.49 | convolution fusion | flops 1879048192 | bytes 7602176 | tf_op jit(solution)/shard_map/dot_general | solution.py:32
  366.5 6.3 %fusion.21 = f32[512,1024]{1,0:T(8,128)S(1)} fusion(bf16[1024,7168]{1,0:T(8,128)(2,1)} %param.8, bf16[3,512,1792]{2,1,0:T(8,128)(2,1)S(1)} %constant_dynamic-update-slice_fusion), kind=kOutput, calls=%fused_computation.41 | convolution fusion | flops 1879048192 | bytes 7602176 | tf_op jit(solution)/shard_map/dot_general | solution.py:32
  372.8 5.5 %add_convert_fusion = bf16[512,1024]{1,0:T(8,128)(2,1)} fusion(f32[512,1024]{1,0:T(8,128)S(1)} %fusion.21, f32[512,1024]{1,0:T(8,128)S(1)} %fusion.25, f32[512,1024]{1,0:T(8,128)S(1)} %fusion.29, f32[512,1024]{1,0:T(8,128)S(1)} %fusion.33, f32[512,1024]{1,0:T(8,128)S(1)} %fusion.37, f32[512,1024]{1,0:T(8,128)S(1)} %fusion.45, f32[512,1024]{1,0:T(8,128)S(1)} %fusion.41, ...), kind=kOutput, calls=%fused_computation.93 | convolution fusion | flops 1883242496 | bytes 21233664 | tf_op jit(solution)/shard_map/dot_general | solution.py:32
  378.3 5.6 %fusion.4 = bf16[1024,7168]{1,0:T(8,128)(2,1)} fusion(bf16[1024,7168]{1,0:T(8,128)(2,1)} %fusion.5, bf16[3,512,1792]{2,1,0:T(8,128)(2,1)} %copy-done.5, bf16[512,2048]{1,0:T(8,128)(2,1)S(1)} %copy-done.10), kind=kOutput, calls=%fused_computation.18 | convolution fusion | flops 1880883200 | bytes 6553600 | tf_op jit(solution)/shard_map/dot_general | solution.py:26
  383.9 5.6 %fusion.1 = bf16[7168,1024]{1,0:T(8,128)(2,1)} fusion(bf16[7168,1024]{1,0:T(8,128)(2,1)} %fusion.2, bf16[3,512,1792]{2,1,0:T(8,128)(2,1)} %copy-done.5, bf16[512,2048]{1,0:T(8,128)(2,1)S(1)} %copy-done.10), kind=kOutput, calls=%fused_computation.11 | convolution fusion | flops 1880883200 | bytes 6553600 | tf_op jit(solution)/shard_map/dot_general | solution.py:26
  389.5 4.0 fusion.6
  393.4 4.0 fusion.3
  397.4 4.0 fusion
  (157 shorter events, 96.2 us)
Async XLA Ops:
  7.2 51.6 %all-gather.2.cloned.1.call-start = ((), (), s32[]{:S(2)}) async-start(), calls=%async_computation.1 | async-start | bytes 2621440 | tf_op jit(solution)/shard_map/all_gather | solution.py:74
  9.1 394.4 %reduce-scatter.2.cloned.1.call-start = ((), (), s32[]{:S(2)}) async-start(), calls=%async_computation.2 | async-start | bytes 1310720 | tf_op jit(solution)/shard_map/reduce_scatter | solution.py:171
  58.8 4.6 %copy-start.6 = (bf16[512,2048]{1,0:T(8,128)(2,1)S(1)}, bf16[512,2048]{1,0:T(8,128)(2,1)}, u32[]{:S(2)}) copy-start(bf16[512,2048]{1,0:T(8,128)(2,1)} %all-gather.2.cloned.1.call-done) | copy-start | bytes 6291460
  72.4 3.3 copy-start.1
  72.4 3.3 copy-start.11
  75.7 5.3 %collective-permute-start = (bf16[3,256,1792]{2,1,0:T(8,128)(2,1)}, bf16[3,256,1792]{2,1,0:T(8,128)(2,1)S(1)}, u32[]{:S(2)}, u32[]{:S(2)}) collective-permute-start(bf16[3,256,1792]{2,1,0:T(8,128)(2,1)} %constant_dynamic-slice_fusion.3), channel_id=1, source_target_pairs={{0,4},{4,0},{8,12},{12,8},{16,20},{20,16},{24,28},{28,24},{1,5},{5... | collective-permute-start | bytes 8257544 | tf_op jit(solution)/shard_map/ppermute | solution.py:112
  83.3 2.4 copy-start.2
  85.9 11.0 %collective-permute-start.1 = (bf16[3,64,1792]{2,1,0:T(8,128)(2,1)S(1)}, bf16[3,64,1792]{2,1,0:T(8,128)(2,1)S(1)}, u32[]{:S(2)}, u32[]{:S(2)}) collective-permute-start(bf16[3,64,1792]{2,1,0:T(8,128)(2,1)S(1)} %dynamic-slice_convert_fusion.3), channel_id=1, source_target_pairs={{0,8},{4,20},{8,24},{12,4},{16,0},{20,28},{24,16},{28,12},{1,9},{5... | collective-permute-start | bytes 2064392 | tf_op jit(solution)/shard_map/ppermute | solution.py:119
  89.4 7.5 %copy-start.3 = (f32[3,256,1792]{2,1,0:T(8,128)S(1)}, f32[3,256,1792]{2,1,0:T(8,128)}, u32[]{:S(2)}) copy-start(f32[3,256,1792]{2,1,0:T(8,128)} %copy-done.2) | copy-start | bytes 16515076
  94.0 4.7 %copy-start.7 = (bf16[512,2048]{1,0:T(8,128)(2,1)S(1)}, bf16[512,2048]{1,0:T(8,128)(2,1)}, u32[]{:S(2)}) copy-start(bf16[512,2048]{1,0:T(8,128)(2,1)} %all-gather.2.cloned.1.call-done) | copy-start | bytes 6291460
  97.0 11.2 %collective-permute-start.2 = (bf16[3,64,1792]{2,1,0:T(8,128)(2,1)S(1)}, bf16[3,64,1792]{2,1,0:T(8,128)(2,1)S(1)}, u32[]{:S(2)}, u32[]{:S(2)}) collective-permute-start(bf16[3,64,1792]{2,1,0:T(8,128)(2,1)S(1)} %add_convert_fusion.8), channel_id=1, source_target_pairs={{0,8},{4,20},{8,24},{12,4},{16,0},{20,28},{24,16},{28,12},{1,9},{5... | collective-permute-start | bytes 2064392 | tf_op jit(solution)/shard_map/ppermute | solution.py:119
  108.3 11.0 %collective-permute-start.3 = (bf16[3,64,1792]{2,1,0:T(8,128)(2,1)S(1)}, bf16[3,64,1792]{2,1,0:T(8,128)(2,1)S(1)}, u32[]{:S(2)}, u32[]{:S(2)}) collective-permute-start(bf16[3,64,1792]{2,1,0:T(8,128)(2,1)S(1)} %add_convert_fusion.7), channel_id=1, source_target_pairs={{0,8},{4,20},{8,24},{12,4},{16,0},{20,28},{24,16},{28,12},{1,9},{5... | collective-permute-start | bytes 2064392 | tf_op jit(solution)/shard_map/ppermute | solution.py:119
  119.4 5.2 %collective-permute-start.8 = (bf16[3,256,1792]{2,1,0:T(8,128)(2,1)S(1)}, bf16[3,256,1792]{2,1,0:T(8,128)(2,1)S(1)}, u32[]{:S(2)}, u32[]{:S(2)}) collective-permute-start(bf16[3,256,1792]{2,1,0:T(8,128)(2,1)S(1)} %constant_dynamic-slice_fusion.2), channel_id=1, source_target_pairs={{0,4},{4,0},{8,12},{12,8},{16,20},{20,16},{24,28},{28,24},{1,5},{5... | collective-permute-start | bytes 8257544 | tf_op jit(solution)/shard_map/ppermute | solution.py:112
  125.3 11.0 %collective-permute-start.9 = (bf16[3,64,1792]{2,1,0:T(8,128)(2,1)S(1)}, bf16[3,64,1792]{2,1,0:T(8,128)(2,1)S(1)}, u32[]{:S(2)}, u32[]{:S(2)}) collective-permute-start(bf16[3,64,1792]{2,1,0:T(8,128)(2,1)S(1)} %dynamic-slice_convert_fusion.2), channel_id=1, source_target_pairs={{0,8},{4,20},{8,24},{12,4},{16,0},{20,28},{24,16},{28,12},{1,9},{5... | collective-permute-start | bytes 2064392 | tf_op jit(solution)/shard_map/ppermute | solution.py:119
  130.9 7.0 %copy-start.8 = (bf16[512,2048]{1,0:T(8,128)(2,1)S(1)}, bf16[512,2048]{1,0:T(8,128)(2,1)}, u32[]{:S(2)}) copy-start(bf16[512,2048]{1,0:T(8,128)(2,1)} %all-gather.2.cloned.1.call-done) | copy-start | bytes 6291460
  136.4 11.0 %collective-permute-start.10 = (bf16[3,64,1792]{2,1,0:T(8,128)(2,1)S(1)}, bf16[3,64,1792]{2,1,0:T(8,128)(2,1)S(1)}, u32[]{:S(2)}, u32[]{:S(2)}) collective-permute-start(bf16[3,64,1792]{2,1,0:T(8,128)(2,1)S(1)} %add_convert_fusion.6), channel_id=1, source_target_pairs={{0,8},{4,20},{8,24},{12,4},{16,0},{20,28},{24,16},{28,12},{1,9},{5... | collective-permute-start | bytes 2064392 | tf_op jit(solution)/shard_map/ppermute | solution.py:119
  147.5 11.0 %collective-permute-start.11 = (bf16[3,64,1792]{2,1,0:T(8,128)(2,1)S(1)}, bf16[3,64,1792]{2,1,0:T(8,128)(2,1)S(1)}, u32[]{:S(2)}, u32[]{:S(2)}) collective-permute-start(bf16[3,64,1792]{2,1,0:T(8,128)(2,1)S(1)} %add_convert_fusion.5), channel_id=1, source_target_pairs={{0,8},{4,20},{8,24},{12,4},{16,0},{20,28},{24,16},{28,12},{1,9},{5... | collective-permute-start | bytes 2064392 | tf_op jit(solution)/shard_map/ppermute | solution.py:119
  149.7 3.3 copy-start
  158.6 25.1 %collective-permute-start.16 = (bf16[3,256,1792]{2,1,0:T(8,128)(2,1)}, bf16[3,256,1792]{2,1,0:T(8,128)(2,1)}, u32[]{:S(2)}, u32[]{:S(2)}) collective-permute-start(bf16[3,256,1792]{2,1,0:T(8,128)(2,1)} %constant_dynamic-slice_fusion.1), channel_id=1, source_target_pairs={{0,4},{4,0},{8,12},{12,8},{16,20},{20,16},{24,28},{28,24},{1,5},{5... | collective-permute-start | bytes 8257544 | tf_op jit(solution)/shard_map/ppermute | solution.py:112
  159.9 11.4 %collective-permute-start.4 = (bf16[3,64,1792]{2,1,0:T(8,128)(2,1)S(1)}, bf16[3,64,1792]{2,1,0:T(8,128)(2,1)S(1)}, u32[]{:S(2)}, u32[]{:S(2)}) collective-permute-start(bf16[3,64,1792]{2,1,0:T(8,128)(2,1)S(1)} %get-tuple-element.22), channel_id=1, source_target_pairs={{0,8},{4,20},{8,24},{12,4},{16,0},{20,28},{24,16},{28,12},{1,9},{5... | collective-permute-start | bytes 2064392 | tf_op jit(solution)/shard_map/ppermute | solution.py:128
  171.3 10.9 %collective-permute-start.5 = (bf16[3,64,1792]{2,1,0:T(8,128)(2,1)S(1)}, bf16[3,64,1792]{2,1,0:T(8,128)(2,1)S(1)}, u32[]{:S(2)}, u32[]{:S(2)}) collective-permute-start(bf16[3,64,1792]{2,1,0:T(8,128)(2,1)S(1)} %collective-permute-done.4), channel_id=1, source_target_pairs={{0,8},{4,20},{8,24},{12,4},{16,0},{20,28},{24,16},{28,12},{1,9},{5... | collective-permute-start | bytes 2064392 | tf_op jit(solution)/shard_map/ppermute | solution.py:128
  172.7 10.9 %slice-start = ((s8[5505024]{0:T(1024)(128)(4,1)}), s8[4194304]{0:T(1024)(128)(4,1)S(1)}, s32[]{:S(2)}) async-start(s8[5505024]{0:T(1024)(128)(4,1)} %bitcast.75), calls=%async_computation.3 | async-start | bytes 8388608
  177.0 6.7 %slice-start.1 = ((s8[5505024]{0:T(1024)(128)(4,1)}), s8[1310720]{0:T(1024)(128)(4,1)S(1)}, s32[]{:S(2)}) async-start(s8[5505024]{0:T(1024)(128)(4,1)} %bitcast.75), calls=%async_computation.4 | async-start | bytes 2621440
  182.2 10.9 %collective-permute-start.6 = (bf16[3,64,1792]{2,1,0:T(8,128)(2,1)S(1)}, bf16[3,64,1792]{2,1,0:T(8,128)(2,1)S(1)}, u32[]{:S(2)}, u32[]{:S(2)}) collective-permute-start(bf16[3,64,1792]{2,1,0:T(8,128)(2,1)S(1)} %collective-permute-done.5), channel_id=1, source_target_pairs={{0,8},{4,20},{8,24},{12,4},{16,0},{20,28},{24,16},{28,12},{1,9},{5... | collective-permute-start | bytes 2064392 | tf_op jit(solution)/shard_map/ppermute | solution.py:128
  186.3 14.2 %collective-permute-start.17 = (bf16[3,64,1792]{2,1,0:T(8,128)(2,1)S(1)}, bf16[3,64,1792]{2,1,0:T(8,128)(2,1)S(1)}, u32[]{:S(2)}, u32[]{:S(2)}) collective-permute-start(bf16[3,64,1792]{2,1,0:T(8,128)(2,1)S(1)} %dynamic-slice_convert_fusion.1), channel_id=1, source_target_pairs={{0,8},{4,20},{8,24},{12,4},{16,0},{20,28},{24,16},{28,12},{1,9},{5... | collective-permute-start | bytes 2064392 | tf_op jit(solution)/shard_map/ppermute | solution.py:119
  193.2 29.8 %collective-permute-start.7 = (bf16[3,256,1792]{2,1,0:T(8,128)(2,1)S(1)}, bf16[3,256,1792]{2,1,0:T(8,128)(2,1)}, u32[]{:S(2)}, u32[]{:S(2)}) collective-permute-start(bf16[3,256,1792]{2,1,0:T(8,128)(2,1)S(1)} %constant_dynamic-update-slice_fusion.20), channel_id=1, source_target_pairs={{0,4},{4,0},{8,12},{12,8},{16,20},{20,16},{24,28},{28,24},{1,5},{5... | collective-permute-start | bytes 8257544 | tf_op jit(solution)/shard_map/ppermute | solution.py:130
  200.7 11.0 %collective-permute-start.18 = (bf16[3,64,1792]{2,1,0:T(8,128)(2,1)S(1)}, bf16[3,64,1792]{2,1,0:T(8,128)(2,1)S(1)}, u32[]{:S(2)}, u32[]{:S(2)}) collective-permute-start(bf16[3,64,1792]{2,1,0:T(8,128)(2,1)S(1)} %add_convert_fusion.4), channel_id=1, source_target_pairs={{0,8},{4,20},{8,24},{12,4},{16,0},{20,28},{24,16},{28,12},{1,9},{5... | collective-permute-start | bytes 2064392 | tf_op jit(solution)/shard_map/ppermute | solution.py:119
  211.8 11.0 %collective-permute-start.19 = (bf16[3,64,1792]{2,1,0:T(8,128)(2,1)S(1)}, bf16[3,64,1792]{2,1,0:T(8,128)(2,1)S(1)}, u32[]{:S(2)}, u32[]{:S(2)}) collective-permute-start(bf16[3,64,1792]{2,1,0:T(8,128)(2,1)S(1)} %add_convert_fusion.3), channel_id=1, source_target_pairs={{0,8},{4,20},{8,24},{12,4},{16,0},{20,28},{24,16},{28,12},{1,9},{5... | collective-permute-start | bytes 2064392 | tf_op jit(solution)/shard_map/ppermute | solution.py:119
  213.8 16.3 %collective-permute-start.12 = (bf16[3,64,1792]{2,1,0:T(8,128)(2,1)S(1)}, bf16[3,64,1792]{2,1,0:T(8,128)(2,1)S(1)}, u32[]{:S(2)}, u32[]{:S(2)}) collective-permute-start(bf16[3,64,1792]{2,1,0:T(8,128)(2,1)S(1)} %get-tuple-element.24), channel_id=1, source_target_pairs={{0,8},{4,20},{8,24},{12,4},{16,0},{20,28},{24,16},{28,12},{1,9},{5... | collective-permute-start | bytes 2064392 | tf_op jit(solution)/shard_map/ppermute | solution.py:128
  222.9 46.9 %collective-permute-start.24 = (bf16[3,256,1792]{2,1,0:T(8,128)(2,1)S(1)}, bf16[3,256,1792]{2,1,0:T(8,128)(2,1)S(1)}, u32[]{:S(2)}, u32[]{:S(2)}) collective-permute-start(bf16[3,256,1792]{2,1,0:T(8,128)(2,1)S(1)} %constant_dynamic-slice_fusion), channel_id=1, source_target_pairs={{0,4},{4,0},{8,12},{12,8},{16,20},{20,16},{24,28},{28,24},{1,5},{5... | collective-permute-start | bytes 8257544 | tf_op jit(solution)/shard_map/ppermute | solution.py:112
  230.2 11.1 %collective-permute-start.13 = (bf16[3,64,1792]{2,1,0:T(8,128)(2,1)S(1)}, bf16[3,64,1792]{2,1,0:T(8,128)(2,1)S(1)}, u32[]{:S(2)}, u32[]{:S(2)}) collective-permute-start(bf16[3,64,1792]{2,1,0:T(8,128)(2,1)S(1)} %collective-permute-done.12), channel_id=1, source_target_pairs={{0,8},{4,20},{8,24},{12,4},{16,0},{20,28},{24,16},{28,12},{1,9},{5... | collective-permute-start | bytes 2064392 | tf_op jit(solution)/shard_map/ppermute | solution.py:128
  241.3 28.4 %collective-permute-start.14 = (bf16[3,64,1792]{2,1,0:T(8,128)(2,1)S(1)}, bf16[3,64,1792]{2,1,0:T(8,128)(2,1)S(1)}, u32[]{:S(2)}, u32[]{:S(2)}) collective-permute-start(bf16[3,64,1792]{2,1,0:T(8,128)(2,1)S(1)} %collective-permute-done.13), channel_id=1, source_target_pairs={{0,8},{4,20},{8,24},{12,4},{16,0},{20,28},{24,16},{28,12},{1,9},{5... | collective-permute-start | bytes 2064392 | tf_op jit(solution)/shard_map/ppermute | solution.py:128
  269.8 28.2 %collective-permute-start.15 = (bf16[3,256,1792]{2,1,0:T(8,128)(2,1)S(1)}, bf16[3,256,1792]{2,1,0:T(8,128)(2,1)S(1)}, u32[]{:S(2)}, u32[]{:S(2)}) collective-permute-start(bf16[3,256,1792]{2,1,0:T(8,128)(2,1)S(1)} %constant_dynamic-update-slice_fusion.14), channel_id=1, source_target_pairs={{0,4},{4,0},{8,12},{12,8},{16,20},{20,16},{24,28},{28,24},{1,5},{5... | collective-permute-start | bytes 8257544 | tf_op jit(solution)/shard_map/ppermute | solution.py:130
  270.6 11.0 %collective-permute-start.25 = (bf16[3,64,1792]{2,1,0:T(8,128)(2,1)S(1)}, bf16[3,64,1792]{2,1,0:T(8,128)(2,1)S(1)}, u32[]{:S(2)}, u32[]{:S(2)}) collective-permute-start(bf16[3,64,1792]{2,1,0:T(8,128)(2,1)S(1)} %dynamic-slice_convert_fusion), channel_id=1, source_target_pairs={{0,8},{4,20},{8,24},{12,4},{16,0},{20,28},{24,16},{28,12},{1,9},{5... | collective-permute-start | bytes 2064392 | tf_op jit(solution)/shard_map/ppermute | solution.py:119
  272.6 16.3 %collective-permute-start.20 = (bf16[3,64,1792]{2,1,0:T(8,128)(2,1)S(1)}, bf16[3,64,1792]{2,1,0:T(8,128)(2,1)S(1)}, u32[]{:S(2)}, u32[]{:S(2)}) collective-permute-start(bf16[3,64,1792]{2,1,0:T(8,128)(2,1)S(1)} %get-tuple-element.26), channel_id=1, source_target_pairs={{0,8},{4,20},{8,24},{12,4},{16,0},{20,28},{24,16},{28,12},{1,9},{5... | collective-permute-start | bytes 2064392 | tf_op jit(solution)/shard_map/ppermute | solution.py:128
  281.7 14.6 %collective-permute-start.26 = (bf16[3,64,1792]{2,1,0:T(8,128)(2,1)S(1)}, bf16[3,64,1792]{2,1,0:T(8,128)(2,1)S(1)}, u32[]{:S(2)}, u32[]{:S(2)}) collective-permute-start(bf16[3,64,1792]{2,1,0:T(8,128)(2,1)S(1)} %add_convert_fusion.2), channel_id=1, source_target_pairs={{0,8},{4,20},{8,24},{12,4},{16,0},{20,28},{24,16},{28,12},{1,9},{5... | collective-permute-start | bytes 2064392 | tf_op jit(solution)/shard_map/ppermute | solution.py:119
  288.9 14.7 %collective-permute-start.21 = (bf16[3,64,1792]{2,1,0:T(8,128)(2,1)S(1)}, bf16[3,64,1792]{2,1,0:T(8,128)(2,1)S(1)}, u32[]{:S(2)}, u32[]{:S(2)}) collective-permute-start(bf16[3,64,1792]{2,1,0:T(8,128)(2,1)S(1)} %collective-permute-done.20), channel_id=1, source_target_pairs={{0,8},{4,20},{8,24},{12,4},{16,0},{20,28},{24,16},{28,12},{1,9},{5... | collective-permute-start | bytes 2064392 | tf_op jit(solution)/shard_map/ppermute | solution.py:128
  296.4 14.6 %collective-permute-start.27 = (bf16[3,64,1792]{2,1,0:T(8,128)(2,1)S(1)}, bf16[3,64,1792]{2,1,0:T(8,128)(2,1)S(1)}, u32[]{:S(2)}, u32[]{:S(2)}) collective-permute-start(bf16[3,64,1792]{2,1,0:T(8,128)(2,1)S(1)} %add_convert_fusion.1), channel_id=1, source_target_pairs={{0,8},{4,20},{8,24},{12,4},{16,0},{20,28},{24,16},{28,12},{1,9},{5... | collective-permute-start | bytes 2064392 | tf_op jit(solution)/shard_map/ppermute | solution.py:119
  303.7 14.7 %collective-permute-start.22 = (bf16[3,64,1792]{2,1,0:T(8,128)(2,1)S(1)}, bf16[3,64,1792]{2,1,0:T(8,128)(2,1)S(1)}, u32[]{:S(2)}, u32[]{:S(2)}) collective-permute-start(bf16[3,64,1792]{2,1,0:T(8,128)(2,1)S(1)} %collective-permute-done.21), channel_id=1, source_target_pairs={{0,8},{4,20},{8,24},{12,4},{16,0},{20,28},{24,16},{28,12},{1,9},{5... | collective-permute-start | bytes 2064392 | tf_op jit(solution)/shard_map/ppermute | solution.py:128
  311.7 14.1 %collective-permute-start.28 = (bf16[3,64,1792]{2,1,0:T(8,128)(2,1)S(1)}, bf16[3,64,1792]{2,1,0:T(8,128)(2,1)S(1)}, u32[]{:S(2)}, u32[]{:S(2)}) collective-permute-start(bf16[3,64,1792]{2,1,0:T(8,128)(2,1)S(1)} %get-tuple-element.28), channel_id=1, source_target_pairs={{0,8},{4,20},{8,24},{12,4},{16,0},{20,28},{24,16},{28,12},{1,9},{5... | collective-permute-start | bytes 2064392 | tf_op jit(solution)/shard_map/ppermute | solution.py:128
  318.5 34.4 %collective-permute-start.23 = (bf16[3,256,1792]{2,1,0:T(8,128)(2,1)S(1)}, bf16[3,256,1792]{2,1,0:T(8,128)(2,1)S(1)}, u32[]{:S(2)}, u32[]{:S(2)}) collective-permute-start(bf16[3,256,1792]{2,1,0:T(8,128)(2,1)S(1)} %constant_dynamic-update-slice_fusion.8), channel_id=1, source_target_pairs={{0,4},{4,0},{8,12},{12,8},{16,20},{20,16},{24,28},{28,24},{1,5},{5... | collective-permute-start | bytes 8257544 | tf_op jit(solution)/shard_map/ppermute | solution.py:130
  325.8 10.9 %collective-permute-start.29 = (bf16[3,64,1792]{2,1,0:T(8,128)(2,1)S(1)}, bf16[3,64,1792]{2,1,0:T(8,128)(2,1)S(1)}, u32[]{:S(2)}, u32[]{:S(2)}) collective-permute-start(bf16[3,64,1792]{2,1,0:T(8,128)(2,1)S(1)} %collective-permute-done.28), channel_id=1, source_target_pairs={{0,8},{4,20},{8,24},{12,4},{16,0},{20,28},{24,16},{28,12},{1,9},{5... | collective-permute-start | bytes 2064392 | tf_op jit(solution)/shard_map/ppermute | solution.py:128
  336.7 11.3 %collective-permute-start.30 = (bf16[3,64,1792]{2,1,0:T(8,128)(2,1)S(1)}, bf16[3,64,1792]{2,1,0:T(8,128)(2,1)S(1)}, u32[]{:S(2)}, u32[]{:S(2)}) collective-permute-start(bf16[3,64,1792]{2,1,0:T(8,128)(2,1)S(1)} %collective-permute-done.29), channel_id=1, source_target_pairs={{0,8},{4,20},{8,24},{12,4},{16,0},{20,28},{24,16},{28,12},{1,9},{5... | collective-permute-start | bytes 2064392 | tf_op jit(solution)/shard_map/ppermute | solution.py:128
  348.1 18.0 %collective-permute-start.31 = (bf16[3,256,1792]{2,1,0:T(8,128)(2,1)S(1)}, bf16[3,256,1792]{2,1,0:T(8,128)(2,1)S(1)}, u32[]{:S(2)}, u32[]{:S(2)}) collective-permute-start(bf16[3,256,1792]{2,1,0:T(8,128)(2,1)S(1)} %constant_dynamic-update-slice_fusion.2), channel_id=1, source_target_pairs={{0,4},{4,0},{8,12},{12,8},{16,20},{20,16},{24,28},{28,24},{1,5},{5... | collective-permute-start | bytes 8257544 | tf_op jit(solution)/shard_map/ppermute | solution.py:130
  353.2 8.1 %copy-start.5 = (bf16[3,512,1792]{2,1,0:T(8,128)(2,1)}, bf16[3,512,1792]{2,1,0:T(8,128)(2,1)S(1)}, u32[]{:S(2)}) copy-start(bf16[3,512,1792]{2,1,0:T(8,128)(2,1)S(1)} %constant_dynamic-update-slice_fusion.6) | copy-start | bytes 16515076
  366.4 6.3 %copy-start.4 = (bf16[3,512,1792]{2,1,0:T(8,128)(2,1)}, bf16[3,512,1792]{2,1,0:T(8,128)(2,1)S(1)}, u32[]{:S(2)}) copy-start(bf16[3,512,1792]{2,1,0:T(8,128)(2,1)S(1)} %constant_dynamic-update-slice_fusion) | copy-start | bytes 16515076
  378.3 11.2 %slice-start.2 = ((s8[5505024]{0:T(1024)(128)(4,1)}), s8[4194304]{0:T(1024)(128)(4,1)S(1)}, s32[]{:S(2)}) async-start(s8[5505024]{0:T(1024)(128)(4,1)} %bitcast.77), calls=%async_computation.5 | async-start | bytes 8388608
  383.9 5.6 %slice-start.3 = ((s8[5505024]{0:T(1024)(128)(4,1)}), s8[1310720]{0:T(1024)(128)(4,1)S(1)}, s32[]{:S(2)}) async-start(s8[5505024]{0:T(1024)(128)(4,1)} %bitcast.77), calls=%async_computation.6 | async-start | bytes 2621440
  (2 other events, 4.6 us)
Sparse Core Ops, SparseCore 0:
  10.1 48.6 all-gather.1
  378.4 25.0 reduce-scatter.1
